TPU v7x, 1024 devices: a whole 8x8x8 slice. The times are simulated.
1024 devices in a mesh: row: 32 (over x, y_lo), col: 32 (over y_hi, z, core).
Axes of the slice: x: 8, y: 8 (y_hi: 2, y_lo: 4; y = y_hi * 4 + y_lo), z: 8, core: 2. Of those that a mesh axis runs over, the one named last changes fastest.
Arguments:
- basis: bfloat16 [512, 32768], P('row', 'col'), may hold values from -6 to 6
- position: int32 [2, 32768], P(None, 'col'), may hold values from 0 to 65535, as said below
- poles: float32 [65536], P(('row', 'col')), may hold values from 0 to 65536, as said below
- weights: float32 [65536], P(('row', 'col')), may hold values from -2 to 2
- kept: int32 [65536], P(('row', 'col')), may hold values 0 or 1
- eigenvalues: float32 [4096], P('col'), may hold values from 0.5 to 65536, as said below
- scales: float32 [4096], P('col'), may hold values from 0.5 to 2
Outputs:
- vectors: bfloat16 [512, 4096], P('row', 'col')
Inputs may be any that keep to these rules, and one draw needn't show every extreme that they name: `position`: each of 0 to 65535 appears once. The poles need not be sorted along the merged order, and every pole's fractional part lies within 0.05 to 0.45. `eigenvalues`: every eigenvalue's fractional part lies within 0.5 to 0.95, so that every eigenvalue stands 0.05 or more away from every pole.
All inputs are finite; a program needn't handle non-finite values. No bound on the sum of `kept` on one device may be relied on, other than what follows from the above.
Results may differ from a plain program's by a relative error of at most 0.0014.
Values may be sent and summed in bfloat16 or wider, within the bound.
No kernel may reach another device: no remote copies, remote signals or barrier semaphores. Data moves between devices by JAX's collectives and lax.ppermute only.
A program may use at most 32 MiB of HBM per device.

v0:
```python
import math

import jax
import jax.numpy as jnp
from jax import lax
from jax.sharding import PartitionSpec as P


def split_parts(cauchy):
    upper = cauchy.astype(jnp.bfloat16)
    upper = lax.optimization_barrier(upper)
    lower = (cauchy - upper.astype(jnp.float32)).astype(jnp.bfloat16)
    return (upper, lower)


def cauchy_tile(pole_data, pole_index, value_row, scale_row):
    pole_at = pole_data[0][pole_index]
    live_at = pole_data[1][pole_index]
    return live_at[:, None] / (pole_at[:, None] - value_row[None, :]) * scale_row[None, :]


def per_device(basis, position, poles, weights, kept, eigenvalues, scales):
    live_weight = weights * kept.astype(jnp.float32)
    pole_data = lax.all_gather(jnp.stack([poles, live_weight]), ("row", "col"), axis=1, tiled=True)
    row_total = lax.axis_size("row")
    child_id = lax.axis_index("row") // (row_total // 2)
    own_index = lax.dynamic_index_in_dim(position, child_id, 0, keepdims=False)
    rows_dev = basis.shape[0]
    cols_dev = eigenvalues.shape[0]
    child_index = lax.all_gather(own_index, "col", axis=0, tiled=True)
    zeros_init = jnp.zeros((rows_dev, cols_dev), jnp.float32)
    columns_in = lax.all_gather(basis, "col", axis=1, tiled=True)
    span_cols = columns_in.shape[1]
    stride = math.gcd(span_cols, 4096)

    def add_block(block_id, partial_sum):
        offset = block_id * stride
        cols_block = lax.dynamic_slice_in_dim(columns_in, offset, stride, 1)
        pole_index = lax.dynamic_slice_in_dim(child_index, offset, stride, 0)
        upper, lower = split_parts(cauchy_tile(pole_data, pole_index, eigenvalues, scales))
        first_term = jnp.dot(cols_block, upper, preferred_element_type=jnp.float32)
        second_term = jnp.dot(cols_block, lower, preferred_element_type=jnp.float32)
        return partial_sum + (first_term + second_term)

    summed = lax.fori_loop(0, span_cols // stride, add_block, zeros_init)
    return summed.astype(jnp.bfloat16)


def solution(mesh):
    placed = (
        P("row", "col"),
        P(None, "col"),
        P(("row", "col")),
        P(("row", "col")),
        P(("row", "col")),
        P("col"),
        P("col"),
    )
    return jax.shard_map(
        per_device, mesh=mesh, in_specs=placed, out_specs=P("row", "col"), check_vma=False
    )
```

profile of v0, /device:TPU:1, one launch (start us, length us, event | category | flops | bytes accessed | tf_op | source)
XLA Modules:
  0.0 1911.4 jit_solution(1081193160782693395)
XLA Ops:
  8.6 1429.9 %all-gather.1 = f32[1024,64,2]{1,2,0:T(2,128)S(1)} all-gather(f32[1,64,2]{1,2,0:T(2,128)S(1)} %maximum_bitcast_fusion), channel_id=1, replica_groups=mesh['row'=32,'col'=32] {'row','col'}, dimensions={0}, use_global_device_ids=true | all-gather | bytes 524800 | tf_op jit(solution)/shard_map/all_gather | solution.py:24
  1439.2 46.9 %all-gather = s32[1,32768]{1,0:T(1,128)S(1)} all-gather(s32[1,1024]{1,0:T(1,128)S(1)} %constant_dynamic-slice_fusion), channel_id=2, replica_groups=mesh['row'=32,'col'=32] {'col'}, dimensions={1}, use_global_device_ids=true | all-gather | bytes 135168 | tf_op jit(solution)/shard_map/all_gather | solution.py:30
  1486.0 418.0 %while.14 = (s32[]{:T(128)}, f32[16,128]{1,0:T(8,128)S(1)}, bf16[16,32768]{1,0:T(8,128)(2,1)}, f32[2,65536]{1,0:T(2,128)S(1)}, s32[32768]{0:T(1024)S(1)}, /*inde...) while((s32[]{:T(128)}, f32[16,128]{1,0:T(8,128)S(1)}, ...), condition=%wide.region_1.2_spmd.clone, body=%wide.region_0.1_spmd.clone.sunk | while | flops 38819844 | bytes 4688049 | solution.py:45
  1486.5 23.0 %gather_fusion.1 = f32[4096]{0:T(1024)S(1)} fusion(f32[65536]{0:T(1024)S(1)} %bitcast.21, s32[4096]{0:T(1024)S(1)} %fusion.22), kind=kCustom, calls=%fused_computation.clone.clone.1 | custom fusion | bytes 49152 | tf_op jit(solution)/shard_map/while/body/eval_jaxpr/gather | solution.py:18
  1509.5 23.0 %gather_fusion = f32[4096]{0:T(1024)S(1)} fusion(f32[65536]{0:T(1024)S(1)} %bitcast.20, s32[4096]{0:T(1024)S(1)} %fusion.22), kind=kCustom, calls=%fused_computation.1.clone.clone.1 | custom fusion | bytes 49152 | tf_op jit(solution)/shard_map/while/body/eval_jaxpr/gather | solution.py:17
  1532.6 2.4 fusion.23
  1538.7 23.0 %gather_fusion.1 = f32[4096]{0:T(1024)S(1)} fusion(f32[65536]{0:T(1024)S(1)} %bitcast.21, s32[4096]{0:T(1024)S(1)} %fusion.22), kind=kCustom, calls=%fused_computation.clone.clone.1 | custom fusion | bytes 49152 | tf_op jit(solution)/shard_map/while/body/eval_jaxpr/gather | solution.py:18
  1561.8 23.0 %gather_fusion = f32[4096]{0:T(1024)S(1)} fusion(f32[65536]{0:T(1024)S(1)} %bitcast.20, s32[4096]{0:T(1024)S(1)} %fusion.22), kind=kCustom, calls=%fused_computation.1.clone.clone.1 | custom fusion | bytes 49152 | tf_op jit(solution)/shard_map/while/body/eval_jaxpr/gather | solution.py:17
  1584.8 2.4 fusion.23
  1591.0 23.0 %gather_fusion.1 = f32[4096]{0:T(1024)S(1)} fusion(f32[65536]{0:T(1024)S(1)} %bitcast.21, s32[4096]{0:T(1024)S(1)} %fusion.22), kind=kCustom, calls=%fused_computation.clone.clone.1 | custom fusion | bytes 49152 | tf_op jit(solution)/shard_map/while/body/eval_jaxpr/gather | solution.py:18
  1614.0 23.0 %gather_fusion = f32[4096]{0:T(1024)S(1)} fusion(f32[65536]{0:T(1024)S(1)} %bitcast.20, s32[4096]{0:T(1024)S(1)} %fusion.22), kind=kCustom, calls=%fused_computation.1.clone.clone.1 | custom fusion | bytes 49152 | tf_op jit(solution)/shard_map/while/body/eval_jaxpr/gather | solution.py:17
  1637.1 2.4 fusion.23
  1643.2 23.0 %gather_fusion.1 = f32[4096]{0:T(1024)S(1)} fusion(f32[65536]{0:T(1024)S(1)} %bitcast.21, s32[4096]{0:T(1024)S(1)} %fusion.22), kind=kCustom, calls=%fused_computation.clone.clone.1 | custom fusion | bytes 49152 | tf_op jit(solution)/shard_map/while/body/eval_jaxpr/gather | solution.py:18
  1666.3 23.0 %gather_fusion = f32[4096]{0:T(1024)S(1)} fusion(f32[65536]{0:T(1024)S(1)} %bitcast.20, s32[4096]{0:T(1024)S(1)} %fusion.22), kind=kCustom, calls=%fused_computation.1.clone.clone.1 | custom fusion | bytes 49152 | tf_op jit(solution)/shard_map/while/body/eval_jaxpr/gather | solution.py:17
  1689.3 2.4 fusion.23
  1695.5 23.0 %gather_fusion.1 = f32[4096]{0:T(1024)S(1)} fusion(f32[65536]{0:T(1024)S(1)} %bitcast.21, s32[4096]{0:T(1024)S(1)} %fusion.22), kind=kCustom, calls=%fused_computation.clone.clone.1 | custom fusion | bytes 49152 | tf_op jit(solution)/shard_map/while/body/eval_jaxpr/gather | solution.py:18
  1718.5 23.0 %gather_fusion = f32[4096]{0:T(1024)S(1)} fusion(f32[65536]{0:T(1024)S(1)} %bitcast.20, s32[4096]{0:T(1024)S(1)} %fusion.22), kind=kCustom, calls=%fused_computation.1.clone.clone.1 | custom fusion | bytes 49152 | tf_op jit(solution)/shard_map/while/body/eval_jaxpr/gather | solution.py:17
  1741.5 2.4 fusion.23
  1747.7 23.0 %gather_fusion.1 = f32[4096]{0:T(1024)S(1)} fusion(f32[65536]{0:T(1024)S(1)} %bitcast.21, s32[4096]{0:T(1024)S(1)} %fusion.22), kind=kCustom, calls=%fused_computation.clone.clone.1 | custom fusion | bytes 49152 | tf_op jit(solution)/shard_map/while/body/eval_jaxpr/gather | solution.py:18
  1770.7 23.0 %gather_fusion = f32[4096]{0:T(1024)S(1)} fusion(f32[65536]{0:T(1024)S(1)} %bitcast.20, s32[4096]{0:T(1024)S(1)} %fusion.22), kind=kCustom, calls=%fused_computation.1.clone.clone.1 | custom fusion | bytes 49152 | tf_op jit(solution)/shard_map/while/body/eval_jaxpr/gather | solution.py:17
  1799.9 23.0 %gather_fusion.1 = f32[4096]{0:T(1024)S(1)} fusion(f32[65536]{0:T(1024)S(1)} %bitcast.21, s32[4096]{0:T(1024)S(1)} %fusion.22), kind=kCustom, calls=%fused_computation.clone.clone.1 | custom fusion | bytes 49152 | tf_op jit(solution)/shard_map/while/body/eval_jaxpr/gather | solution.py:18
  1823.0 23.0 %gather_fusion = f32[4096]{0:T(1024)S(1)} fusion(f32[65536]{0:T(1024)S(1)} %bitcast.20, s32[4096]{0:T(1024)S(1)} %fusion.22), kind=kCustom, calls=%fused_computation.1.clone.clone.1 | custom fusion | bytes 49152 | tf_op jit(solution)/shard_map/while/body/eval_jaxpr/gather | solution.py:17
  1852.2 23.0 %gather_fusion.1 = f32[4096]{0:T(1024)S(1)} fusion(f32[65536]{0:T(1024)S(1)} %bitcast.21, s32[4096]{0:T(1024)S(1)} %fusion.22), kind=kCustom, calls=%fused_computation.clone.clone.1 | custom fusion | bytes 49152 | tf_op jit(solution)/shard_map/while/body/eval_jaxpr/gather | solution.py:18
  1875.2 23.0 %gather_fusion = f32[4096]{0:T(1024)S(1)} fusion(f32[65536]{0:T(1024)S(1)} %bitcast.20, s32[4096]{0:T(1024)S(1)} %fusion.22), kind=kCustom, calls=%fused_computation.1.clone.clone.1 | custom fusion | bytes 49152 | tf_op jit(solution)/shard_map/while/body/eval_jaxpr/gather | solution.py:17
  (51 shorter events, 40.4 us)
Async XLA Ops:
  6.5 1432.6 %copy-start = (s32[2,1024]{1,0:T(2,128)S(1)}, s32[2,1024]{1,0:T(2,128)}, u32[]{:S(2)}) copy-start(s32[2,1024]{1,0:T(2,128)} %param.10) | copy-start | bytes 24580
  6.5 1479.5 %all-gather.4.cloned.1.call-start = ((), (), s32[]{:S(2)}) async-start(), calls=%async_computation | async-start | bytes 1081344 | tf_op jit(solution)/shard_map/all_gather | solution.py:32
  1438.6 47.5 %copy-start.1 = (f32[128]{0:T(128)S(1)}, f32[128]{0:T(128)}, u32[]{:S(2)}) copy-start(f32[128]{0:T(128)} %param.14) | copy-start | bytes 1540
  1438.6 47.5 %copy-start.2 = (f32[128]{0:T(128)S(1)}, f32[128]{0:T(128)}, u32[]{:S(2)}) copy-start(f32[128]{0:T(128)} %param.15) | copy-start | bytes 1540
Sparse Core Ops, SparseCore 0:
  11.9 107.3 all-gather.3
where the time goes:
time: 1930 us; the launch traced here: 1910 us
  blocking collectives  1480 us (77%)
  local copies, waits for them, and re-layouts  372 us (19%)
  matrix products  26.7 us (1%)
  other arithmetic  21.1 us (1%)
    all_gather x1, blocking collectives, per_device(): lax.all_gather(jnp.stack([poles, live_weight]), ('row', 'col'), axis=1, t...  1430 us
    gather x8, local copies, waits for them, and re-layouts, cauchy_tile(): live_at = pole_data[1][pole_index]  184 us
    gather x8, local copies, waits for them, and re-layouts, cauchy_tile(): pole_at = pole_data[0][pole_index]  184 us
    all_gather x1, blocking collectives, per_device(): child_index = lax.all_gather(own_index, 'col', axis=0, tiled=True)  46.9 us
  transfers between devices with their start and end apart: 1, of which 0 were waited for; matrix products, arithmetic and copies ran while one was open for 0% of the time, Pallas kernels for 0%

commit v1 on v0

--- a/solution.py
+++ b/solution.py
@@ -13,21 +13,21 @@
     return (upper, lower)
 
 
-def cauchy_tile(pole_data, pole_index, value_row, scale_row):
-    pole_at = pole_data[0][pole_index]
-    live_at = pole_data[1][pole_index]
+def cauchy_tile(pole_at, live_at, value_row, scale_row):
     return live_at[:, None] / (pole_at[:, None] - value_row[None, :]) * scale_row[None, :]
 
 
 def per_device(basis, position, poles, weights, kept, eigenvalues, scales):
     live_weight = weights * kept.astype(jnp.float32)
-    pole_data = lax.all_gather(jnp.stack([poles, live_weight]), ("row", "col"), axis=1, tiled=True)
+    pole_data = lax.all_gather(jnp.stack([poles, live_weight]), "col", axis=1, tiled=True)
+    pole_data = lax.all_gather(pole_data, "row", axis=1, tiled=True)
     row_total = lax.axis_size("row")
     child_id = lax.axis_index("row") // (row_total // 2)
     own_index = lax.dynamic_index_in_dim(position, child_id, 0, keepdims=False)
+    own_poles = jnp.stack([pole_data[0][own_index], pole_data[1][own_index]])
+    child_poles = lax.all_gather(own_poles, "col", axis=1, tiled=True)
     rows_dev = basis.shape[0]
     cols_dev = eigenvalues.shape[0]
-    child_index = lax.all_gather(own_index, "col", axis=0, tiled=True)
     zeros_init = jnp.zeros((rows_dev, cols_dev), jnp.float32)
     columns_in = lax.all_gather(basis, "col", axis=1, tiled=True)
     span_cols = columns_in.shape[1]
@@ -36,8 +36,8 @@
     def add_block(block_id, partial_sum):
         offset = block_id * stride
         cols_block = lax.dynamic_slice_in_dim(columns_in, offset, stride, 1)
-        pole_index = lax.dynamic_slice_in_dim(child_index, offset, stride, 0)
-        upper, lower = split_parts(cauchy_tile(pole_data, pole_index, eigenvalues, scales))
+        poles_block = lax.dynamic_slice_in_dim(child_poles, offset, stride, 1)
+        upper, lower = split_parts(cauchy_tile(poles_block[0], poles_block[1], eigenvalues, scales))
         first_term = jnp.dot(cols_block, upper, preferred_element_type=jnp.float32)
         second_term = jnp.dot(cols_block, lower, preferred_element_type=jnp.float32)
         return partial_sum + (first_term + second_term)

time: 1930 us -> 271 us (0.14)
  blocking collectives: 1480 us -> 195 us
  local copies, waits for them, and re-layouts: 372 us -> 13.7 us
    all_gather x2 -> x3, blocking collectives: 1480 us -> 195 us  [the longest x1 68.5 us: per_device(): lax.all_gather(jnp.stack([poles, live_weight]), 'col', axis=1, tiled=True)]
    gather x16 -> x2, local copies, waits for them, and re-layouts: 369 us -> 12.3 us  [per_device(): own_poles = jnp.stack([pole_data[0][own_index], pole_data[1][own_index]])]
  transfers between devices with their start and end apart: 1 -> 1, of which waited for: 0 -> 0; matrix products, arithmetic and copies ran while one was open for 0% -> 5% of each run, Pallas kernels for 0% -> 0%
where the time goes in v1:
time: 271 us
  blocking collectives  195 us (72%)
  matrix products  26.7 us (10%)
  other arithmetic  21.1 us (8%)
  local copies, waits for them, and re-layouts  13.7 us (5%)
  between operations  13.5 us (5%)
    all_gather x1, blocking collectives, per_device(): lax.all_gather(jnp.stack([poles, live_weight]), 'col', axis=1, tiled=True)  68.5 us
    all_gather x1, blocking collectives, per_device(): pole_data = lax.all_gather(pole_data, 'row', axis=1, tiled=True)  66.5 us
    all_gather x1, blocking collectives, per_device(): child_poles = lax.all_gather(own_poles, 'col', axis=1, tiled=True)  59.9 us
    convert_element_type x8, other arithmetic, split_parts(): upper = cauchy.astype(jnp.bfloat16)  19.1 us
    dot_general x8, matrix products, add_block(): second_term = jnp.dot(cols_block, lower, preferred_element_type=jnp.float32)  17.4 us
    gather x2, local copies, waits for them, and re-layouts, per_device(): own_poles = jnp.stack([pole_data[0][own_index], pole_data[1][own_index]])  12.3 us
    dot_general x8, matrix products, add_block(): first_term = jnp.dot(cols_block, upper, preferred_element_type=jnp.float32)  9.26 us
  transfers between devices with their start and end apart: 1, of which 0 were waited for; matrix products, arithmetic and copies ran while one was open for 5% of the time, Pallas kernels for 0%

profile of v1, /device:TPU:1, one launch (start us, length us, event | category | flops | bytes accessed | tf_op | source)
XLA Modules:
  0.0 270.6 jit_solution(12250340465681392625)
XLA Ops:
  8.6 68.5 %all-gather = f32[32,64,2]{1,2,0:T(2,128)S(1)} all-gather(f32[1,64,2]{1,2,0:T(2,128)S(1)} %maximum_bitcast_fusion), channel_id=1, replica_groups=mesh['row'=32,'col'=32] {'col'}, dimensions={0}, use_global_device_ids=true | all-gather | bytes 16896 | tf_op jit(solution)/shard_map/all_gather | solution.py:22
  77.1 66.5 %all_gather.14 = f32[2,65536]{1,0:T(2,128)S(1)} all-gather(f32[2,2048]{1,0:T(2,128)S(1)} %bitcast.32), channel_id=1, replica_groups=mesh['row'=32,'col'=32] {'row'}, dimensions={1}, use_global_device_ids=true | all-gather | bytes 540672 | tf_op jit(solution)/shard_map/all_gather | solution.py:23
  144.1 6.2 %gather_fusion = f32[1024]{0:T(1024)S(1)} fusion(f32[65536]{0:T(1024)S(1)} %bitcast.27, s32[1024]{0:T(1024)S(1)} %broadcast_clamp_fusion), kind=kCustom, calls=%fused_computation | custom fusion | bytes 12288 | tf_op jit(solution)/shard_map/gather | solution.py:27
  150.3 6.2 %gather_fusion.1 = f32[1024]{0:T(1024)S(1)} fusion(f32[65536]{0:T(1024)S(1)} %bitcast.26, s32[1024]{0:T(1024)S(1)} %broadcast_clamp_fusion), kind=kCustom, calls=%fused_computation.1 | custom fusion | bytes 12288 | tf_op jit(solution)/shard_map/gather | solution.py:27
  156.5 59.9 %all_gather.15 = f32[2,32768]{1,0:T(2,128)S(1)} all-gather(f32[2,1024]{1,0:T(2,128)S(1)} %pad_maximum_fusion), channel_id=1, replica_groups=mesh['row'=32,'col'=32] {'col'}, dimensions={1}, use_global_device_ids=true | all-gather | bytes 270336 | tf_op jit(solution)/shard_map/all_gather | solution.py:28
  216.4 46.8 %while.14 = (s32[]{:T(128)}, f32[16,128]{1,0:T(8,128)S(1)}, bf16[16,32768]{1,0:T(8,128)(2,1)}, f32[2,32768]{1,0:T(2,128)S(1)}, f32[128]{0:T(128)S(1)}, /*index=5...) while((s32[]{:T(128)}, f32[16,128]{1,0:T(8,128)S(1)}, ...), condition=%wide.region_1.2_spmd.clone, body=%wide.region_0.1_spmd.clone.sunk | while | flops 38803464 | bytes 3573961 | solution.py:45
  216.5 2.4 fusion.21
  220.1 2.2 fusion.23
  222.4 2.4 fusion.21
  224.8 1.2 fusion.22
  225.9 2.2 fusion.23
  228.2 2.4 fusion.21
  230.6 1.2 fusion.22
  231.8 2.2 fusion.23
  234.1 2.4 fusion.21
  237.6 2.2 fusion.23
  239.9 2.4 fusion.21
  243.5 2.2 fusion.23
  245.8 2.4 fusion.21
  249.3 2.2 fusion.23
  251.6 2.4 fusion.21
  255.2 2.2 fusion.23
  257.4 2.4 fusion.21
  261.0 2.2 fusion.23
  (33 shorter events, 11.0 us)
Async XLA Ops:
  6.5 137.6 %copy-start.2 = (s32[2,1024]{1,0:T(2,128)S(1)}, s32[2,1024]{1,0:T(2,128)}, u32[]{:S(2)}) copy-start(s32[2,1024]{1,0:T(2,128)} %param.10) | copy-start | bytes 24580
  6.5 209.9 %all-gather.3.cloned.1.call-start = ((), (), s32[]{:S(2)}) async-start(), calls=%async_computation | async-start | bytes 1081344 | tf_op jit(solution)/shard_map/all_gather | solution.py:32
  150.3 66.1 %copy-start = (f32[128]{0:T(128)S(1)}, f32[128]{0:T(128)}, u32[]{:S(2)}) copy-start(f32[128]{0:T(128)} %param.14) | copy-start | bytes 1540
  150.3 66.1 %copy-start.1 = (f32[128]{0:T(128)S(1)}, f32[128]{0:T(128)}, u32[]{:S(2)}) copy-start(f32[128]{0:T(128)} %param.15) | copy-start | bytes 1540
Sparse Core Ops, SparseCore 0:
  11.9 108.5 all-gather.2

commit v2 on v1

v2 whole, which is shorter than its diff:
```python
import jax
import jax.numpy as jnp
from jax import lax
from jax.sharding import PartitionSpec as P


def split_parts(cauchy):
    upper = cauchy.astype(jnp.bfloat16)
    upper = lax.optimization_barrier(upper)
    lower = (cauchy - upper.astype(jnp.float32)).astype(jnp.bfloat16)
    return (upper, lower)


def cauchy_tile(pole_at, live_at, value_row, scale_row):
    return live_at[:, None] / (pole_at[:, None] - value_row[None, :]) * scale_row[None, :]


def per_device(basis, position, poles, weights, kept, eigenvalues, scales):
    live_weight = weights * kept.astype(jnp.float32)
    pole_data = lax.all_gather(jnp.stack([poles, live_weight]), "col", axis=1, tiled=True)
    pole_data = lax.all_gather(pole_data, "row", axis=1, tiled=True)
    row_total = lax.axis_size("row")
    child_id = lax.axis_index("row") // (row_total // 2)
    own_index = lax.dynamic_index_in_dim(position, child_id, 0, keepdims=False)
    pole_at = pole_data[0][own_index]
    live_at = pole_data[1][own_index]
    value_data = lax.all_gather(jnp.stack([eigenvalues, scales]), "col", axis=1, tiled=True)
    span_new = value_data.shape[1]
    stride = 512

    def add_block(block_id, partial):
        offset = block_id * stride
        values = lax.dynamic_slice_in_dim(value_data, offset, stride, 1)
        upper, lower = split_parts(cauchy_tile(pole_at, live_at, values[0], values[1]))
        first_term = jnp.dot(basis, upper, preferred_element_type=jnp.float32)
        second_term = jnp.dot(basis, lower, preferred_element_type=jnp.float32)
        return lax.dynamic_update_slice_in_dim(partial, first_term + second_term, offset, 1)

    partial = jnp.zeros((basis.shape[0], span_new), jnp.float32)
    partial = lax.fori_loop(0, span_new // stride, add_block, partial)
    summed = lax.psum_scatter(partial, "col", scatter_dimension=1, tiled=True)
    return summed.astype(jnp.bfloat16)


def solution(mesh):
    placed = (
        P("row", "col"),
        P(None, "col"),
        P(("row", "col")),
        P(("row", "col")),
        P(("row", "col")),
        P("col"),
        P("col"),
    )
    return jax.shard_map(
        per_device, mesh=mesh, in_specs=placed, out_specs=P("row", "col"), check_vma=False
    )
```

time: 271 us -> 358 us (1.32); the launches traced: 271 us -> 353 us
  waiting for transfers between devices: 0.71 us -> 131 us
  matrix products: 26.7 us -> 7.12 us
  blocking collectives: 195 us -> 180 us
  other arithmetic: 21.1 us -> 7.11 us
    reduce_scatter x0 -> x1, waiting for transfers between devices: none -> 131 us  [per_device(): summed = lax.psum_scatter(partial, 'col', scatter_dimension=1, tiled=True)]
    all_gather x1, blocking collectives: 68.5 us -> 46.3 us  [per_device(): lax.all_gather(jnp.stack([poles, live_weight]), 'col', axis=1, tiled=True)]
    dot_general x16, matrix products: 26.7 us -> 7.12 us  [the longest x8 5.21 us: add_block(): second_term = jnp.dot(basis, lower, preferred_element_type=jnp.float32)]
    convert_element_type x8, other arithmetic: 19.1 us -> 3.09 us  [split_parts(): upper = cauchy.astype(jnp.bfloat16)]
    all_gather x1, blocking collectives: 59.9 us -> 68.4 us  [per_device(): lax.all_gather(jnp.stack([eigenvalues, scales]), 'col', axis=1, tiled=True)]
  transfers between devices with their start and end apart: 1 -> 1, of which waited for: 0 -> 1; matrix products, arithmetic and copies ran while one was open for 5% -> 0% of each run, Pallas kernels for 0% -> 0%
where the time goes in v2:
time: 358 us; the launch traced here: 353 us
  blocking collectives  180 us (50%)
  waiting for transfers between devices  131 us (37%)
  local copies, waits for them, and re-layouts  14.1 us (4%)
  between operations  13.5 us (4%)
  matrix products  7.12 us (2%)
  other arithmetic  7.11 us (2%)
    reduce_scatter x1, waiting for transfers between devices, per_device(): summed = lax.psum_scatter(partial, 'col', scatter_dimension=1, tiled=True)  131 us
    all_gather x1, blocking collectives, per_device(): lax.all_gather(jnp.stack([eigenvalues, scales]), 'col', axis=1, tiled=True)  68.4 us
    all_gather x1, blocking collectives, per_device(): pole_data = lax.all_gather(pole_data, 'row', axis=1, tiled=True)  65.7 us
    all_gather x1, blocking collectives, per_device(): lax.all_gather(jnp.stack([poles, live_weight]), 'col', axis=1, tiled=True)  46.3 us
  transfers between devices with their start and end apart: 1, of which 1 were waited for; matrix products, arithmetic and copies ran while one was open for 0% of the time, Pallas kernels for 0%

profile of v2, /device:TPU:1, one launch (start us, length us, event | category | flops | bytes accessed | tf_op | source)
XLA Modules:
  0.0 353.3 jit_solution(14180974313478579957)
XLA Ops:
  6.5 0.7 compare_select_fusion
  7.3 0.7 pad_maximum_fusion
  7.9 68.4 %all_gather.11 = f32[2,4096]{1,0:T(2,128)S(1)} all-gather(f32[2,128]{1,0:T(2,128)S(1)} %pad_maximum_fusion), channel_id=1, replica_groups=mesh['row'=32,'col'=32] {'col'}, dimensions={1}, use_global_device_ids=true | all-gather | bytes 33792 | tf_op jit(solution)/shard_map/all_gather | solution.py:27
  76.4 0.7 multiply_bitcast_fusion
  77.1 0.7 maximum_bitcast_fusion
  77.7 46.3 %all-gather = f32[32,64,2]{1,2,0:T(2,128)S(1)} all-gather(f32[1,64,2]{1,2,0:T(2,128)S(1)} %maximum_bitcast_fusion), channel_id=1, replica_groups=mesh['row'=32,'col'=32] {'col'}, dimensions={0}, use_global_device_ids=true | all-gather | bytes 16896 | tf_op jit(solution)/shard_map/all_gather | solution.py:20
  124.1 65.7 %all_gather.10 = f32[2,65536]{1,0:T(2,128)S(1)} all-gather(f32[2,2048]{1,0:T(2,128)S(1)} %bitcast.44), channel_id=1, replica_groups=mesh['row'=32,'col'=32] {'row'}, dimensions={1}, use_global_device_ids=true | all-gather | bytes 540672 | tf_op jit(solution)/shard_map/all_gather | solution.py:21
  189.8 0.4 fusion.3
  190.2 6.2 %gather_fusion.1 = f32[1024]{0:T(1024)S(1)} fusion(f32[65536]{0:T(1024)S(1)} %bitcast.39, s32[1024]{0:T(1024)S(1)} %broadcast_clamp_fusion), kind=kCustom, calls=%fused_computation.1 | custom fusion | bytes 12288 | tf_op jit(solution)/shard_map/gather | solution.py:25
  196.4 6.2 %gather_fusion = f32[1024]{0:T(1024)S(1)} fusion(f32[65536]{0:T(1024)S(1)} %bitcast.38, s32[1024]{0:T(1024)S(1)} %broadcast_clamp_fusion), kind=kCustom, calls=%fused_computation | custom fusion | bytes 12288 | tf_op jit(solution)/shard_map/gather | solution.py:26
  202.6 10.9 %while.13 = (s32[]{:T(128)}, f32[16,4096]{1,0:T(8,128)S(1)}, f32[1024]{0:T(1024)S(1)}, f32[1024]{0:T(1024)S(1)}, f32[2,4096]{1,0:T(2,128)S(1)}, /*index=5*/bf16[...) while((s32[]{:T(128)}, f32[16,4096]{1,0:T(8,128)S(1)}, ...), condition=%wide.region_1.2_spmd, body=%wide.region_0.1_spmd.sunk | while | flops 38805512 | bytes 3342515 | solution.py:40
  203.3 0.7 fusion.19
  204.1 0.4 fusion.17
  204.7 0.7 fusion.19
  205.4 0.4 fusion.17
  206.1 0.7 fusion.19
  207.4 0.7 fusion.19
  208.8 0.7 fusion.19
  210.1 0.7 fusion.19
  211.5 0.7 fusion.19
  212.9 0.7 fusion.19
  213.5 0.7 copy-done
  214.2 131.0 %reduce-scatter.2.cloned.1.call-done = f32[16,128]{1,0:T(8,128)} async-done(((f32[16,4096]{1,0:T(8,128)}), f32[16,128]{1,0:T(8,128)}) %reduce-scatter.2.cloned.1.call-update) | async-done | bytes 8208 | tf_op jit(solution)/shard_map/reduce_scatter | solution.py:41
  345.2 1.3 convert_element_type.28
  (31 shorter events, 5.0 us)
Async XLA Ops:
  6.5 338.7 %reduce-scatter.2.cloned.1.call-start = ((), (), s32[]{:S(2)}) async-start(), calls=%async_computation.1 | async-start | bytes 270336 | tf_op jit(solution)/shard_map/reduce_scatter | solution.py:41
  196.4 6.2 %copy-start.1 = (bf16[16,1024]{1,0:T(8,128)(2,1)S(1)}, bf16[16,1024]{1,0:T(8,128)(2,1)}, u32[]{:S(2)}) copy-start(bf16[16,1024]{1,0:T(8,128)(2,1)} %param.9) | copy-start | bytes 98308
  213.5 0.7 copy-start
Sparse Core Ops, SparseCore 0:
  214.4 130.7 reduce-scatter.1

commit v3 on v1

--- a/solution.py
+++ b/solution.py
@@ -17,15 +17,28 @@
     return live_at[:, None] / (pole_at[:, None] - value_row[None, :]) * scale_row[None, :]
 
 
+def gather_by_pairs(block, axis):
+    size = lax.axis_size(axis)
+    index = lax.axis_index(axis)
+    held = block
+    step = 1
+    while step < size:
+        other = lax.ppermute(held, axis, perm=[(i, i ^ step) for i in range(size)])
+        low_half = (index // step) % 2 == 0
+        held = jnp.where(low_half, jnp.concatenate([held, other], -1), jnp.concatenate([other, held], -1))
+        step *= 2
+    return held
+
+
 def per_device(basis, position, poles, weights, kept, eigenvalues, scales):
     live_weight = weights * kept.astype(jnp.float32)
-    pole_data = lax.all_gather(jnp.stack([poles, live_weight]), "col", axis=1, tiled=True)
-    pole_data = lax.all_gather(pole_data, "row", axis=1, tiled=True)
+    pole_data = gather_by_pairs(jnp.stack([poles, live_weight]), "col")
+    pole_data = gather_by_pairs(pole_data, "row")
     row_total = lax.axis_size("row")
     child_id = lax.axis_index("row") // (row_total // 2)
     own_index = lax.dynamic_index_in_dim(position, child_id, 0, keepdims=False)
     own_poles = jnp.stack([pole_data[0][own_index], pole_data[1][own_index]])
-    child_poles = lax.all_gather(own_poles, "col", axis=1, tiled=True)
+    child_poles = gather_by_pairs(own_poles, "col")
     rows_dev = basis.shape[0]
     cols_dev = eigenvalues.shape[0]
     zeros_init = jnp.zeros((rows_dev, cols_dev), jnp.float32)

time: 271 us -> 293 us (1.081)
  blocking collectives: 195 us -> 0 us
  waiting for transfers between devices: 0.71 us -> 139 us
  starting transfers between devices: 0.01 us -> 76.1 us
    all_gather x3 -> x0, blocking collectives: 195 us -> none  [the longest x1 68.5 us: per_device(): lax.all_gather(jnp.stack([poles, live_weight]), 'col', axis=1, tiled=True)]
    all_gather x1, waiting for transfers between devices: 0.01 us -> 89.6 us  [per_device(): columns_in = lax.all_gather(basis, 'col', axis=1, tiled=True)]
    ppermute x0 -> x15, starting transfers between devices: none -> 76.1 us  [gather_by_pairs(): other = lax.ppermute(held, axis, perm=[(i, i ^ step) for i in range(size)])]
    ppermute x0 -> x15, waiting for transfers between devices: none -> 49.6 us  [gather_by_pairs(): other = lax.ppermute(held, axis, perm=[(i, i ^ step) for i in range(size)])]
  transfers between devices with their start and end apart: 1 -> 16, of which waited for: 0 -> 16; matrix products, arithmetic and copies ran while one was open for 5% -> 0% of each run, Pallas kernels for 0% -> 0%
where the time goes in v3:
time: 293 us
  waiting for transfers between devices  139 us (47%)
  starting transfers between devices  76.1 us (26%)
  matrix products  26.7 us (9%)
  other arithmetic  23 us (8%)
  between operations  13.9 us (5%)
  local copies, waits for them, and re-layouts  13.6 us (5%)
    all_gather x1, waiting for transfers between devices, per_device(): columns_in = lax.all_gather(basis, 'col', axis=1, tiled=True)  89.6 us
    ppermute x15, starting transfers between devices, gather_by_pairs(): other = lax.ppermute(held, axis, perm=[(i, i ^ step) for i in range(size)])  76.1 us
    ppermute x15, waiting for transfers between devices, gather_by_pairs(): other = lax.ppermute(held, axis, perm=[(i, i ^ step) for i in range(size)])  49.6 us
    convert_element_type x8, other arithmetic, split_parts(): upper = cauchy.astype(jnp.bfloat16)  19.1 us
    dot_general x8, matrix products, add_block(): second_term = jnp.dot(cols_block, lower, preferred_element_type=jnp.float32)  17.4 us
    gather x2, local copies, waits for them, and re-layouts, per_device(): own_poles = jnp.stack([pole_data[0][own_index], pole_data[1][own_index]])  12.3 us
    dot_general x8, matrix products, add_block(): first_term = jnp.dot(cols_block, upper, preferred_element_type=jnp.float32)  9.26 us
  transfers between devices with their start and end apart: 16, of which 16 were waited for; matrix products, arithmetic and copies ran while one was open for 0% of the time, Pallas kernels for 0%

profile of v3, /device:TPU:1, one launch (start us, length us, event | category | flops | bytes accessed | tf_op | source)
XLA Modules:
  0.0 292.6 jit_solution(4570889590483868592)
XLA Ops:
  7.9 16.1 %collective-permute-start = (f32[2,64]{1,0:T(2,128)S(1)}, f32[2,64]{1,0:T(2,128)S(1)}, u32[]{:S(2)}, u32[]{:S(2)}) collective-permute-start(f32[2,64]{1,0:T(2,128)S(1)} %pad_maximum_fusion.1), channel_id=1, source_target_pairs={{0,1},{1,0},{2,3},{3,2},{4,5},{5,4},{6,7},{7,6},{8,9},{9,8},{10,11... | collective-permute-start | bytes 1544 | tf_op jit(solution)/shard_map/ppermute | solution.py:26
  31.8 3.3 %collective-permute-done.2 = f32[2,256]{1,0:T(2,128)S(1)} collective-permute-done((f32[2,256]{1,0:T(2,128)S(1)}, f32[2,256]{1,0:T(2,128)S(1)}, u32[]{:S(2)}, u32[]{:S(2)}) %collective-permute-start.2) | collective-permute-done | bytes 2080 | tf_op jit(solution)/shard_map/ppermute | solution.py:26
  35.1 3.8 %collective-permute-start.3 = (f32[2,512]{1,0:T(2,128)S(1)}, f32[2,512]{1,0:T(2,128)S(1)}, u32[]{:S(2)}, u32[]{:S(2)}) collective-permute-start(f32[2,512]{1,0:T(2,128)S(1)} %maximum_select_fusion.12), channel_id=1, source_target_pairs={{0,8},{1,9},{2,10},{3,11},{4,12},{5,13},{6,14},{7,15},{8,0},{9,1},... | collective-permute-start | bytes 12296 | tf_op jit(solution)/shard_map/ppermute | solution.py:26
  39.0 4.4 %collective-permute-done.3 = f32[2,512]{1,0:T(2,128)S(1)} collective-permute-done((f32[2,512]{1,0:T(2,128)S(1)}, f32[2,512]{1,0:T(2,128)S(1)}, u32[]{:S(2)}, u32[]{:S(2)}) %collective-permute-start.3) | collective-permute-done | bytes 4128 | tf_op jit(solution)/shard_map/ppermute | solution.py:26
  43.3 4.5 %collective-permute-start.4 = (f32[2,1024]{1,0:T(2,128)S(1)}, f32[2,1024]{1,0:T(2,128)S(1)}, u32[]{:S(2)}, u32[]{:S(2)}) collective-permute-start(f32[2,1024]{1,0:T(2,128)S(1)} %maximum_select_fusion.11), channel_id=1, source_target_pairs={{0,16},{1,17},{2,18},{3,19},{4,20},{5,21},{6,22},{7,23},{8,24},{9,... | collective-permute-start | bytes 24584 | tf_op jit(solution)/shard_map/ppermute | solution.py:26
  47.8 3.8 %collective-permute-done.4 = f32[2,1024]{1,0:T(2,128)S(1)} collective-permute-done((f32[2,1024]{1,0:T(2,128)S(1)}, f32[2,1024]{1,0:T(2,128)S(1)}, u32[]{:S(2)}, u32[]{:S(2)}) %collective-permute-start.4) | collective-permute-done | bytes 8224 | tf_op jit(solution)/shard_map/ppermute | solution.py:26
  53.6 2.6 collective-permute-done.5
  58.1 3.7 %collective-permute-done.6 = f32[2,4096]{1,0:T(2,128)S(1)} collective-permute-done((f32[2,4096]{1,0:T(2,128)S(1)}, f32[2,4096]{1,0:T(2,128)S(1)}, u32[]{:S(2)}, u32[]{:S(2)}) %collective-permute-start.6) | collective-permute-done | bytes 32800 | tf_op jit(solution)/shard_map/ppermute | solution.py:26
  63.9 3.1 %collective-permute-done.7 = f32[2,8192]{1,0:T(2,128)S(1)} collective-permute-done((f32[2,8192]{1,0:T(2,128)S(1)}, f32[2,8192]{1,0:T(2,128)S(1)}, u32[]{:S(2)}, u32[]{:S(2)}) %collective-permute-start.7) | collective-permute-done | bytes 65568 | tf_op jit(solution)/shard_map/ppermute | solution.py:26
  68.9 6.0 %collective-permute-done.8 = f32[2,16384]{1,0:T(2,128)S(1)} collective-permute-done((f32[2,16384]{1,0:T(2,128)S(1)}, f32[2,16384]{1,0:T(2,128)S(1)}, u32[]{:S(2)}, u32[]{:S(2)}) %collective-permute-start.8) | collective-permute-done | bytes 131104 | tf_op jit(solution)/shard_map/ppermute | solution.py:26
  75.2 4.5 %collective-permute-start.9 = (f32[2,32768]{1,0:T(2,128)S(1)}, f32[2,32768]{1,0:T(2,128)S(1)}, u32[]{:S(2)}, u32[]{:S(2)}) collective-permute-start(f32[2,32768]{1,0:T(2,128)S(1)} %maximum_select_fusion.1), channel_id=1, source_target_pairs={{0,512},{32,544},{64,576},{96,608},{128,640},{160,672},{192,704},{... | collective-permute-start | bytes 786440 | tf_op jit(solution)/shard_map/ppermute | solution.py:26
  79.8 9.2 %collective-permute-done.9 = f32[2,32768]{1,0:T(2,128)S(1)} collective-permute-done((f32[2,32768]{1,0:T(2,128)S(1)}, f32[2,32768]{1,0:T(2,128)S(1)}, u32[]{:S(2)}, u32[]{:S(2)}) %collective-permute-start.9) | collective-permute-done | bytes 262176 | tf_op jit(solution)/shard_map/ppermute | solution.py:26
  89.8 6.2 %gather_fusion = f32[1024]{0:T(1024)S(1)} fusion(f32[65536]{0:T(1024)S(1)} %bitcast.20, s32[1024]{0:T(1024)S(1)} %broadcast_clamp_fusion), kind=kCustom, calls=%fused_computation | custom fusion | bytes 12288 | tf_op jit(solution)/shard_map/gather | solution.py:40
  96.0 6.2 %gather_fusion.1 = f32[1024]{0:T(1024)S(1)} fusion(f32[65536]{0:T(1024)S(1)} %bitcast.19, s32[1024]{0:T(1024)S(1)} %broadcast_clamp_fusion), kind=kCustom, calls=%fused_computation.1 | custom fusion | bytes 12288 | tf_op jit(solution)/shard_map/gather | solution.py:40
  102.2 16.7 %collective-permute-start.10 = (f32[2,1024]{1,0:T(2,128)S(1)}, f32[2,1024]{1,0:T(2,128)S(1)}, u32[]{:S(2)}, u32[]{:S(2)}) collective-permute-start(f32[2,1024]{1,0:T(2,128)S(1)} %pad_maximum_fusion), channel_id=1, source_target_pairs={{0,1},{1,0},{2,3},{3,2},{4,5},{5,4},{6,7},{7,6},{8,9},{9,8},{10,11... | collective-permute-start | bytes 24584 | tf_op jit(solution)/shard_map/ppermute | solution.py:26
  119.7 3.3 %collective-permute-start.11 = (f32[2,2048]{1,0:T(2,128)S(1)}, f32[2,2048]{1,0:T(2,128)S(1)}, u32[]{:S(2)}, u32[]{:S(2)}) collective-permute-start(f32[2,2048]{1,0:T(2,128)S(1)} %maximum_select_fusion.10), channel_id=1, source_target_pairs={{0,2},{1,3},{2,0},{3,1},{4,6},{5,7},{6,4},{7,5},{8,10},{9,11},{10,... | collective-permute-start | bytes 49160 | tf_op jit(solution)/shard_map/ppermute | solution.py:26
  124.2 3.6 %collective-permute-start.12 = (f32[2,4096]{1,0:T(2,128)S(1)}, f32[2,4096]{1,0:T(2,128)S(1)}, u32[]{:S(2)}, u32[]{:S(2)}) collective-permute-start(f32[2,4096]{1,0:T(2,128)S(1)} %maximum_select_fusion.8), channel_id=1, source_target_pairs={{0,4},{1,5},{2,6},{3,7},{4,0},{5,1},{6,2},{7,3},{8,12},{9,13},{10,... | collective-permute-start | bytes 98312 | tf_op jit(solution)/shard_map/ppermute | solution.py:26
  129.8 5.5 %collective-permute-start.13 = (f32[2,8192]{1,0:T(2,128)S(1)}, f32[2,8192]{1,0:T(2,128)S(1)}, u32[]{:S(2)}, u32[]{:S(2)}) collective-permute-start(f32[2,8192]{1,0:T(2,128)S(1)} %maximum_select_fusion.6), channel_id=1, source_target_pairs={{0,8},{1,9},{2,10},{3,11},{4,12},{5,13},{6,14},{7,15},{8,0},{9,1},... | collective-permute-start | bytes 196616 | tf_op jit(solution)/shard_map/ppermute | solution.py:26
  135.3 3.5 %collective-permute-done.13 = f32[2,8192]{1,0:T(2,128)S(1)} collective-permute-done((f32[2,8192]{1,0:T(2,128)S(1)}, f32[2,8192]{1,0:T(2,128)S(1)}, u32[]{:S(2)}, u32[]{:S(2)}) %collective-permute-start.13) | collective-permute-done | bytes 65568 | tf_op jit(solution)/shard_map/ppermute | solution.py:26
  138.9 6.8 %collective-permute-start.14 = (f32[2,16384]{1,0:T(2,128)S(1)}, f32[2,16384]{1,0:T(2,128)S(1)}, u32[]{:S(2)}, u32[]{:S(2)}) collective-permute-start(f32[2,16384]{1,0:T(2,128)S(1)} %maximum_select_fusion.4), channel_id=1, source_target_pairs={{0,16},{1,17},{2,18},{3,19},{4,20},{5,21},{6,22},{7,23},{8,24},{9,... | collective-permute-start | bytes 393224 | tf_op jit(solution)/shard_map/ppermute | solution.py:26
  145.7 2.9 collective-permute-done.14
  148.8 89.6 %all-gather.2.cloned.1.call-done = bf16[16,32768]{1,0:T(8,128)(2,1)} async-done(((bf16[16,1024]{1,0:T(8,128)(2,1)}), bf16[16,32768]{1,0:T(8,128)(2,1)}) %all-gather.2.cloned.1.call-update) | async-done | bytes 1048592 | tf_op jit(solution)/shard_map/all_gather | solution.py:45
  238.4 46.8 %while.14 = (s32[]{:T(128)}, f32[16,128]{1,0:T(8,128)S(1)}, bf16[16,32768]{1,0:T(8,128)(2,1)}, f32[2,32768]{1,0:T(2,128)S(1)}, f32[128]{0:T(128)S(1)}, /*index=5...) while((s32[]{:T(128)}, f32[16,128]{1,0:T(8,128)S(1)}, ...), condition=%wide.region_1.2_spmd.clone, body=%wide.region_0.1_spmd.clone.sunk | while | flops 38803464 | bytes 3573961 | solution.py:58
  238.5 2.4 fusion.21
  (73 shorter events, 67.2 us)
Async XLA Ops:
  6.5 73.2 %copy-start.2 = (s32[2,1024]{1,0:T(2,128)S(1)}, s32[2,1024]{1,0:T(2,128)}, u32[]{:S(2)}) copy-start(s32[2,1024]{1,0:T(2,128)} %param.10) | copy-start | bytes 24580
  6.5 231.8 %all-gather.2.cloned.1.call-start = ((), (), s32[]{:S(2)}) async-start(), calls=%async_computation | async-start | bytes 1081344 | tf_op jit(solution)/shard_map/all_gather | solution.py:45
  7.9 16.9 %collective-permute-start = (f32[2,64]{1,0:T(2,128)S(1)}, f32[2,64]{1,0:T(2,128)S(1)}, u32[]{:S(2)}, u32[]{:S(2)}) collective-permute-start(f32[2,64]{1,0:T(2,128)S(1)} %pad_maximum_fusion.1), channel_id=1, source_target_pairs={{0,1},{1,0},{2,3},{3,2},{4,5},{5,4},{6,7},{7,6},{8,9},{9,8},{10,11... | collective-permute-start | bytes 1544 | tf_op jit(solution)/shard_map/ppermute | solution.py:26
  25.6 4.3 %collective-permute-start.1 = (f32[2,128]{1,0:T(2,128)S(1)}, f32[2,128]{1,0:T(2,128)S(1)}, u32[]{:S(2)}, u32[]{:S(2)}) collective-permute-start(f32[2,128]{1,0:T(2,128)S(1)} %maximum_select_fusion.14), channel_id=1, source_target_pairs={{0,2},{1,3},{2,0},{3,1},{4,6},{5,7},{6,4},{7,5},{8,10},{9,11},{10,... | collective-permute-start | bytes 3080 | tf_op jit(solution)/shard_map/ppermute | solution.py:26
  29.9 5.2 %collective-permute-start.2 = (f32[2,256]{1,0:T(2,128)S(1)}, f32[2,256]{1,0:T(2,128)S(1)}, u32[]{:S(2)}, u32[]{:S(2)}) collective-permute-start(f32[2,256]{1,0:T(2,128)S(1)} %maximum_select_fusion.13), channel_id=1, source_target_pairs={{0,4},{1,5},{2,6},{3,7},{4,0},{5,1},{6,2},{7,3},{8,12},{9,13},{10,... | collective-permute-start | bytes 6152 | tf_op jit(solution)/shard_map/ppermute | solution.py:26
  35.1 8.2 %collective-permute-start.3 = (f32[2,512]{1,0:T(2,128)S(1)}, f32[2,512]{1,0:T(2,128)S(1)}, u32[]{:S(2)}, u32[]{:S(2)}) collective-permute-start(f32[2,512]{1,0:T(2,128)S(1)} %maximum_select_fusion.12), channel_id=1, source_target_pairs={{0,8},{1,9},{2,10},{3,11},{4,12},{5,13},{6,14},{7,15},{8,0},{9,1},... | collective-permute-start | bytes 12296 | tf_op jit(solution)/shard_map/ppermute | solution.py:26
  43.3 8.3 %collective-permute-start.4 = (f32[2,1024]{1,0:T(2,128)S(1)}, f32[2,1024]{1,0:T(2,128)S(1)}, u32[]{:S(2)}, u32[]{:S(2)}) collective-permute-start(f32[2,1024]{1,0:T(2,128)S(1)} %maximum_select_fusion.11), channel_id=1, source_target_pairs={{0,16},{1,17},{2,18},{3,19},{4,20},{5,21},{6,22},{7,23},{8,24},{9,... | collective-permute-start | bytes 24584 | tf_op jit(solution)/shard_map/ppermute | solution.py:26
  51.6 4.5 %collective-permute-start.5 = (f32[2,2048]{1,0:T(2,128)S(1)}, f32[2,2048]{1,0:T(2,128)S(1)}, u32[]{:S(2)}, u32[]{:S(2)}) collective-permute-start(f32[2,2048]{1,0:T(2,128)S(1)} %maximum_select_fusion.9), channel_id=1, source_target_pairs={{0,32},{32,0},{64,96},{96,64},{128,160},{160,128},{192,224},{224,1... | collective-permute-start | bytes 49160 | tf_op jit(solution)/shard_map/ppermute | solution.py:26
  56.2 5.7 %collective-permute-start.6 = (f32[2,4096]{1,0:T(2,128)S(1)}, f32[2,4096]{1,0:T(2,128)S(1)}, u32[]{:S(2)}, u32[]{:S(2)}) collective-permute-start(f32[2,4096]{1,0:T(2,128)S(1)} %maximum_select_fusion.7), channel_id=1, source_target_pairs={{0,64},{32,96},{64,0},{96,32},{128,192},{160,224},{192,128},{224,1... | collective-permute-start | bytes 98312 | tf_op jit(solution)/shard_map/ppermute | solution.py:26
  61.9 5.0 %collective-permute-start.7 = (f32[2,8192]{1,0:T(2,128)S(1)}, f32[2,8192]{1,0:T(2,128)S(1)}, u32[]{:S(2)}, u32[]{:S(2)}) collective-permute-start(f32[2,8192]{1,0:T(2,128)S(1)} %maximum_select_fusion.5), channel_id=1, source_target_pairs={{0,128},{32,160},{64,192},{96,224},{128,0},{160,32},{192,64},{224,... | collective-permute-start | bytes 196616 | tf_op jit(solution)/shard_map/ppermute | solution.py:26
  67.0 8.0 %collective-permute-start.8 = (f32[2,16384]{1,0:T(2,128)S(1)}, f32[2,16384]{1,0:T(2,128)S(1)}, u32[]{:S(2)}, u32[]{:S(2)}) collective-permute-start(f32[2,16384]{1,0:T(2,128)S(1)} %maximum_select_fusion.3), channel_id=1, source_target_pairs={{0,256},{32,288},{64,320},{96,352},{128,384},{160,416},{192,448},{... | collective-permute-start | bytes 393224 | tf_op jit(solution)/shard_map/ppermute | solution.py:26
  75.2 13.8 %collective-permute-start.9 = (f32[2,32768]{1,0:T(2,128)S(1)}, f32[2,32768]{1,0:T(2,128)S(1)}, u32[]{:S(2)}, u32[]{:S(2)}) collective-permute-start(f32[2,32768]{1,0:T(2,128)S(1)} %maximum_select_fusion.1), channel_id=1, source_target_pairs={{0,512},{32,544},{64,576},{96,608},{128,640},{160,672},{192,704},{... | collective-permute-start | bytes 786440 | tf_op jit(solution)/shard_map/ppermute | solution.py:26
  102.1 136.2 %copy-start = (f32[128]{0:T(128)S(1)}, f32[128]{0:T(128)}, u32[]{:S(2)}) copy-start(f32[128]{0:T(128)} %param.14) | copy-start | bytes 1540
  102.1 136.2 %copy-start.1 = (f32[128]{0:T(128)S(1)}, f32[128]{0:T(128)}, u32[]{:S(2)}) copy-start(f32[128]{0:T(128)} %param.15) | copy-start | bytes 1540
  102.2 17.5 %collective-permute-start.10 = (f32[2,1024]{1,0:T(2,128)S(1)}, f32[2,1024]{1,0:T(2,128)S(1)}, u32[]{:S(2)}, u32[]{:S(2)}) collective-permute-start(f32[2,1024]{1,0:T(2,128)S(1)} %pad_maximum_fusion), channel_id=1, source_target_pairs={{0,1},{1,0},{2,3},{3,2},{4,5},{5,4},{6,7},{7,6},{8,9},{9,8},{10,11... | collective-permute-start | bytes 24584 | tf_op jit(solution)/shard_map/ppermute | solution.py:26
  119.7 4.5 %collective-permute-start.11 = (f32[2,2048]{1,0:T(2,128)S(1)}, f32[2,2048]{1,0:T(2,128)S(1)}, u32[]{:S(2)}, u32[]{:S(2)}) collective-permute-start(f32[2,2048]{1,0:T(2,128)S(1)} %maximum_select_fusion.10), channel_id=1, source_target_pairs={{0,2},{1,3},{2,0},{3,1},{4,6},{5,7},{6,4},{7,5},{8,10},{9,11},{10,... | collective-permute-start | bytes 49160 | tf_op jit(solution)/shard_map/ppermute | solution.py:26
  124.2 5.6 %collective-permute-start.12 = (f32[2,4096]{1,0:T(2,128)S(1)}, f32[2,4096]{1,0:T(2,128)S(1)}, u32[]{:S(2)}, u32[]{:S(2)}) collective-permute-start(f32[2,4096]{1,0:T(2,128)S(1)} %maximum_select_fusion.8), channel_id=1, source_target_pairs={{0,4},{1,5},{2,6},{3,7},{4,0},{5,1},{6,2},{7,3},{8,12},{9,13},{10,... | collective-permute-start | bytes 98312 | tf_op jit(solution)/shard_map/ppermute | solution.py:26
  129.8 9.0 %collective-permute-start.13 = (f32[2,8192]{1,0:T(2,128)S(1)}, f32[2,8192]{1,0:T(2,128)S(1)}, u32[]{:S(2)}, u32[]{:S(2)}) collective-permute-start(f32[2,8192]{1,0:T(2,128)S(1)} %maximum_select_fusion.6), channel_id=1, source_target_pairs={{0,8},{1,9},{2,10},{3,11},{4,12},{5,13},{6,14},{7,15},{8,0},{9,1},... | collective-permute-start | bytes 196616 | tf_op jit(solution)/shard_map/ppermute | solution.py:26
  138.9 9.7 %collective-permute-start.14 = (f32[2,16384]{1,0:T(2,128)S(1)}, f32[2,16384]{1,0:T(2,128)S(1)}, u32[]{:S(2)}, u32[]{:S(2)}) collective-permute-start(f32[2,16384]{1,0:T(2,128)S(1)} %maximum_select_fusion.4), channel_id=1, source_target_pairs={{0,16},{1,17},{2,18},{3,19},{4,20},{5,21},{6,22},{7,23},{8,24},{9,... | collective-permute-start | bytes 393224 | tf_op jit(solution)/shard_map/ppermute | solution.py:26
Sparse Core Ops, SparseCore 0:
  145.8 92.5 all-gather.1

commit v4 on v3

--- a/solution.py
+++ b/solution.py
@@ -13,8 +13,8 @@
     return (upper, lower)
 
 
-def cauchy_tile(pole_at, live_at, value_row, scale_row):
-    return live_at[:, None] / (pole_at[:, None] - value_row[None, :]) * scale_row[None, :]
+def cauchy_tile_t(pole_row, live_row, value_at, scale_at):
+    return live_row[None, :] / (pole_row[None, :] - value_at[:, None]) * scale_at[:, None]
 
 
 def gather_by_pairs(block, axis):
@@ -34,6 +34,8 @@
     live_weight = weights * kept.astype(jnp.float32)
     pole_data = gather_by_pairs(jnp.stack([poles, live_weight]), "col")
     pole_data = gather_by_pairs(pole_data, "row")
+    columns_in = gather_by_pairs(basis, "col")
+    pole_data, columns_in = lax.optimization_barrier((pole_data, columns_in))
     row_total = lax.axis_size("row")
     child_id = lax.axis_index("row") // (row_total // 2)
     own_index = lax.dynamic_index_in_dim(position, child_id, 0, keepdims=False)
@@ -42,7 +44,6 @@
     rows_dev = basis.shape[0]
     cols_dev = eigenvalues.shape[0]
     zeros_init = jnp.zeros((rows_dev, cols_dev), jnp.float32)
-    columns_in = lax.all_gather(basis, "col", axis=1, tiled=True)
     span_cols = columns_in.shape[1]
     stride = math.gcd(span_cols, 4096)
 
@@ -50,9 +51,10 @@
         offset = block_id * stride
         cols_block = lax.dynamic_slice_in_dim(columns_in, offset, stride, 1)
         poles_block = lax.dynamic_slice_in_dim(child_poles, offset, stride, 1)
-        upper, lower = split_parts(cauchy_tile(poles_block[0], poles_block[1], eigenvalues, scales))
-        first_term = jnp.dot(cols_block, upper, preferred_element_type=jnp.float32)
-        second_term = jnp.dot(cols_block, lower, preferred_element_type=jnp.float32)
+        upper, lower = split_parts(cauchy_tile_t(poles_block[0], poles_block[1], eigenvalues, scales))
+        contract = (((1,), (1,)), ((), ()))
+        first_term = lax.dot_general(cols_block, upper, contract, preferred_element_type=jnp.float32)
+        second_term = lax.dot_general(cols_block, lower, contract, preferred_element_type=jnp.float32)
         return partial_sum + (first_term + second_term)
 
     summed = lax.fori_loop(0, span_cols // stride, add_block, zeros_init)

time: 293 us -> 183 us (0.62)
  the two profiles are of different devices: /device:TPU:1 before, /device:TPU:22 now
where the time goes in v4:
time: 183 us; the launch traced here: 182 us
  starting transfers between devices  97.7 us (53%)
  waiting for transfers between devices  52.5 us (29%)
  local copies, waits for them, and re-layouts  13.6 us (7%)
  other arithmetic  9.03 us (5%)
  matrix products  8.42 us (5%)
    ppermute x20, starting transfers between devices, gather_by_pairs(): other = lax.ppermute(held, axis, perm=[(i, i ^ step) for i in range(size)])  97.7 us
    ppermute x20, waiting for transfers between devices, gather_by_pairs(): other = lax.ppermute(held, axis, perm=[(i, i ^ step) for i in range(size)])  52.5 us
    gather x2, local copies, waits for them, and re-layouts, per_device(): own_poles = jnp.stack([pole_data[0][own_index], pole_data[1][own_index]])  12.3 us
    dot_general x8, matrix products, add_block(): lax.dot_general(cols_block, lower, contract, preferred_element_type=jnp.f...  5.42 us
  transfers between devices with their start and end apart: 20, of which 13 were waited for; matrix products, arithmetic and copies ran while one was open for 1% of the time, Pallas kernels for 0%

profile of v4, /device:TPU:22, one launch (start us, length us, event | category | flops | bytes accessed | tf_op | source)
XLA Modules:
  0.0 182.0 jit_solution(8295080842425557238)
XLA Ops:
  5.2 5.2 %collective-permute-start.1 = (f32[2,128]{1,0:T(2,128)S(1)}, f32[2,128]{1,0:T(2,128)S(1)}, u32[]{:S(2)}, u32[]{:S(2)}) collective-permute-start(f32[2,128]{1,0:T(2,128)S(1)} %maximum_select_fusion.19), channel_id=1, source_target_pairs={{0,2},{1,3},{2,0},{3,1},{4,6},{5,7},{6,4},{7,5},{8,10},{9,11},{10,... | collective-permute-start | bytes 3080 | tf_op jit(solution)/shard_map/ppermute | solution.py:26
  11.9 7.9 %collective-permute-start.2 = (f32[2,256]{1,0:T(2,128)S(1)}, f32[2,256]{1,0:T(2,128)S(1)}, u32[]{:S(2)}, u32[]{:S(2)}) collective-permute-start(f32[2,256]{1,0:T(2,128)S(1)} %maximum_select_fusion.18), channel_id=1, source_target_pairs={{0,4},{1,5},{2,6},{3,7},{4,0},{5,1},{6,2},{7,3},{8,12},{9,13},{10,... | collective-permute-start | bytes 6152 | tf_op jit(solution)/shard_map/ppermute | solution.py:26
  21.4 11.8 %collective-permute-start.3 = (f32[2,512]{1,0:T(2,128)S(1)}, f32[2,512]{1,0:T(2,128)S(1)}, u32[]{:S(2)}, u32[]{:S(2)}) collective-permute-start(f32[2,512]{1,0:T(2,128)S(1)} %maximum_select_fusion.17), channel_id=1, source_target_pairs={{0,8},{1,9},{2,10},{3,11},{4,12},{5,13},{6,14},{7,15},{8,0},{9,1},... | collective-permute-start | bytes 12296 | tf_op jit(solution)/shard_map/ppermute | solution.py:26
  35.2 7.3 %collective-permute-start.4 = (f32[2,1024]{1,0:T(2,128)S(1)}, f32[2,1024]{1,0:T(2,128)S(1)}, u32[]{:S(2)}, u32[]{:S(2)}) collective-permute-start(f32[2,1024]{1,0:T(2,128)S(1)} %maximum_select_fusion.16), channel_id=1, source_target_pairs={{0,16},{1,17},{2,18},{3,19},{4,20},{5,21},{6,22},{7,23},{8,24},{9,... | collective-permute-start | bytes 24584 | tf_op jit(solution)/shard_map/ppermute | solution.py:26
  44.8 2.5 %collective-permute-start.5 = (f32[2,2048]{1,0:T(2,128)S(1)}, f32[2,2048]{1,0:T(2,128)S(1)}, u32[]{:S(2)}, u32[]{:S(2)}) collective-permute-start(f32[2,2048]{1,0:T(2,128)S(1)} %maximum_select_fusion.14), channel_id=1, source_target_pairs={{0,32},{32,0},{64,96},{96,64},{128,160},{160,128},{192,224},{224,1... | collective-permute-start | bytes 49160 | tf_op jit(solution)/shard_map/ppermute | solution.py:26
  47.4 3.0 %collective-permute-done.5 = f32[2,2048]{1,0:T(2,128)S(1)} collective-permute-done((f32[2,2048]{1,0:T(2,128)S(1)}, f32[2,2048]{1,0:T(2,128)S(1)}, u32[]{:S(2)}, u32[]{:S(2)}) %collective-permute-start.5) | collective-permute-done | bytes 16416 | tf_op jit(solution)/shard_map/ppermute | solution.py:26
  50.4 4.6 %collective-permute-start.6 = (f32[2,4096]{1,0:T(2,128)S(1)}, f32[2,4096]{1,0:T(2,128)S(1)}, u32[]{:S(2)}, u32[]{:S(2)}) collective-permute-start(f32[2,4096]{1,0:T(2,128)S(1)} %maximum_select_fusion.12), channel_id=1, source_target_pairs={{0,64},{32,96},{64,0},{96,32},{128,192},{160,224},{192,128},{224,1... | collective-permute-start | bytes 98312 | tf_op jit(solution)/shard_map/ppermute | solution.py:26
  55.9 3.9 %collective-permute-start.11 = (bf16[16,2048]{1,0:T(8,128)(2,1)S(1)}, bf16[16,2048]{1,0:T(8,128)(2,1)S(1)}, u32[]{:S(2)}, u32[]{:S(2)}) collective-permute-start(bf16[16,2048]{1,0:T(8,128)(2,1)S(1)} %maximum_select_fusion.10), channel_id=1, source_target_pairs={{0,2},{1,3},{2,0},{3,1},{4,6},{5,7},{6,4},{7,5},{8,10},{9,11},{10,... | collective-permute-start | bytes 196616 | tf_op jit(solution)/shard_map/ppermute | solution.py:26
  59.9 2.4 %collective-permute-start.7 = (f32[2,8192]{1,0:T(2,128)S(1)}, f32[2,8192]{1,0:T(2,128)S(1)}, u32[]{:S(2)}, u32[]{:S(2)}) collective-permute-start(f32[2,8192]{1,0:T(2,128)S(1)} %maximum_select_fusion.9), channel_id=1, source_target_pairs={{0,128},{32,160},{64,192},{96,224},{128,0},{160,32},{192,64},{224,... | collective-permute-start | bytes 196616 | tf_op jit(solution)/shard_map/ppermute | solution.py:26
  62.4 4.8 %collective-permute-start.12 = (bf16[16,4096]{1,0:T(8,128)(2,1)S(1)}, bf16[16,4096]{1,0:T(8,128)(2,1)S(1)}, u32[]{:S(2)}, u32[]{:S(2)}) collective-permute-start(bf16[16,4096]{1,0:T(8,128)(2,1)S(1)} %maximum_select_fusion.7), channel_id=1, source_target_pairs={{0,4},{1,5},{2,6},{3,7},{4,0},{5,1},{6,2},{7,3},{8,12},{9,13},{10,... | collective-permute-start | bytes 393224 | tf_op jit(solution)/shard_map/ppermute | solution.py:26
  67.3 2.4 %collective-permute-start.8 = (f32[2,16384]{1,0:T(2,128)S(1)}, f32[2,16384]{1,0:T(2,128)S(1)}, u32[]{:S(2)}, u32[]{:S(2)}) collective-permute-start(f32[2,16384]{1,0:T(2,128)S(1)} %maximum_select_fusion.6), channel_id=1, source_target_pairs={{0,256},{32,288},{64,320},{96,352},{128,384},{160,416},{192,448},{... | collective-permute-start | bytes 393224 | tf_op jit(solution)/shard_map/ppermute | solution.py:26
  71.7 6.4 %collective-permute-start.13 = (bf16[16,8192]{1,0:T(8,128)(2,1)S(1)}, bf16[16,8192]{1,0:T(8,128)(2,1)S(1)}, u32[]{:S(2)}, u32[]{:S(2)}) collective-permute-start(bf16[16,8192]{1,0:T(8,128)(2,1)S(1)} %maximum_select_fusion.4), channel_id=1, source_target_pairs={{0,8},{1,9},{2,10},{3,11},{4,12},{5,13},{6,14},{7,15},{8,0},{9,1},... | collective-permute-start | bytes 786440 | tf_op jit(solution)/shard_map/ppermute | solution.py:26
  78.3 6.6 %collective-permute-start.9 = (f32[2,32768]{1,0:T(2,128)S(1)}, f32[2,32768]{1,0:T(2,128)S(1)}, u32[]{:S(2)}, u32[]{:S(2)}) collective-permute-start(f32[2,32768]{1,0:T(2,128)S(1)} %maximum_select_fusion.3), channel_id=1, source_target_pairs={{0,512},{32,544},{64,576},{96,608},{128,640},{160,672},{192,704},{... | collective-permute-start | bytes 786440 | tf_op jit(solution)/shard_map/ppermute | solution.py:26
  84.9 3.5 %collective-permute-done.13 = bf16[16,8192]{1,0:T(8,128)(2,1)S(1)} collective-permute-done((bf16[16,8192]{1,0:T(8,128)(2,1)S(1)}, bf16[16,8192]{1,0:T(8,128)(2,1)S(1)}, u32[]{:S(2)}, u32[]{:S(2)}) %collective-permute-start.13) | collective-permute-done | bytes 262176 | tf_op jit(solution)/shard_map/ppermute | solution.py:26
  88.5 5.4 %collective-permute-start.14 = (bf16[16,16384]{1,0:T(8,128)(2,1)S(1)}, bf16[16,16384]{1,0:T(8,128)(2,1)S(1)}, u32[]{:S(2)}, u32[]{:S(2)}) collective-permute-start(bf16[16,16384]{1,0:T(8,128)(2,1)S(1)} %maximum_select_fusion.2), channel_id=1, source_target_pairs={{0,16},{1,17},{2,18},{3,19},{4,20},{5,21},{6,22},{7,23},{8,24},{9,... | collective-permute-start | bytes 1572872 | tf_op jit(solution)/shard_map/ppermute | solution.py:26
  94.4 16.5 %collective-permute-done.14 = bf16[16,16384]{1,0:T(8,128)(2,1)S(1)} collective-permute-done((bf16[16,16384]{1,0:T(8,128)(2,1)S(1)}, bf16[16,16384]{1,0:T(8,128)(2,1)S(1)}, u32[]{:S(2)}, u32[]{:S(2)}) %collective-permute-start.14) | collective-permute-done | bytes 524320 | tf_op jit(solution)/shard_map/ppermute | solution.py:26
  111.6 6.2 %gather_fusion = f32[1024]{0:T(1024)S(1)} fusion(f32[65536]{0:T(1024)S(1)} %bitcast.20, s32[1024]{0:T(1024)S(1)} %broadcast_clamp_fusion), kind=kCustom, calls=%fused_computation | custom fusion | bytes 12288 | tf_op jit(solution)/shard_map/gather | solution.py:42
  117.8 6.2 %gather_fusion.1 = f32[1024]{0:T(1024)S(1)} fusion(f32[65536]{0:T(1024)S(1)} %bitcast.19, s32[1024]{0:T(1024)S(1)} %broadcast_clamp_fusion), kind=kCustom, calls=%fused_computation.1 | custom fusion | bytes 12288 | tf_op jit(solution)/shard_map/gather | solution.py:42
  129.0 3.7 %collective-permute-done.16 = f32[2,2048]{1,0:T(2,128)S(1)} collective-permute-done((f32[2,2048]{1,0:T(2,128)S(1)}, f32[2,2048]{1,0:T(2,128)S(1)}, u32[]{:S(2)}, u32[]{:S(2)}) %collective-permute-start.16) | collective-permute-done | bytes 16416 | tf_op jit(solution)/shard_map/ppermute | solution.py:26
  132.7 10.9 %collective-permute-start.17 = (f32[2,4096]{1,0:T(2,128)S(1)}, f32[2,4096]{1,0:T(2,128)S(1)}, u32[]{:S(2)}, u32[]{:S(2)}) collective-permute-start(f32[2,4096]{1,0:T(2,128)S(1)} %maximum_select_fusion.13), channel_id=1, source_target_pairs={{0,4},{1,5},{2,6},{3,7},{4,0},{5,1},{6,2},{7,3},{8,12},{9,13},{10,... | collective-permute-start | bytes 98312 | tf_op jit(solution)/shard_map/ppermute | solution.py:26
  147.4 8.9 %collective-permute-done.18 = f32[2,8192]{1,0:T(2,128)S(1)} collective-permute-done((f32[2,8192]{1,0:T(2,128)S(1)}, f32[2,8192]{1,0:T(2,128)S(1)}, u32[]{:S(2)}, u32[]{:S(2)}) %collective-permute-start.18) | collective-permute-done | bytes 65568 | tf_op jit(solution)/shard_map/ppermute | solution.py:26
  156.4 5.8 %collective-permute-start.19 = (f32[2,16384]{1,0:T(2,128)S(1)}, f32[2,16384]{1,0:T(2,128)S(1)}, u32[]{:S(2)}, u32[]{:S(2)}) collective-permute-start(f32[2,16384]{1,0:T(2,128)S(1)} %maximum_select_fusion.8), channel_id=1, source_target_pairs={{0,16},{1,17},{2,18},{3,19},{4,20},{5,21},{6,22},{7,23},{8,24},{9,... | collective-permute-start | bytes 393224 | tf_op jit(solution)/shard_map/ppermute | solution.py:26
  162.2 6.4 %collective-permute-done.19 = f32[2,16384]{1,0:T(2,128)S(1)} collective-permute-done((f32[2,16384]{1,0:T(2,128)S(1)}, f32[2,16384]{1,0:T(2,128)S(1)}, u32[]{:S(2)}, u32[]{:S(2)}) %collective-permute-start.19) | collective-permute-done | bytes 131104 | tf_op jit(solution)/shard_map/ppermute | solution.py:26
  168.8 12.5 %while.14 = (s32[]{:T(128)}, f32[16,128]{1,0:T(8,128)S(1)}, bf16[16,32768]{1,0:T(8,128)(2,1)S(1)}, f32[2,32768]{1,0:T(2,128)S(1)}, f32[128]{0:T(128)S(1)}, /*ind...) while((s32[]{:T(128)}, f32[16,128]{1,0:T(8,128)S(1)}, ...), condition=%wide.region_1.2_spmd.clone, body=%wide.region_0.1_spmd.clone.sunk | while | flops 38803464 | bytes 3573953 | solution.py:60
  (83 shorter events, 38.8 us)
Async XLA Ops:
  1.3 3.0 %collective-permute-start = (f32[2,64]{1,0:T(2,128)S(1)}, f32[2,64]{1,0:T(2,128)S(1)}, u32[]{:S(2)}, u32[]{:S(2)}) collective-permute-start(f32[2,64]{1,0:T(2,128)S(1)} %pad_maximum_fusion.1), channel_id=1, source_target_pairs={{0,1},{1,0},{2,3},{3,2},{4,5},{5,4},{6,7},{7,6},{8,9},{9,8},{10,11... | collective-permute-start | bytes 1544 | tf_op jit(solution)/shard_map/ppermute | solution.py:26
  5.2 6.7 %collective-permute-start.1 = (f32[2,128]{1,0:T(2,128)S(1)}, f32[2,128]{1,0:T(2,128)S(1)}, u32[]{:S(2)}, u32[]{:S(2)}) collective-permute-start(f32[2,128]{1,0:T(2,128)S(1)} %maximum_select_fusion.19), channel_id=1, source_target_pairs={{0,2},{1,3},{2,0},{3,1},{4,6},{5,7},{6,4},{7,5},{8,10},{9,11},{10,... | collective-permute-start | bytes 3080 | tf_op jit(solution)/shard_map/ppermute | solution.py:26
  11.9 9.5 %collective-permute-start.2 = (f32[2,256]{1,0:T(2,128)S(1)}, f32[2,256]{1,0:T(2,128)S(1)}, u32[]{:S(2)}, u32[]{:S(2)}) collective-permute-start(f32[2,256]{1,0:T(2,128)S(1)} %maximum_select_fusion.18), channel_id=1, source_target_pairs={{0,4},{1,5},{2,6},{3,7},{4,0},{5,1},{6,2},{7,3},{8,12},{9,13},{10,... | collective-permute-start | bytes 6152 | tf_op jit(solution)/shard_map/ppermute | solution.py:26
  21.4 13.8 %collective-permute-start.3 = (f32[2,512]{1,0:T(2,128)S(1)}, f32[2,512]{1,0:T(2,128)S(1)}, u32[]{:S(2)}, u32[]{:S(2)}) collective-permute-start(f32[2,512]{1,0:T(2,128)S(1)} %maximum_select_fusion.17), channel_id=1, source_target_pairs={{0,8},{1,9},{2,10},{3,11},{4,12},{5,13},{6,14},{7,15},{8,0},{9,1},... | collective-permute-start | bytes 12296 | tf_op jit(solution)/shard_map/ppermute | solution.py:26
  33.2 21.9 %collective-permute-start.10 = (bf16[16,1024]{1,0:T(8,128)(2,1)}, bf16[16,1024]{1,0:T(8,128)(2,1)S(1)}, u32[]{:S(2)}, u32[]{:S(2)}) collective-permute-start(bf16[16,1024]{1,0:T(8,128)(2,1)} %param.9), channel_id=1, source_target_pairs={{0,1},{1,0},{2,3},{3,2},{4,5},{5,4},{6,7},{7,6},{8,9},{9,8},{10,11... | collective-permute-start | bytes 98312 | tf_op jit(solution)/shard_map/ppermute | solution.py:26
  35.2 9.5 %collective-permute-start.4 = (f32[2,1024]{1,0:T(2,128)S(1)}, f32[2,1024]{1,0:T(2,128)S(1)}, u32[]{:S(2)}, u32[]{:S(2)}) collective-permute-start(f32[2,1024]{1,0:T(2,128)S(1)} %maximum_select_fusion.16), channel_id=1, source_target_pairs={{0,16},{1,17},{2,18},{3,19},{4,20},{5,21},{6,22},{7,23},{8,24},{9,... | collective-permute-start | bytes 24584 | tf_op jit(solution)/shard_map/ppermute | solution.py:26
  44.8 5.6 %collective-permute-start.5 = (f32[2,2048]{1,0:T(2,128)S(1)}, f32[2,2048]{1,0:T(2,128)S(1)}, u32[]{:S(2)}, u32[]{:S(2)}) collective-permute-start(f32[2,2048]{1,0:T(2,128)S(1)} %maximum_select_fusion.14), channel_id=1, source_target_pairs={{0,32},{32,0},{64,96},{96,64},{128,160},{160,128},{192,224},{224,1... | collective-permute-start | bytes 49160 | tf_op jit(solution)/shard_map/ppermute | solution.py:26
  50.4 9.5 %collective-permute-start.6 = (f32[2,4096]{1,0:T(2,128)S(1)}, f32[2,4096]{1,0:T(2,128)S(1)}, u32[]{:S(2)}, u32[]{:S(2)}) collective-permute-start(f32[2,4096]{1,0:T(2,128)S(1)} %maximum_select_fusion.12), channel_id=1, source_target_pairs={{0,64},{32,96},{64,0},{96,32},{128,192},{160,224},{192,128},{224,1... | collective-permute-start | bytes 98312 | tf_op jit(solution)/shard_map/ppermute | solution.py:26
  55.9 6.4 %collective-permute-start.11 = (bf16[16,2048]{1,0:T(8,128)(2,1)S(1)}, bf16[16,2048]{1,0:T(8,128)(2,1)S(1)}, u32[]{:S(2)}, u32[]{:S(2)}) collective-permute-start(bf16[16,2048]{1,0:T(8,128)(2,1)S(1)} %maximum_select_fusion.10), channel_id=1, source_target_pairs={{0,2},{1,3},{2,0},{3,1},{4,6},{5,7},{6,4},{7,5},{8,10},{9,11},{10,... | collective-permute-start | bytes 196616 | tf_op jit(solution)/shard_map/ppermute | solution.py:26
  59.9 7.3 %collective-permute-start.7 = (f32[2,8192]{1,0:T(2,128)S(1)}, f32[2,8192]{1,0:T(2,128)S(1)}, u32[]{:S(2)}, u32[]{:S(2)}) collective-permute-start(f32[2,8192]{1,0:T(2,128)S(1)} %maximum_select_fusion.9), channel_id=1, source_target_pairs={{0,128},{32,160},{64,192},{96,224},{128,0},{160,32},{192,64},{224,... | collective-permute-start | bytes 196616 | tf_op jit(solution)/shard_map/ppermute | solution.py:26
  62.4 9.2 %collective-permute-start.12 = (bf16[16,4096]{1,0:T(8,128)(2,1)S(1)}, bf16[16,4096]{1,0:T(8,128)(2,1)S(1)}, u32[]{:S(2)}, u32[]{:S(2)}) collective-permute-start(bf16[16,4096]{1,0:T(8,128)(2,1)S(1)} %maximum_select_fusion.7), channel_id=1, source_target_pairs={{0,4},{1,5},{2,6},{3,7},{4,0},{5,1},{6,2},{7,3},{8,12},{9,13},{10,... | collective-permute-start | bytes 393224 | tf_op jit(solution)/shard_map/ppermute | solution.py:26
  67.3 10.7 %collective-permute-start.8 = (f32[2,16384]{1,0:T(2,128)S(1)}, f32[2,16384]{1,0:T(2,128)S(1)}, u32[]{:S(2)}, u32[]{:S(2)}) collective-permute-start(f32[2,16384]{1,0:T(2,128)S(1)} %maximum_select_fusion.6), channel_id=1, source_target_pairs={{0,256},{32,288},{64,320},{96,352},{128,384},{160,416},{192,448},{... | collective-permute-start | bytes 393224 | tf_op jit(solution)/shard_map/ppermute | solution.py:26
  71.7 16.7 %collective-permute-start.13 = (bf16[16,8192]{1,0:T(8,128)(2,1)S(1)}, bf16[16,8192]{1,0:T(8,128)(2,1)S(1)}, u32[]{:S(2)}, u32[]{:S(2)}) collective-permute-start(bf16[16,8192]{1,0:T(8,128)(2,1)S(1)} %maximum_select_fusion.4), channel_id=1, source_target_pairs={{0,8},{1,9},{2,10},{3,11},{4,12},{5,13},{6,14},{7,15},{8,0},{9,1},... | collective-permute-start | bytes 786440 | tf_op jit(solution)/shard_map/ppermute | solution.py:26
  78.3 15.6 %collective-permute-start.9 = (f32[2,32768]{1,0:T(2,128)S(1)}, f32[2,32768]{1,0:T(2,128)S(1)}, u32[]{:S(2)}, u32[]{:S(2)}) collective-permute-start(f32[2,32768]{1,0:T(2,128)S(1)} %maximum_select_fusion.3), channel_id=1, source_target_pairs={{0,512},{32,544},{64,576},{96,608},{128,640},{160,672},{192,704},{... | collective-permute-start | bytes 786440 | tf_op jit(solution)/shard_map/ppermute | solution.py:26
  88.5 22.4 %collective-permute-start.14 = (bf16[16,16384]{1,0:T(8,128)(2,1)S(1)}, bf16[16,16384]{1,0:T(8,128)(2,1)S(1)}, u32[]{:S(2)}, u32[]{:S(2)}) collective-permute-start(bf16[16,16384]{1,0:T(8,128)(2,1)S(1)} %maximum_select_fusion.2), channel_id=1, source_target_pairs={{0,16},{1,17},{2,18},{3,19},{4,20},{5,21},{6,22},{7,23},{8,24},{9,... | collective-permute-start | bytes 1572872 | tf_op jit(solution)/shard_map/ppermute | solution.py:26
  117.7 51.1 %copy-start = (f32[128]{0:T(128)S(1)}, f32[128]{0:T(128)}, u32[]{:S(2)}) copy-start(f32[128]{0:T(128)} %param.14) | copy-start | bytes 1540
  117.7 51.1 %copy-start.1 = (f32[128]{0:T(128)S(1)}, f32[128]{0:T(128)}, u32[]{:S(2)}) copy-start(f32[128]{0:T(128)} %param.15) | copy-start | bytes 1540
  123.9 3.1 %collective-permute-start.15 = (f32[2,1024]{1,0:T(2,128)S(1)}, f32[2,1024]{1,0:T(2,128)S(1)}, u32[]{:S(2)}, u32[]{:S(2)}) collective-permute-start(f32[2,1024]{1,0:T(2,128)S(1)} %pad_maximum_fusion), channel_id=1, source_target_pairs={{0,1},{1,0},{2,3},{3,2},{4,5},{5,4},{6,7},{7,6},{8,9},{9,8},{10,11... | collective-permute-start | bytes 24584 | tf_op jit(solution)/shard_map/ppermute | solution.py:26
  127.0 5.6 %collective-permute-start.16 = (f32[2,2048]{1,0:T(2,128)S(1)}, f32[2,2048]{1,0:T(2,128)S(1)}, u32[]{:S(2)}, u32[]{:S(2)}) collective-permute-start(f32[2,2048]{1,0:T(2,128)S(1)} %maximum_select_fusion.15), channel_id=1, source_target_pairs={{0,2},{1,3},{2,0},{3,1},{4,6},{5,7},{6,4},{7,5},{8,10},{9,11},{10,... | collective-permute-start | bytes 49160 | tf_op jit(solution)/shard_map/ppermute | solution.py:26
  132.7 12.7 %collective-permute-start.17 = (f32[2,4096]{1,0:T(2,128)S(1)}, f32[2,4096]{1,0:T(2,128)S(1)}, u32[]{:S(2)}, u32[]{:S(2)}) collective-permute-start(f32[2,4096]{1,0:T(2,128)S(1)} %maximum_select_fusion.13), channel_id=1, source_target_pairs={{0,4},{1,5},{2,6},{3,7},{4,0},{5,1},{6,2},{7,3},{8,12},{9,13},{10,... | collective-permute-start | bytes 98312 | tf_op jit(solution)/shard_map/ppermute | solution.py:26
  145.5 10.9 %collective-permute-start.18 = (f32[2,8192]{1,0:T(2,128)S(1)}, f32[2,8192]{1,0:T(2,128)S(1)}, u32[]{:S(2)}, u32[]{:S(2)}) collective-permute-start(f32[2,8192]{1,0:T(2,128)S(1)} %maximum_select_fusion.11), channel_id=1, source_target_pairs={{0,8},{1,9},{2,10},{3,11},{4,12},{5,13},{6,14},{7,15},{8,0},{9,1},... | collective-permute-start | bytes 196616 | tf_op jit(solution)/shard_map/ppermute | solution.py:26
  156.4 12.2 %collective-permute-start.19 = (f32[2,16384]{1,0:T(2,128)S(1)}, f32[2,16384]{1,0:T(2,128)S(1)}, u32[]{:S(2)}, u32[]{:S(2)}) collective-permute-start(f32[2,16384]{1,0:T(2,128)S(1)} %maximum_select_fusion.8), channel_id=1, source_target_pairs={{0,16},{1,17},{2,18},{3,19},{4,20},{5,21},{6,22},{7,23},{8,24},{9,... | collective-permute-start | bytes 393224 | tf_op jit(solution)/shard_map/ppermute | solution.py:26

commit v5 on v4

--- a/solution.py
+++ b/solution.py
@@ -39,25 +39,45 @@
     row_total = lax.axis_size("row")
     child_id = lax.axis_index("row") // (row_total // 2)
     own_index = lax.dynamic_index_in_dim(position, child_id, 0, keepdims=False)
-    own_poles = jnp.stack([pole_data[0][own_index], pole_data[1][own_index]])
-    child_poles = gather_by_pairs(own_poles, "col")
+    held = jnp.stack([pole_data[0][own_index], pole_data[1][own_index]])
     rows_dev = basis.shape[0]
     cols_dev = eigenvalues.shape[0]
-    zeros_init = jnp.zeros((rows_dev, cols_dev), jnp.float32)
-    span_cols = columns_in.shape[1]
-    stride = math.gcd(span_cols, 4096)
+    own_cols = held.shape[1]
+    col_total = lax.axis_size("col")
+    col_index = lax.axis_index("col")
+    tile = 4096
+    contract = (((1,), (1,)), ((), ()))
 
-    def add_block(block_id, partial_sum):
-        offset = block_id * stride
-        cols_block = lax.dynamic_slice_in_dim(columns_in, offset, stride, 1)
-        poles_block = lax.dynamic_slice_in_dim(child_poles, offset, stride, 1)
+    def add_tile(partial_sum, cols_block, poles_block):
         upper, lower = split_parts(cauchy_tile_t(poles_block[0], poles_block[1], eigenvalues, scales))
-        contract = (((1,), (1,)), ((), ()))
         first_term = lax.dot_general(cols_block, upper, contract, preferred_element_type=jnp.float32)
         second_term = lax.dot_general(cols_block, lower, contract, preferred_element_type=jnp.float32)
         return partial_sum + (first_term + second_term)
 
-    summed = lax.fori_loop(0, span_cols // stride, add_block, zeros_init)
+    def add_range(partial_sum, values, offset):
+        length = values.shape[1]
+        if length <= tile:
+            cols_block = lax.dynamic_slice_in_dim(columns_in, offset, length, 1)
+            return add_tile(partial_sum, cols_block, values)
+
+        def add_block(block_id, acc):
+            start = block_id * tile
+            cols_block = lax.dynamic_slice_in_dim(columns_in, offset + start, tile, 1)
+            poles_block = lax.dynamic_slice_in_dim(values, start, tile, 1)
+            return add_tile(acc, cols_block, poles_block)
+
+        return lax.fori_loop(0, length // tile, add_block, partial_sum)
+
+    summed = add_range(jnp.zeros((rows_dev, cols_dev), jnp.float32), held, col_index * own_cols)
+    step = 1
+    while step < col_total:
+        other = lax.ppermute(held, "col", perm=[(i, i ^ step) for i in range(col_total)])
+        other_at = ((col_index // step) ^ 1) * step * own_cols
+        summed = add_range(summed, other, other_at)
+        if step * 2 < col_total:
+            low_half = (col_index // step) % 2 == 0
+            held = jnp.where(low_half, jnp.concatenate([held, other], -1), jnp.concatenate([other, held], -1))
+        step *= 2
     return summed.astype(jnp.bfloat16)
 
 

time: 183 us -> 178 us (0.973)
  waiting for transfers between devices: 52.5 us -> 46.9 us
    ppermute x0 -> x5, starting transfers between devices: none -> 22.4 us  [per_device(): lax.ppermute(held, 'col', perm=[(i, i ^ step) for i in range(col_total)])]
    ppermute x20 -> x15, starting transfers between devices: 97.7 us -> 75.2 us  [gather_by_pairs(): other = lax.ppermute(held, axis, perm=[(i, i ^ step) for i in range(size)])]
    ppermute x20 -> x15, waiting for transfers between devices: 52.5 us -> 30.4 us  [gather_by_pairs(): other = lax.ppermute(held, axis, perm=[(i, i ^ step) for i in range(size)])]
    ppermute x0 -> x5, waiting for transfers between devices: none -> 16.4 us  [per_device(): lax.ppermute(held, 'col', perm=[(i, i ^ step) for i in range(col_total)])]
    dot_general x16 -> x20, matrix products: 8.42 us -> 9.01 us  [the longest x10 5.81 us: add_tile(): lax.dot_general(cols_block, lower, contract, preferred_element_type=jnp.f...]
  transfers between devices with their start and end apart: 20 -> 20, of which waited for: 13 -> 13; matrix products, arithmetic and copies ran while one was open for 1% -> 5% of each run, Pallas kernels for 0% -> 0%
where the time goes in v5:
time: 178 us; the launch traced here: 177 us
  starting transfers between devices  97.7 us (55%)
  waiting for transfers between devices  46.9 us (26%)
  local copies, waits for them, and re-layouts  13.4 us (8%)
  other arithmetic  9.08 us (5%)
  matrix products  9.01 us (5%)
    ppermute x15, starting transfers between devices, gather_by_pairs(): other = lax.ppermute(held, axis, perm=[(i, i ^ step) for i in range(size)])  75.2 us
    ppermute x15, waiting for transfers between devices, gather_by_pairs(): other = lax.ppermute(held, axis, perm=[(i, i ^ step) for i in range(size)])  30.4 us
    ppermute x5, starting transfers between devices, per_device(): lax.ppermute(held, 'col', perm=[(i, i ^ step) for i in range(col_total)])  22.4 us
    ppermute x5, waiting for transfers between devices, per_device(): lax.ppermute(held, 'col', perm=[(i, i ^ step) for i in range(col_total)])  16.4 us
    gather x2, local copies, waits for them, and re-layouts, per_device(): held = jnp.stack([pole_data[0][own_index], pole_data[1][own_index]])  12.3 us
    dot_general x10, matrix products, add_tile(): lax.dot_general(cols_block, lower, contract, preferred_element_type=jnp.f...  5.81 us
  transfers between devices with their start and end apart: 20, of which 13 were waited for; matrix products, arithmetic and copies ran while one was open for 5% of the time, Pallas kernels for 0%

profile of v5, /device:TPU:22, one launch (start us, length us, event | category | flops | bytes accessed | tf_op | source)
XLA Modules:
  0.0 176.9 jit_solution(14672839785131267327)
XLA Ops:
  5.2 5.2 %collective-permute-start.1 = (f32[2,128]{1,0:T(2,128)S(1)}, f32[2,128]{1,0:T(2,128)S(1)}, u32[]{:S(2)}, u32[]{:S(2)}) collective-permute-start(f32[2,128]{1,0:T(2,128)S(1)} %maximum_select_fusion.18), channel_id=1, source_target_pairs={{0,2},{1,3},{2,0},{3,1},{4,6},{5,7},{6,4},{7,5},{8,10},{9,11},{10,... | collective-permute-start | bytes 3080 | tf_op jit(solution)/shard_map/ppermute | solution.py:26
  11.9 7.9 %collective-permute-start.2 = (f32[2,256]{1,0:T(2,128)S(1)}, f32[2,256]{1,0:T(2,128)S(1)}, u32[]{:S(2)}, u32[]{:S(2)}) collective-permute-start(f32[2,256]{1,0:T(2,128)S(1)} %maximum_select_fusion.17), channel_id=1, source_target_pairs={{0,4},{1,5},{2,6},{3,7},{4,0},{5,1},{6,2},{7,3},{8,12},{9,13},{10,... | collective-permute-start | bytes 6152 | tf_op jit(solution)/shard_map/ppermute | solution.py:26
  21.4 11.8 %collective-permute-start.3 = (f32[2,512]{1,0:T(2,128)S(1)}, f32[2,512]{1,0:T(2,128)S(1)}, u32[]{:S(2)}, u32[]{:S(2)}) collective-permute-start(f32[2,512]{1,0:T(2,128)S(1)} %maximum_select_fusion.16), channel_id=1, source_target_pairs={{0,8},{1,9},{2,10},{3,11},{4,12},{5,13},{6,14},{7,15},{8,0},{9,1},... | collective-permute-start | bytes 12296 | tf_op jit(solution)/shard_map/ppermute | solution.py:26
  35.2 7.3 %collective-permute-start.4 = (f32[2,1024]{1,0:T(2,128)S(1)}, f32[2,1024]{1,0:T(2,128)S(1)}, u32[]{:S(2)}, u32[]{:S(2)}) collective-permute-start(f32[2,1024]{1,0:T(2,128)S(1)} %maximum_select_fusion.15), channel_id=1, source_target_pairs={{0,16},{1,17},{2,18},{3,19},{4,20},{5,21},{6,22},{7,23},{8,24},{9,... | collective-permute-start | bytes 24584 | tf_op jit(solution)/shard_map/ppermute | solution.py:26
  44.8 2.5 %collective-permute-start.5 = (f32[2,2048]{1,0:T(2,128)S(1)}, f32[2,2048]{1,0:T(2,128)S(1)}, u32[]{:S(2)}, u32[]{:S(2)}) collective-permute-start(f32[2,2048]{1,0:T(2,128)S(1)} %maximum_select_fusion.13), channel_id=1, source_target_pairs={{0,32},{32,0},{64,96},{96,64},{128,160},{160,128},{192,224},{224,1... | collective-permute-start | bytes 49160 | tf_op jit(solution)/shard_map/ppermute | solution.py:26
  47.4 3.0 %collective-permute-done.5 = f32[2,2048]{1,0:T(2,128)S(1)} collective-permute-done((f32[2,2048]{1,0:T(2,128)S(1)}, f32[2,2048]{1,0:T(2,128)S(1)}, u32[]{:S(2)}, u32[]{:S(2)}) %collective-permute-start.5) | collective-permute-done | bytes 16416 | tf_op jit(solution)/shard_map/ppermute | solution.py:26
  50.4 4.6 %collective-permute-start.6 = (f32[2,4096]{1,0:T(2,128)S(1)}, f32[2,4096]{1,0:T(2,128)S(1)}, u32[]{:S(2)}, u32[]{:S(2)}) collective-permute-start(f32[2,4096]{1,0:T(2,128)S(1)} %maximum_select_fusion.11), channel_id=1, source_target_pairs={{0,64},{32,96},{64,0},{96,32},{128,192},{160,224},{192,128},{224,1... | collective-permute-start | bytes 98312 | tf_op jit(solution)/shard_map/ppermute | solution.py:26
  55.9 3.9 %collective-permute-start.11 = (bf16[16,2048]{1,0:T(8,128)(2,1)S(1)}, bf16[16,2048]{1,0:T(8,128)(2,1)S(1)}, u32[]{:S(2)}, u32[]{:S(2)}) collective-permute-start(bf16[16,2048]{1,0:T(8,128)(2,1)S(1)} %maximum_select_fusion.9), channel_id=1, source_target_pairs={{0,2},{1,3},{2,0},{3,1},{4,6},{5,7},{6,4},{7,5},{8,10},{9,11},{10,... | collective-permute-start | bytes 196616 | tf_op jit(solution)/shard_map/ppermute | solution.py:26
  59.9 2.4 %collective-permute-start.7 = (f32[2,8192]{1,0:T(2,128)S(1)}, f32[2,8192]{1,0:T(2,128)S(1)}, u32[]{:S(2)}, u32[]{:S(2)}) collective-permute-start(f32[2,8192]{1,0:T(2,128)S(1)} %maximum_select_fusion.8), channel_id=1, source_target_pairs={{0,128},{32,160},{64,192},{96,224},{128,0},{160,32},{192,64},{224,... | collective-permute-start | bytes 196616 | tf_op jit(solution)/shard_map/ppermute | solution.py:26
  62.4 4.8 %collective-permute-start.12 = (bf16[16,4096]{1,0:T(8,128)(2,1)S(1)}, bf16[16,4096]{1,0:T(8,128)(2,1)S(1)}, u32[]{:S(2)}, u32[]{:S(2)}) collective-permute-start(bf16[16,4096]{1,0:T(8,128)(2,1)S(1)} %maximum_select_fusion.6), channel_id=1, source_target_pairs={{0,4},{1,5},{2,6},{3,7},{4,0},{5,1},{6,2},{7,3},{8,12},{9,13},{10,... | collective-permute-start | bytes 393224 | tf_op jit(solution)/shard_map/ppermute | solution.py:26
  71.7 6.4 %collective-permute-start.13 = (bf16[16,8192]{1,0:T(8,128)(2,1)S(1)}, bf16[16,8192]{1,0:T(8,128)(2,1)S(1)}, u32[]{:S(2)}, u32[]{:S(2)}) collective-permute-start(bf16[16,8192]{1,0:T(8,128)(2,1)S(1)} %maximum_select_fusion.4), channel_id=1, source_target_pairs={{0,8},{1,9},{2,10},{3,11},{4,12},{5,13},{6,14},{7,15},{8,0},{9,1},... | collective-permute-start | bytes 786440 | tf_op jit(solution)/shard_map/ppermute | solution.py:26
  78.3 6.6 %collective-permute-start.9 = (f32[2,32768]{1,0:T(2,128)S(1)}, f32[2,32768]{1,0:T(2,128)S(1)}, u32[]{:S(2)}, u32[]{:S(2)}) collective-permute-start(f32[2,32768]{1,0:T(2,128)S(1)} %maximum_select_fusion.3), channel_id=1, source_target_pairs={{0,512},{32,544},{64,576},{96,608},{128,640},{160,672},{192,704},{... | collective-permute-start | bytes 786440 | tf_op jit(solution)/shard_map/ppermute | solution.py:26
  84.9 3.5 %collective-permute-done.13 = bf16[16,8192]{1,0:T(8,128)(2,1)S(1)} collective-permute-done((bf16[16,8192]{1,0:T(8,128)(2,1)S(1)}, bf16[16,8192]{1,0:T(8,128)(2,1)S(1)}, u32[]{:S(2)}, u32[]{:S(2)}) %collective-permute-start.13) | collective-permute-done | bytes 262176 | tf_op jit(solution)/shard_map/ppermute | solution.py:26
  88.5 5.5 %collective-permute-start.14 = (bf16[16,16384]{1,0:T(8,128)(2,1)S(1)}, bf16[16,16384]{1,0:T(8,128)(2,1)S(1)}, u32[]{:S(2)}, u32[]{:S(2)}) collective-permute-start(bf16[16,16384]{1,0:T(8,128)(2,1)S(1)} %maximum_select_fusion.2), channel_id=1, source_target_pairs={{0,16},{1,17},{2,18},{3,19},{4,20},{5,21},{6,22},{7,23},{8,24},{9,... | collective-permute-start | bytes 1572872 | tf_op jit(solution)/shard_map/ppermute | solution.py:26
  94.4 16.5 %collective-permute-done.14 = bf16[16,16384]{1,0:T(8,128)(2,1)S(1)} collective-permute-done((bf16[16,16384]{1,0:T(8,128)(2,1)S(1)}, bf16[16,16384]{1,0:T(8,128)(2,1)S(1)}, u32[]{:S(2)}, u32[]{:S(2)}) %collective-permute-start.14) | collective-permute-done | bytes 524320 | tf_op jit(solution)/shard_map/ppermute | solution.py:26
  111.6 6.2 %gather_fusion = f32[1024]{0:T(1024)S(1)} fusion(f32[65536]{0:T(1024)S(1)} %bitcast.39, s32[1024]{0:T(1024)S(1)} %broadcast_clamp_fusion), kind=kCustom, calls=%fused_computation | custom fusion | bytes 12288 | tf_op jit(solution)/shard_map/gather | solution.py:42
  117.8 6.2 %gather_fusion.1 = f32[1024]{0:T(1024)S(1)} fusion(f32[65536]{0:T(1024)S(1)} %bitcast.38, s32[1024]{0:T(1024)S(1)} %broadcast_clamp_fusion), kind=kCustom, calls=%fused_computation.1 | custom fusion | bytes 12288 | tf_op jit(solution)/shard_map/gather | solution.py:42
  130.0 2.7 %collective-permute-done.16 = f32[2,2048]{1,0:T(2,128)S(1)} collective-permute-done((f32[2,2048]{1,0:T(2,128)S(1)}, f32[2,2048]{1,0:T(2,128)S(1)}, u32[]{:S(2)}, u32[]{:S(2)}) %collective-permute-start.16) | collective-permute-done | bytes 16416 | tf_op jit(solution)/shard_map/ppermute | solution.py:74
  133.7 10.9 %collective-permute-start.17 = (f32[2,4096]{1,0:T(2,128)S(1)}, f32[2,4096]{1,0:T(2,128)S(1)}, u32[]{:S(2)}, u32[]{:S(2)}) collective-permute-start(f32[2,4096]{1,0:T(2,128)S(1)} %maximum_select_fusion.12), channel_id=1, source_target_pairs={{0,4},{1,5},{2,6},{3,7},{4,0},{5,1},{6,2},{7,3},{8,12},{9,13},{10,... | collective-permute-start | bytes 98312 | tf_op jit(solution)/shard_map/ppermute | solution.py:74
  149.9 7.9 %collective-permute-done.18 = f32[2,8192]{1,0:T(2,128)S(1)} collective-permute-done((f32[2,8192]{1,0:T(2,128)S(1)}, f32[2,8192]{1,0:T(2,128)S(1)}, u32[]{:S(2)}, u32[]{:S(2)}) %collective-permute-start.18) | collective-permute-done | bytes 65568 | tf_op jit(solution)/shard_map/ppermute | solution.py:74
  157.9 5.8 %collective-permute-start.19 = (f32[2,16384]{1,0:T(2,128)S(1)}, f32[2,16384]{1,0:T(2,128)S(1)}, u32[]{:S(2)}, u32[]{:S(2)}) collective-permute-start(f32[2,16384]{1,0:T(2,128)S(1)} %maximum_select_fusion.7), channel_id=1, source_target_pairs={{0,16},{1,17},{2,18},{3,19},{4,20},{5,21},{6,22},{7,23},{8,24},{9,... | collective-permute-start | bytes 393224 | tf_op jit(solution)/shard_map/ppermute | solution.py:74
  163.7 3.2 %while.26 = (s32[]{:T(128)}, f32[16,128]{1,0:T(8,128)S(1)}, s32[]{:T(128)}, bf16[16,32768]{1,0:T(8,128)(2,1)S(1)}, f32[2,8192]{1,0:T(2,128)S(1)}, /*index=5*/f32...) while((s32[]{:T(128)}, f32[16,128]{1,0:T(8,128)S(1)}, ...), condition=%wide.region_1.2_spmd, body=%wide.region_0.1_spmd.sunk | while | flops 38801416 | bytes 3574013 | solution.py:69
  166.9 3.2 %collective-permute-done.19 = f32[2,16384]{1,0:T(2,128)S(1)} collective-permute-done((f32[2,16384]{1,0:T(2,128)S(1)}, f32[2,16384]{1,0:T(2,128)S(1)}, u32[]{:S(2)}, u32[]{:S(2)}) %collective-permute-start.19) | collective-permute-done | bytes 131104 | tf_op jit(solution)/shard_map/ppermute | solution.py:74
  170.1 6.3 %while.27 = (s32[]{:T(128)}, f32[16,128]{1,0:T(8,128)S(1)}, s32[]{:T(128)}, bf16[16,32768]{1,0:T(8,128)(2,1)S(1)}, f32[2,16384]{1,0:T(2,128)S(1)}, /*index=5*/f3...) while((s32[]{:T(128)}, f32[16,128]{1,0:T(8,128)S(1)}, ...), condition=%wide.region_3.4_spmd, body=%wide.region_2.3_spmd.sunk | while | flops 38801416 | bytes 3574013 | solution.py:69
  (88 shorter events, 41.3 us)
Async XLA Ops:
  1.3 3.0 %collective-permute-start = (f32[2,64]{1,0:T(2,128)S(1)}, f32[2,64]{1,0:T(2,128)S(1)}, u32[]{:S(2)}, u32[]{:S(2)}) collective-permute-start(f32[2,64]{1,0:T(2,128)S(1)} %pad_maximum_fusion.1), channel_id=1, source_target_pairs={{0,1},{1,0},{2,3},{3,2},{4,5},{5,4},{6,7},{7,6},{8,9},{9,8},{10,11... | collective-permute-start | bytes 1544 | tf_op jit(solution)/shard_map/ppermute | solution.py:26
  5.2 6.7 %collective-permute-start.1 = (f32[2,128]{1,0:T(2,128)S(1)}, f32[2,128]{1,0:T(2,128)S(1)}, u32[]{:S(2)}, u32[]{:S(2)}) collective-permute-start(f32[2,128]{1,0:T(2,128)S(1)} %maximum_select_fusion.18), channel_id=1, source_target_pairs={{0,2},{1,3},{2,0},{3,1},{4,6},{5,7},{6,4},{7,5},{8,10},{9,11},{10,... | collective-permute-start | bytes 3080 | tf_op jit(solution)/shard_map/ppermute | solution.py:26
  11.9 9.5 %collective-permute-start.2 = (f32[2,256]{1,0:T(2,128)S(1)}, f32[2,256]{1,0:T(2,128)S(1)}, u32[]{:S(2)}, u32[]{:S(2)}) collective-permute-start(f32[2,256]{1,0:T(2,128)S(1)} %maximum_select_fusion.17), channel_id=1, source_target_pairs={{0,4},{1,5},{2,6},{3,7},{4,0},{5,1},{6,2},{7,3},{8,12},{9,13},{10,... | collective-permute-start | bytes 6152 | tf_op jit(solution)/shard_map/ppermute | solution.py:26
  21.4 13.8 %collective-permute-start.3 = (f32[2,512]{1,0:T(2,128)S(1)}, f32[2,512]{1,0:T(2,128)S(1)}, u32[]{:S(2)}, u32[]{:S(2)}) collective-permute-start(f32[2,512]{1,0:T(2,128)S(1)} %maximum_select_fusion.16), channel_id=1, source_target_pairs={{0,8},{1,9},{2,10},{3,11},{4,12},{5,13},{6,14},{7,15},{8,0},{9,1},... | collective-permute-start | bytes 12296 | tf_op jit(solution)/shard_map/ppermute | solution.py:26
  33.2 21.9 %collective-permute-start.10 = (bf16[16,1024]{1,0:T(8,128)(2,1)}, bf16[16,1024]{1,0:T(8,128)(2,1)S(1)}, u32[]{:S(2)}, u32[]{:S(2)}) collective-permute-start(bf16[16,1024]{1,0:T(8,128)(2,1)} %param.11), channel_id=1, source_target_pairs={{0,1},{1,0},{2,3},{3,2},{4,5},{5,4},{6,7},{7,6},{8,9},{9,8},{10,11... | collective-permute-start | bytes 98312 | tf_op jit(solution)/shard_map/ppermute | solution.py:26
  35.2 9.5 %collective-permute-start.4 = (f32[2,1024]{1,0:T(2,128)S(1)}, f32[2,1024]{1,0:T(2,128)S(1)}, u32[]{:S(2)}, u32[]{:S(2)}) collective-permute-start(f32[2,1024]{1,0:T(2,128)S(1)} %maximum_select_fusion.15), channel_id=1, source_target_pairs={{0,16},{1,17},{2,18},{3,19},{4,20},{5,21},{6,22},{7,23},{8,24},{9,... | collective-permute-start | bytes 24584 | tf_op jit(solution)/shard_map/ppermute | solution.py:26
  44.8 5.6 %collective-permute-start.5 = (f32[2,2048]{1,0:T(2,128)S(1)}, f32[2,2048]{1,0:T(2,128)S(1)}, u32[]{:S(2)}, u32[]{:S(2)}) collective-permute-start(f32[2,2048]{1,0:T(2,128)S(1)} %maximum_select_fusion.13), channel_id=1, source_target_pairs={{0,32},{32,0},{64,96},{96,64},{128,160},{160,128},{192,224},{224,1... | collective-permute-start | bytes 49160 | tf_op jit(solution)/shard_map/ppermute | solution.py:26
  50.4 9.5 %collective-permute-start.6 = (f32[2,4096]{1,0:T(2,128)S(1)}, f32[2,4096]{1,0:T(2,128)S(1)}, u32[]{:S(2)}, u32[]{:S(2)}) collective-permute-start(f32[2,4096]{1,0:T(2,128)S(1)} %maximum_select_fusion.11), channel_id=1, source_target_pairs={{0,64},{32,96},{64,0},{96,32},{128,192},{160,224},{192,128},{224,1... | collective-permute-start | bytes 98312 | tf_op jit(solution)/shard_map/ppermute | solution.py:26
  55.9 6.4 %collective-permute-start.11 = (bf16[16,2048]{1,0:T(8,128)(2,1)S(1)}, bf16[16,2048]{1,0:T(8,128)(2,1)S(1)}, u32[]{:S(2)}, u32[]{:S(2)}) collective-permute-start(bf16[16,2048]{1,0:T(8,128)(2,1)S(1)} %maximum_select_fusion.9), channel_id=1, source_target_pairs={{0,2},{1,3},{2,0},{3,1},{4,6},{5,7},{6,4},{7,5},{8,10},{9,11},{10,... | collective-permute-start | bytes 196616 | tf_op jit(solution)/shard_map/ppermute | solution.py:26
  59.9 7.3 %collective-permute-start.7 = (f32[2,8192]{1,0:T(2,128)S(1)}, f32[2,8192]{1,0:T(2,128)S(1)}, u32[]{:S(2)}, u32[]{:S(2)}) collective-permute-start(f32[2,8192]{1,0:T(2,128)S(1)} %maximum_select_fusion.8), channel_id=1, source_target_pairs={{0,128},{32,160},{64,192},{96,224},{128,0},{160,32},{192,64},{224,... | collective-permute-start | bytes 196616 | tf_op jit(solution)/shard_map/ppermute | solution.py:26
  62.4 9.2 %collective-permute-start.12 = (bf16[16,4096]{1,0:T(8,128)(2,1)S(1)}, bf16[16,4096]{1,0:T(8,128)(2,1)S(1)}, u32[]{:S(2)}, u32[]{:S(2)}) collective-permute-start(bf16[16,4096]{1,0:T(8,128)(2,1)S(1)} %maximum_select_fusion.6), channel_id=1, source_target_pairs={{0,4},{1,5},{2,6},{3,7},{4,0},{5,1},{6,2},{7,3},{8,12},{9,13},{10,... | collective-permute-start | bytes 393224 | tf_op jit(solution)/shard_map/ppermute | solution.py:26
  67.3 10.7 %collective-permute-start.8 = (f32[2,16384]{1,0:T(2,128)S(1)}, f32[2,16384]{1,0:T(2,128)S(1)}, u32[]{:S(2)}, u32[]{:S(2)}) collective-permute-start(f32[2,16384]{1,0:T(2,128)S(1)} %maximum_select_fusion.5), channel_id=1, source_target_pairs={{0,256},{32,288},{64,320},{96,352},{128,384},{160,416},{192,448},{... | collective-permute-start | bytes 393224 | tf_op jit(solution)/shard_map/ppermute | solution.py:26
  71.7 16.7 %collective-permute-start.13 = (bf16[16,8192]{1,0:T(8,128)(2,1)S(1)}, bf16[16,8192]{1,0:T(8,128)(2,1)S(1)}, u32[]{:S(2)}, u32[]{:S(2)}) collective-permute-start(bf16[16,8192]{1,0:T(8,128)(2,1)S(1)} %maximum_select_fusion.4), channel_id=1, source_target_pairs={{0,8},{1,9},{2,10},{3,11},{4,12},{5,13},{6,14},{7,15},{8,0},{9,1},... | collective-permute-start | bytes 786440 | tf_op jit(solution)/shard_map/ppermute | solution.py:26
  78.3 15.7 %collective-permute-start.9 = (f32[2,32768]{1,0:T(2,128)S(1)}, f32[2,32768]{1,0:T(2,128)S(1)}, u32[]{:S(2)}, u32[]{:S(2)}) collective-permute-start(f32[2,32768]{1,0:T(2,128)S(1)} %maximum_select_fusion.3), channel_id=1, source_target_pairs={{0,512},{32,544},{64,576},{96,608},{128,640},{160,672},{192,704},{... | collective-permute-start | bytes 786440 | tf_op jit(solution)/shard_map/ppermute | solution.py:26
  88.5 22.4 %collective-permute-start.14 = (bf16[16,16384]{1,0:T(8,128)(2,1)S(1)}, bf16[16,16384]{1,0:T(8,128)(2,1)S(1)}, u32[]{:S(2)}, u32[]{:S(2)}) collective-permute-start(bf16[16,16384]{1,0:T(8,128)(2,1)S(1)} %maximum_select_fusion.2), channel_id=1, source_target_pairs={{0,16},{1,17},{2,18},{3,19},{4,20},{5,21},{6,22},{7,23},{8,24},{9,... | collective-permute-start | bytes 1572872 | tf_op jit(solution)/shard_map/ppermute | solution.py:26
  117.7 11.2 %copy-start = (f32[128]{0:T(128)S(1)}, f32[128]{0:T(128)}, u32[]{:S(2)}) copy-start(f32[128]{0:T(128)} %param.17) | copy-start | bytes 1540
  117.7 11.2 %copy-start.1 = (f32[128]{0:T(128)S(1)}, f32[128]{0:T(128)}, u32[]{:S(2)}) copy-start(f32[128]{0:T(128)} %param.16) | copy-start | bytes 1540
  123.9 3.1 %collective-permute-start.15 = (f32[2,1024]{1,0:T(2,128)S(1)}, f32[2,1024]{1,0:T(2,128)S(1)}, u32[]{:S(2)}, u32[]{:S(2)}) collective-permute-start(f32[2,1024]{1,0:T(2,128)S(1)} %pad_maximum_fusion), channel_id=1, source_target_pairs={{0,1},{1,0},{2,3},{3,2},{4,5},{5,4},{6,7},{7,6},{8,9},{9,8},{10,11... | collective-permute-start | bytes 24584 | tf_op jit(solution)/shard_map/ppermute | solution.py:74
  127.0 5.6 %collective-permute-start.16 = (f32[2,2048]{1,0:T(2,128)S(1)}, f32[2,2048]{1,0:T(2,128)S(1)}, u32[]{:S(2)}, u32[]{:S(2)}) collective-permute-start(f32[2,2048]{1,0:T(2,128)S(1)} %maximum_select_fusion.14), channel_id=1, source_target_pairs={{0,2},{1,3},{2,0},{3,1},{4,6},{5,7},{6,4},{7,5},{8,10},{9,11},{10,... | collective-permute-start | bytes 49160 | tf_op jit(solution)/shard_map/ppermute | solution.py:74
  133.7 12.8 %collective-permute-start.17 = (f32[2,4096]{1,0:T(2,128)S(1)}, f32[2,4096]{1,0:T(2,128)S(1)}, u32[]{:S(2)}, u32[]{:S(2)}) collective-permute-start(f32[2,4096]{1,0:T(2,128)S(1)} %maximum_select_fusion.12), channel_id=1, source_target_pairs={{0,4},{1,5},{2,6},{3,7},{4,0},{5,1},{6,2},{7,3},{8,12},{9,13},{10,... | collective-permute-start | bytes 98312 | tf_op jit(solution)/shard_map/ppermute | solution.py:74
  146.9 10.9 %collective-permute-start.18 = (f32[2,8192]{1,0:T(2,128)S(1)}, f32[2,8192]{1,0:T(2,128)S(1)}, u32[]{:S(2)}, u32[]{:S(2)}) collective-permute-start(f32[2,8192]{1,0:T(2,128)S(1)} %maximum_select_fusion.10), channel_id=1, source_target_pairs={{0,8},{1,9},{2,10},{3,11},{4,12},{5,13},{6,14},{7,15},{8,0},{9,1},... | collective-permute-start | bytes 196616 | tf_op jit(solution)/shard_map/ppermute | solution.py:74
  157.9 12.2 %collective-permute-start.19 = (f32[2,16384]{1,0:T(2,128)S(1)}, f32[2,16384]{1,0:T(2,128)S(1)}, u32[]{:S(2)}, u32[]{:S(2)}) collective-permute-start(f32[2,16384]{1,0:T(2,128)S(1)} %maximum_select_fusion.7), channel_id=1, source_target_pairs={{0,16},{1,17},{2,18},{3,19},{4,20},{5,21},{6,22},{7,23},{8,24},{9,... | collective-permute-start | bytes 393224 | tf_op jit(solution)/shard_map/ppermute | solution.py:74

commit v6 on v4

v6 whole, which is shorter than its diff:
```python
import jax
import jax.numpy as jnp
from jax import lax
from jax.sharding import PartitionSpec as P


def split_parts(cauchy):
    upper = cauchy.astype(jnp.bfloat16)
    upper = lax.optimization_barrier(upper)
    lower = (cauchy - upper.astype(jnp.float32)).astype(jnp.bfloat16)
    return (upper, lower)


def cauchy_tile_t(pole_row, live_row, value_at, scale_at):
    return live_row[None, :] / (pole_row[None, :] - value_at[:, None]) * scale_at[:, None]


def gather_by_pairs(block, axis):
    size = lax.axis_size(axis)
    index = lax.axis_index(axis)
    held = block
    step = 1
    while step < size:
        other = lax.ppermute(held, axis, perm=[(i, i ^ step) for i in range(size)])
        low_half = (index // step) % 2 == 0
        held = jnp.where(low_half, jnp.concatenate([held, other], -1), jnp.concatenate([other, held], -1))
        step *= 2
    return held


def reduce_by_halves(compute_range, total, axis):
    size = lax.axis_size(axis)
    index = lax.axis_index(axis)
    step = size // 2
    width = total // 2
    bit = (index // step) % 2
    sent = compute_range((1 - bit) * width, width)
    got = lax.ppermute(sent, axis, perm=[(i, i ^ step) for i in range(size)])
    held = compute_range(bit * width, width) + got
    step //= 2
    while step >= 1:
        width //= 2
        bit = (index // step) % 2
        sent = lax.dynamic_slice_in_dim(held, (1 - bit) * width, width, -1)
        kept = lax.dynamic_slice_in_dim(held, bit * width, width, -1)
        held = kept + lax.ppermute(sent, axis, perm=[(i, i ^ step) for i in range(size)])
        step //= 2
    return held


def per_device(basis, position, poles, weights, kept, eigenvalues, scales):
    live_weight = weights * kept.astype(jnp.float32)
    col_total = lax.axis_size("col")
    pole_dev = poles.shape[0]
    both = jnp.concatenate([jnp.stack([poles, live_weight]), jnp.stack([eigenvalues, scales])], 1)
    both = gather_by_pairs(both, "col").reshape(2, col_total, -1)
    pole_data = both[:, :, :pole_dev].reshape(2, -1)
    value_data = both[:, :, pole_dev:].reshape(2, -1)
    pole_data = gather_by_pairs(pole_data, "row")
    row_total = lax.axis_size("row")
    child_id = lax.axis_index("row") // (row_total // 2)
    own_index = lax.dynamic_index_in_dim(position, child_id, 0, keepdims=False)
    pole_at = pole_data[0][own_index]
    live_at = pole_data[1][own_index]
    chunk = 512
    contract = (((1,), (1,)), ((), ()))

    def compute_range(offset, width):
        parts = []
        for start in range(0, width, chunk):
            values = lax.dynamic_slice_in_dim(value_data, offset + start, chunk, 1)
            upper, lower = split_parts(cauchy_tile_t(pole_at, live_at, values[0], values[1]))
            first_term = lax.dot_general(basis, upper, contract, preferred_element_type=jnp.float32)
            second_term = lax.dot_general(basis, lower, contract, preferred_element_type=jnp.float32)
            parts.append(first_term + second_term)
        return jnp.concatenate(parts, 1)

    summed = reduce_by_halves(compute_range, value_data.shape[1], "col")
    return summed.astype(jnp.bfloat16)


def solution(mesh):
    placed = (
        P("row", "col"),
        P(None, "col"),
        P(("row", "col")),
        P(("row", "col")),
        P(("row", "col")),
        P("col"),
        P("col"),
    )
    return jax.shard_map(
        per_device, mesh=mesh, in_specs=placed, out_specs=P("row", "col"), check_vma=False
    )
```

time: 183 us -> 161 us (0.88)
  the two profiles are of different devices: /device:TPU:22 before, /device:TPU:1 now
where the time goes in v6:
time: 161 us; the launch traced here: 160 us
  starting transfers between devices  74.1 us (46%)
  waiting for transfers between devices  56.5 us (35%)
  local copies, waits for them, and re-layouts  13.5 us (8%)
  matrix products  8.59 us (5%)
  other arithmetic  6.93 us (4%)
    ppermute x10, starting transfers between devices, gather_by_pairs(): other = lax.ppermute(held, axis, perm=[(i, i ^ step) for i in range(size)])  40.5 us
    ppermute x10, waiting for transfers between devices, gather_by_pairs(): other = lax.ppermute(held, axis, perm=[(i, i ^ step) for i in range(size)])  38.7 us
    ppermute x4, starting transfers between devices, reduce_by_halves(): lax.ppermute(sent, axis, perm=[(i, i ^ step) for i in range(size)])  28.5 us
    ppermute x4, waiting for transfers between devices, reduce_by_halves(): lax.ppermute(sent, axis, perm=[(i, i ^ step) for i in range(size)])  12.6 us
    gather x1, local copies, waits for them, and re-layouts, per_device(): live_at = pole_data[1][own_index]  6.15 us
    gather x1, local copies, waits for them, and re-layouts, per_device(): pole_at = pole_data[0][own_index]  6.15 us
    dot_general x8, matrix products, compute_range(): lax.dot_general(basis, lower, contract, preferred_element_type=jnp.float32)  5.55 us
    ppermute x1, waiting for transfers between devices, reduce_by_halves(): got = lax.ppermute(sent, axis, perm=[(i, i ^ step) for i in range(size)])  5.23 us
  transfers between devices with their start and end apart: 15, of which 15 were waited for; matrix products, arithmetic and copies ran while one was open for 1% of the time, Pallas kernels for 0%

profile of v6, /device:TPU:1, one launch (start us, length us, event | category | flops | bytes accessed | tf_op | source)
XLA Modules:
  0.0 160.3 jit_solution(15011240459486972805)
XLA Ops:
  1.5 16.1 %collective-permute-start = (f32[2,192]{1,0:T(2,128)S(1)}, f32[2,192]{1,0:T(2,128)S(1)}, u32[]{:S(2)}, u32[]{:S(2)}) collective-permute-start(f32[2,192]{1,0:T(2,128)S(1)} %maximum_maximum_fusion), channel_id=1, source_target_pairs={{0,1},{1,0},{2,3},{3,2},{4,5},{5,4},{6,7},{7,6},{8,9},{9,8},{10,11... | collective-permute-start | bytes 4616 | tf_op jit(solution)/shard_map/ppermute | solution.py:24
  21.2 2.2 %collective-permute-done.1 = f32[2,384]{1,0:T(2,128)S(1)} collective-permute-done((f32[2,384]{1,0:T(2,128)S(1)}, f32[2,384]{1,0:T(2,128)S(1)}, u32[]{:S(2)}, u32[]{:S(2)}) %collective-permute-start.1) | collective-permute-done | bytes 3104 | tf_op jit(solution)/shard_map/ppermute | solution.py:24
  25.5 3.2 %collective-permute-done.2 = f32[2,768]{1,0:T(2,128)S(1)} collective-permute-done((f32[2,768]{1,0:T(2,128)S(1)}, f32[2,768]{1,0:T(2,128)S(1)}, u32[]{:S(2)}, u32[]{:S(2)}) %collective-permute-start.2) | collective-permute-done | bytes 6176 | tf_op jit(solution)/shard_map/ppermute | solution.py:24
  28.8 3.8 %collective-permute-start.3 = (f32[2,1536]{1,0:T(2,128)S(1)}, f32[2,1536]{1,0:T(2,128)S(1)}, u32[]{:S(2)}, u32[]{:S(2)}) collective-permute-start(f32[2,1536]{1,0:T(2,128)S(1)} %maximum_select_fusion.9), channel_id=1, source_target_pairs={{0,8},{1,9},{2,10},{3,11},{4,12},{5,13},{6,14},{7,15},{8,0},{9,1},... | collective-permute-start | bytes 36872 | tf_op jit(solution)/shard_map/ppermute | solution.py:24
  32.7 4.4 %collective-permute-done.3 = f32[2,1536]{1,0:T(2,128)S(1)} collective-permute-done((f32[2,1536]{1,0:T(2,128)S(1)}, f32[2,1536]{1,0:T(2,128)S(1)}, u32[]{:S(2)}, u32[]{:S(2)}) %collective-permute-start.3) | collective-permute-done | bytes 12320 | tf_op jit(solution)/shard_map/ppermute | solution.py:24
  37.1 4.5 %collective-permute-start.4 = (f32[2,3072]{1,0:T(2,128)S(1)}, f32[2,3072]{1,0:T(2,128)S(1)}, u32[]{:S(2)}, u32[]{:S(2)}) collective-permute-start(f32[2,3072]{1,0:T(2,128)S(1)} %maximum_select_fusion.7), channel_id=1, source_target_pairs={{0,16},{1,17},{2,18},{3,19},{4,20},{5,21},{6,22},{7,23},{8,24},{9,... | collective-permute-start | bytes 73736 | tf_op jit(solution)/shard_map/ppermute | solution.py:24
  41.7 3.9 %collective-permute-done.4 = f32[2,3072]{1,0:T(2,128)S(1)} collective-permute-done((f32[2,3072]{1,0:T(2,128)S(1)}, f32[2,3072]{1,0:T(2,128)S(1)}, u32[]{:S(2)}, u32[]{:S(2)}) %collective-permute-start.4) | collective-permute-done | bytes 24608 | tf_op jit(solution)/shard_map/ppermute | solution.py:24
  47.7 2.7 %collective-permute-done.5 = f32[2,2048]{1,0:T(2,128)S(1)} collective-permute-done((f32[2,2048]{1,0:T(2,128)S(1)}, f32[2,2048]{1,0:T(2,128)S(1)}, u32[]{:S(2)}, u32[]{:S(2)}) %collective-permute-start.5) | collective-permute-done | bytes 16416 | tf_op jit(solution)/shard_map/ppermute | solution.py:24
  52.5 3.5 %collective-permute-done.6 = f32[2,4096]{1,0:T(2,128)S(1)} collective-permute-done((f32[2,4096]{1,0:T(2,128)S(1)}, f32[2,4096]{1,0:T(2,128)S(1)}, u32[]{:S(2)}, u32[]{:S(2)}) %collective-permute-start.6) | collective-permute-done | bytes 32800 | tf_op jit(solution)/shard_map/ppermute | solution.py:24
  56.0 1.9 %collective-permute-start.7 = (f32[2,8192]{1,0:T(2,128)S(1)}, f32[2,8192]{1,0:T(2,128)S(1)}, u32[]{:S(2)}, u32[]{:S(2)}) collective-permute-start(f32[2,8192]{1,0:T(2,128)S(1)} %maximum_select_fusion.4), channel_id=1, source_target_pairs={{0,128},{32,160},{64,192},{96,224},{128,0},{160,32},{192,64},{224,... | collective-permute-start | bytes 196616 | tf_op jit(solution)/shard_map/ppermute | solution.py:24
  58.0 3.0 %collective-permute-done.7 = f32[2,8192]{1,0:T(2,128)S(1)} collective-permute-done((f32[2,8192]{1,0:T(2,128)S(1)}, f32[2,8192]{1,0:T(2,128)S(1)}, u32[]{:S(2)}, u32[]{:S(2)}) %collective-permute-start.7) | collective-permute-done | bytes 65568 | tf_op jit(solution)/shard_map/ppermute | solution.py:24
  63.1 6.0 %collective-permute-done.8 = f32[2,16384]{1,0:T(2,128)S(1)} collective-permute-done((f32[2,16384]{1,0:T(2,128)S(1)}, f32[2,16384]{1,0:T(2,128)S(1)}, u32[]{:S(2)}, u32[]{:S(2)}) %collective-permute-start.8) | collective-permute-done | bytes 131104 | tf_op jit(solution)/shard_map/ppermute | solution.py:24
  69.3 4.6 %collective-permute-start.9 = (f32[2,32768]{1,0:T(2,128)S(1)}, f32[2,32768]{1,0:T(2,128)S(1)}, u32[]{:S(2)}, u32[]{:S(2)}) collective-permute-start(f32[2,32768]{1,0:T(2,128)S(1)} %maximum_select_fusion.1), channel_id=1, source_target_pairs={{0,512},{32,544},{64,576},{96,608},{128,640},{160,672},{192,704},{... | collective-permute-start | bytes 786440 | tf_op jit(solution)/shard_map/ppermute | solution.py:24
  74.2 8.9 %collective-permute-done.9 = f32[2,32768]{1,0:T(2,128)S(1)} collective-permute-done((f32[2,32768]{1,0:T(2,128)S(1)}, f32[2,32768]{1,0:T(2,128)S(1)}, u32[]{:S(2)}, u32[]{:S(2)}) %collective-permute-start.9) | collective-permute-done | bytes 262176 | tf_op jit(solution)/shard_map/ppermute | solution.py:24
  83.9 6.2 %gather_fusion = f32[1024]{0:T(1024)S(1)} fusion(f32[65536]{0:T(1024)S(1)} %bitcast.74, s32[1024]{0:T(1024)S(1)} %broadcast_clamp_fusion), kind=kCustom, calls=%fused_computation | custom fusion | bytes 12288 | tf_op jit(solution)/shard_map/gather | solution.py:64
  90.1 6.2 %gather_fusion.1 = f32[1024]{0:T(1024)S(1)} fusion(f32[65536]{0:T(1024)S(1)} %bitcast.73, s32[1024]{0:T(1024)S(1)} %broadcast_clamp_fusion), kind=kCustom, calls=%fused_computation.1 | custom fusion | bytes 12288 | tf_op jit(solution)/shard_map/gather | solution.py:63
  96.3 3.2 %fusion = (bf16[512,1024]{1,0:T(8,128)(2,1)S(1)}, bf16[512,1024]{1,0:T(8,128)(2,1)S(1)}, bf16[512,1024]{1,0:T(8,128)(2,1)S(1)}, bf16[512,1024]{1,0:T(8,128)(2,1)...) fusion(f32[512]{0:T(512)S(1)} %bitcast.107, ...), kind=kLoop, calls=%fused_computation.18 | loop fusion | flops 16777216 | bytes 8429568 | tf_op jit(solution)/shard_map/convert_element_type | solution.py:8
  107.4 5.1 %collective-permute-start.10 = (f32[16,2048]{1,0:T(8,128)S(1)}, f32[16,2048]{1,0:T(8,128)S(1)}, u32[]{:S(2)}, u32[]{:S(2)}) collective-permute-start(f32[16,2048]{1,0:T(8,128)S(1)} %pad_maximum_fusion), channel_id=1, source_target_pairs={{0,16},{1,17},{2,18},{3,19},{4,20},{5,21},{6,22},{7,23},{8,24},{9,... | collective-permute-start | bytes 393224 | tf_op jit(solution)/shard_map/ppermute | solution.py:38
  113.2 5.2 %collective-permute-done.10 = f32[16,2048]{1,0:T(8,128)S(1)} collective-permute-done((f32[16,2048]{1,0:T(8,128)S(1)}, f32[16,2048]{1,0:T(8,128)S(1)}, u32[]{:S(2)}, u32[]{:S(2)}) %collective-permute-start.10) | collective-permute-done | bytes 131104 | tf_op jit(solution)/shard_map/ppermute | solution.py:38
  118.5 3.6 %collective-permute-start.11 = (f32[16,1024]{1,0:T(8,128)S(1)}, f32[16,1024]{1,0:T(8,128)S(1)}, u32[]{:S(2)}, u32[]{:S(2)}) collective-permute-start(f32[16,1024]{1,0:T(8,128)S(1)} %constant_dynamic-slice_fusion.4), channel_id=1, source_target_pairs={{0,8},{1,9},{2,10},{3,11},{4,12},{5,13},{6,14},{7,15},{8,0},{9,1},... | collective-permute-start | bytes 196616 | tf_op jit(solution)/shard_map/ppermute | solution.py:46
  122.1 5.3 %collective-permute-done.11 = f32[16,1024]{1,0:T(8,128)S(1)} collective-permute-done((f32[16,1024]{1,0:T(8,128)S(1)}, f32[16,1024]{1,0:T(8,128)S(1)}, u32[]{:S(2)}, u32[]{:S(2)}) %collective-permute-start.11) | collective-permute-done | bytes 65568 | tf_op jit(solution)/shard_map/ppermute | solution.py:46
  129.4 3.9 %collective-permute-done.12 = f32[16,512]{1,0:T(8,128)S(1)} collective-permute-done((f32[16,512]{1,0:T(8,128)S(1)}, f32[16,512]{1,0:T(8,128)S(1)}, u32[]{:S(2)}, u32[]{:S(2)}) %collective-permute-start.12) | collective-permute-done | bytes 32800 | tf_op jit(solution)/shard_map/ppermute | solution.py:46
  135.2 2.5 %collective-permute-done.13 = f32[16,256]{1,0:T(8,128)S(1)} collective-permute-done((f32[16,256]{1,0:T(8,128)S(1)}, f32[16,256]{1,0:T(8,128)S(1)}, u32[]{:S(2)}, u32[]{:S(2)}) %collective-permute-start.13) | collective-permute-done | bytes 16416 | tf_op jit(solution)/shard_map/ppermute | solution.py:46
  137.8 21.1 %collective-permute-start.14 = (f32[16,128]{1,0:T(8,128)S(1)}, f32[16,128]{1,0:T(8,128)S(1)}, u32[]{:S(2)}, u32[]{:S(2)}) collective-permute-start(f32[16,128]{1,0:T(8,128)S(1)} %constant_dynamic-slice_fusion.1), channel_id=1, source_target_pairs={{0,1},{1,0},{2,3},{3,2},{4,5},{5,4},{6,7},{7,6},{8,9},{9,8},{10,11... | collective-permute-start | bytes 24584 | tf_op jit(solution)/shard_map/ppermute | solution.py:46
  (67 shorter events, 28.5 us)
Async XLA Ops:
  0.0 99.5 %copy-start = (bf16[16,1024]{1,0:T(8,128)(2,1)S(1)}, bf16[16,1024]{1,0:T(8,128)(2,1)}, u32[]{:S(2)}) copy-start(bf16[16,1024]{1,0:T(8,128)(2,1)} %param.7) | copy-start | bytes 98308
  0.0 58.0 %copy-start.1 = (s32[2,1024]{1,0:T(2,128)S(1)}, s32[2,1024]{1,0:T(2,128)}, u32[]{:S(2)}) copy-start(s32[2,1024]{1,0:T(2,128)} %param.8) | copy-start | bytes 24580
  1.5 16.9 %collective-permute-start = (f32[2,192]{1,0:T(2,128)S(1)}, f32[2,192]{1,0:T(2,128)S(1)}, u32[]{:S(2)}, u32[]{:S(2)}) collective-permute-start(f32[2,192]{1,0:T(2,128)S(1)} %maximum_maximum_fusion), channel_id=1, source_target_pairs={{0,1},{1,0},{2,3},{3,2},{4,5},{5,4},{6,7},{7,6},{8,9},{9,8},{10,11... | collective-permute-start | bytes 4616 | tf_op jit(solution)/shard_map/ppermute | solution.py:24
  19.1 4.3 %collective-permute-start.1 = (f32[2,384]{1,0:T(2,128)S(1)}, f32[2,384]{1,0:T(2,128)S(1)}, u32[]{:S(2)}, u32[]{:S(2)}) collective-permute-start(f32[2,384]{1,0:T(2,128)S(1)} %maximum_select_fusion.12), channel_id=1, source_target_pairs={{0,2},{1,3},{2,0},{3,1},{4,6},{5,7},{6,4},{7,5},{8,10},{9,11},{10,... | collective-permute-start | bytes 9224 | tf_op jit(solution)/shard_map/ppermute | solution.py:24
  23.5 5.3 %collective-permute-start.2 = (f32[2,768]{1,0:T(2,128)S(1)}, f32[2,768]{1,0:T(2,128)S(1)}, u32[]{:S(2)}, u32[]{:S(2)}) collective-permute-start(f32[2,768]{1,0:T(2,128)S(1)} %maximum_select_fusion.11), channel_id=1, source_target_pairs={{0,4},{1,5},{2,6},{3,7},{4,0},{5,1},{6,2},{7,3},{8,12},{9,13},{10,... | collective-permute-start | bytes 18440 | tf_op jit(solution)/shard_map/ppermute | solution.py:24
  28.8 8.3 %collective-permute-start.3 = (f32[2,1536]{1,0:T(2,128)S(1)}, f32[2,1536]{1,0:T(2,128)S(1)}, u32[]{:S(2)}, u32[]{:S(2)}) collective-permute-start(f32[2,1536]{1,0:T(2,128)S(1)} %maximum_select_fusion.9), channel_id=1, source_target_pairs={{0,8},{1,9},{2,10},{3,11},{4,12},{5,13},{6,14},{7,15},{8,0},{9,1},... | collective-permute-start | bytes 36872 | tf_op jit(solution)/shard_map/ppermute | solution.py:24
  37.1 8.5 %collective-permute-start.4 = (f32[2,3072]{1,0:T(2,128)S(1)}, f32[2,3072]{1,0:T(2,128)S(1)}, u32[]{:S(2)}, u32[]{:S(2)}) collective-permute-start(f32[2,3072]{1,0:T(2,128)S(1)} %maximum_select_fusion.7), channel_id=1, source_target_pairs={{0,16},{1,17},{2,18},{3,19},{4,20},{5,21},{6,22},{7,23},{8,24},{9,... | collective-permute-start | bytes 73736 | tf_op jit(solution)/shard_map/ppermute | solution.py:24
  45.8 4.6 %collective-permute-start.5 = (f32[2,2048]{1,0:T(2,128)S(1)}, f32[2,2048]{1,0:T(2,128)S(1)}, u32[]{:S(2)}, u32[]{:S(2)}) collective-permute-start(f32[2,2048]{1,0:T(2,128)S(1)} %reshape.69), channel_id=1, source_target_pairs={{0,32},{32,0},{64,96},{96,64},{128,160},{160,128},{192,224},{224,1... | collective-permute-start | bytes 49160 | tf_op jit(solution)/shard_map/ppermute | solution.py:24
  50.4 5.6 %collective-permute-start.6 = (f32[2,4096]{1,0:T(2,128)S(1)}, f32[2,4096]{1,0:T(2,128)S(1)}, u32[]{:S(2)}, u32[]{:S(2)}) collective-permute-start(f32[2,4096]{1,0:T(2,128)S(1)} %maximum_select_fusion.6), channel_id=1, source_target_pairs={{0,64},{32,96},{64,0},{96,32},{128,192},{160,224},{192,128},{224,1... | collective-permute-start | bytes 98312 | tf_op jit(solution)/shard_map/ppermute | solution.py:24
  56.0 5.0 %collective-permute-start.7 = (f32[2,8192]{1,0:T(2,128)S(1)}, f32[2,8192]{1,0:T(2,128)S(1)}, u32[]{:S(2)}, u32[]{:S(2)}) collective-permute-start(f32[2,8192]{1,0:T(2,128)S(1)} %maximum_select_fusion.4), channel_id=1, source_target_pairs={{0,128},{32,160},{64,192},{96,224},{128,0},{160,32},{192,64},{224,... | collective-permute-start | bytes 196616 | tf_op jit(solution)/shard_map/ppermute | solution.py:24
  61.1 7.9 %collective-permute-start.8 = (f32[2,16384]{1,0:T(2,128)S(1)}, f32[2,16384]{1,0:T(2,128)S(1)}, u32[]{:S(2)}, u32[]{:S(2)}) collective-permute-start(f32[2,16384]{1,0:T(2,128)S(1)} %maximum_select_fusion.2), channel_id=1, source_target_pairs={{0,256},{32,288},{64,320},{96,352},{128,384},{160,416},{192,448},{... | collective-permute-start | bytes 393224 | tf_op jit(solution)/shard_map/ppermute | solution.py:24
  69.3 13.8 %collective-permute-start.9 = (f32[2,32768]{1,0:T(2,128)S(1)}, f32[2,32768]{1,0:T(2,128)S(1)}, u32[]{:S(2)}, u32[]{:S(2)}) collective-permute-start(f32[2,32768]{1,0:T(2,128)S(1)} %maximum_select_fusion.1), channel_id=1, source_target_pairs={{0,512},{32,544},{64,576},{96,608},{128,640},{160,672},{192,704},{... | collective-permute-start | bytes 786440 | tf_op jit(solution)/shard_map/ppermute | solution.py:24
  107.4 11.0 %collective-permute-start.10 = (f32[16,2048]{1,0:T(8,128)S(1)}, f32[16,2048]{1,0:T(8,128)S(1)}, u32[]{:S(2)}, u32[]{:S(2)}) collective-permute-start(f32[16,2048]{1,0:T(8,128)S(1)} %pad_maximum_fusion), channel_id=1, source_target_pairs={{0,16},{1,17},{2,18},{3,19},{4,20},{5,21},{6,22},{7,23},{8,24},{9,... | collective-permute-start | bytes 393224 | tf_op jit(solution)/shard_map/ppermute | solution.py:38
  118.5 8.9 %collective-permute-start.11 = (f32[16,1024]{1,0:T(8,128)S(1)}, f32[16,1024]{1,0:T(8,128)S(1)}, u32[]{:S(2)}, u32[]{:S(2)}) collective-permute-start(f32[16,1024]{1,0:T(8,128)S(1)} %constant_dynamic-slice_fusion.4), channel_id=1, source_target_pairs={{0,8},{1,9},{2,10},{3,11},{4,12},{5,13},{6,14},{7,15},{8,0},{9,1},... | collective-permute-start | bytes 196616 | tf_op jit(solution)/shard_map/ppermute | solution.py:46
  127.4 5.9 %collective-permute-start.12 = (f32[16,512]{1,0:T(8,128)S(1)}, f32[16,512]{1,0:T(8,128)S(1)}, u32[]{:S(2)}, u32[]{:S(2)}) collective-permute-start(f32[16,512]{1,0:T(8,128)S(1)} %constant_dynamic-slice_fusion.3), channel_id=1, source_target_pairs={{0,4},{1,5},{2,6},{3,7},{4,0},{5,1},{6,2},{7,3},{8,12},{9,13},{10,... | collective-permute-start | bytes 98312 | tf_op jit(solution)/shard_map/ppermute | solution.py:46
  133.3 4.5 %collective-permute-start.13 = (f32[16,256]{1,0:T(8,128)S(1)}, f32[16,256]{1,0:T(8,128)S(1)}, u32[]{:S(2)}, u32[]{:S(2)}) collective-permute-start(f32[16,256]{1,0:T(8,128)S(1)} %constant_dynamic-slice_fusion.2), channel_id=1, source_target_pairs={{0,2},{1,3},{2,0},{3,1},{4,6},{5,7},{6,4},{7,5},{8,10},{9,11},{10,... | collective-permute-start | bytes 49160 | tf_op jit(solution)/shard_map/ppermute | solution.py:46
  137.8 21.9 %collective-permute-start.14 = (f32[16,128]{1,0:T(8,128)S(1)}, f32[16,128]{1,0:T(8,128)S(1)}, u32[]{:S(2)}, u32[]{:S(2)}) collective-permute-start(f32[16,128]{1,0:T(8,128)S(1)} %constant_dynamic-slice_fusion.1), channel_id=1, source_target_pairs={{0,1},{1,0},{2,3},{3,2},{4,5},{5,4},{6,7},{7,6},{8,9},{9,8},{10,11... | collective-permute-start | bytes 24584 | tf_op jit(solution)/shard_map/ppermute | solution.py:46

commit v7 on v6

--- a/solution.py
+++ b/solution.py
@@ -54,14 +54,35 @@
     pole_dev = poles.shape[0]
     both = jnp.concatenate([jnp.stack([poles, live_weight]), jnp.stack([eigenvalues, scales])], 1)
     both = gather_by_pairs(both, "col").reshape(2, col_total, -1)
-    pole_data = both[:, :, :pole_dev].reshape(2, -1)
+    pole_part = both[:, :, :pole_dev].reshape(2, -1)
     value_data = both[:, :, pole_dev:].reshape(2, -1)
-    pole_data = gather_by_pairs(pole_data, "row")
+    part_len = pole_part.shape[1]
+    base = lax.axis_index("row") * part_len
+    pieces = []
+    rest = pole_part
+    for _ in range(3):
+        piece = lax.optimization_barrier(rest.astype(jnp.bfloat16))
+        rest = rest - piece.astype(jnp.float32)
+        pieces.append(piece)
+    table = jnp.concatenate(pieces, 0)
+    local = position.reshape(-1) - base
+    looked = []
+    span = 512
+    for start in range(0, local.shape[0], span):
+        hits = local[start:start + span, None] == lax.iota(jnp.int32, part_len)[None, :]
+        found = lax.dot_general(table, hits.astype(jnp.bfloat16), (((1,), (1,)), ((), ())), preferred_element_type=jnp.float32)
+        looked.append((found[0:2] + found[2:4]) + found[4:6])
+    looked = jnp.concatenate(looked, 1)
     row_total = lax.axis_size("row")
+    step = 1
+    while step < row_total:
+        looked = looked + lax.ppermute(looked, "row", perm=[(i, i ^ step) for i in range(row_total)])
+        step *= 2
     child_id = lax.axis_index("row") // (row_total // 2)
-    own_index = lax.dynamic_index_in_dim(position, child_id, 0, keepdims=False)
-    pole_at = pole_data[0][own_index]
-    live_at = pole_data[1][own_index]
+    own_cols = position.shape[1]
+    own_poles = lax.dynamic_slice_in_dim(looked, child_id * own_cols, own_cols, 1)
+    pole_at = own_poles[0]
+    live_at = own_poles[1]
     chunk = 512
     contract = (((1,), (1,)), ((), ()))
 

time: 161 us -> 138 us (0.86)
  local copies, waits for them, and re-layouts: 13.5 us -> 0.81 us
  waiting for transfers between devices: 56.5 us -> 47.8 us
  starting transfers between devices: 74.1 us -> 69.3 us
  matrix products: 8.59 us -> 12.3 us
    ppermute x10 -> x5, waiting for transfers between devices: 38.7 us -> 13.8 us  [gather_by_pairs(): other = lax.ppermute(held, axis, perm=[(i, i ^ step) for i in range(size)])]
    ppermute x0 -> x5, waiting for transfers between devices: none -> 15.5 us  [per_device(): lax.ppermute(looked, 'row', perm=[(i, i ^ step) for i in range(row_total)])]
    ppermute x10 -> x5, starting transfers between devices: 40.5 us -> 28.2 us  [gather_by_pairs(): other = lax.ppermute(held, axis, perm=[(i, i ^ step) for i in range(size)])]
    gather x2 -> x0, local copies, waits for them, and re-layouts: 12.3 us -> none  [the longest x1 6.15 us: per_device(): live_at = pole_data[1][own_index]]
    ppermute x0 -> x5, starting transfers between devices: none -> 12.3 us  [per_device(): lax.ppermute(looked, 'row', perm=[(i, i ^ step) for i in range(row_total)])]
    ppermute x4, starting transfers between devices: 28.5 us -> 24.3 us  [reduce_by_halves(): lax.ppermute(sent, axis, perm=[(i, i ^ step) for i in range(size)])]
    dot_general x0 -> x4, matrix products: none -> 3.66 us  [per_device(): lax.dot_general(table, hits.astype(jnp.bfloat16), (((1,), (1,)), ((), ())...]
  transfers between devices with their start and end apart: 15 -> 15, of which waited for: 15 -> 14; matrix products, arithmetic and copies ran while one was open for 1% -> 1% of each run, Pallas kernels for 0% -> 0%
where the time goes in v7:
time: 138 us
  starting transfers between devices  69.3 us (50%)
  waiting for transfers between devices  47.8 us (35%)
  matrix products  12.3 us (9%)
  other arithmetic  7.01 us (5%)
    ppermute x5, starting transfers between devices, gather_by_pairs(): other = lax.ppermute(held, axis, perm=[(i, i ^ step) for i in range(size)])  28.2 us
    ppermute x4, starting transfers between devices, reduce_by_halves(): lax.ppermute(sent, axis, perm=[(i, i ^ step) for i in range(size)])  24.3 us
    ppermute x5, waiting for transfers between devices, per_device(): lax.ppermute(looked, 'row', perm=[(i, i ^ step) for i in range(row_total)])  15.5 us
    ppermute x5, waiting for transfers between devices, gather_by_pairs(): other = lax.ppermute(held, axis, perm=[(i, i ^ step) for i in range(size)])  13.8 us
    ppermute x4, waiting for transfers between devices, reduce_by_halves(): lax.ppermute(sent, axis, perm=[(i, i ^ step) for i in range(size)])  12.7 us
    ppermute x5, starting transfers between devices, per_device(): lax.ppermute(looked, 'row', perm=[(i, i ^ step) for i in range(row_total)])  12.3 us
    ppermute x1, waiting for transfers between devices, reduce_by_halves(): got = lax.ppermute(sent, axis, perm=[(i, i ^ step) for i in range(size)])  5.82 us
    dot_general x8, matrix products, compute_range(): lax.dot_general(basis, lower, contract, preferred_element_type=jnp.float32)  5.55 us
  transfers between devices with their start and end apart: 15, of which 14 were waited for; matrix products, arithmetic and copies ran while one was open for 1% of the time, Pallas kernels for 0%

profile of v7, /device:TPU:1, one launch (start us, length us, event | category | flops | bytes accessed | tf_op | source)
XLA Modules:
  0.0 137.8 jit_solution(9536357641834003558)
XLA Ops:
  1.4 16.1 %collective-permute-start = (f32[2,192]{1,0:T(2,128)S(1)}, f32[2,192]{1,0:T(2,128)S(1)}, u32[]{:S(2)}, u32[]{:S(2)}) collective-permute-start(f32[2,192]{1,0:T(2,128)S(1)} %maximum_maximum_fusion), channel_id=1, source_target_pairs={{0,1},{1,0},{2,3},{3,2},{4,5},{5,4},{6,7},{7,6},{8,9},{9,8},{10,11... | collective-permute-start | bytes 4616 | tf_op jit(solution)/shard_map/ppermute | solution.py:24
  21.2 2.2 %collective-permute-done.1 = f32[2,384]{1,0:T(2,128)S(1)} collective-permute-done((f32[2,384]{1,0:T(2,128)S(1)}, f32[2,384]{1,0:T(2,128)S(1)}, u32[]{:S(2)}, u32[]{:S(2)}) %collective-permute-start.1) | collective-permute-done | bytes 3104 | tf_op jit(solution)/shard_map/ppermute | solution.py:24
  25.5 3.2 %collective-permute-done.2 = f32[2,768]{1,0:T(2,128)S(1)} collective-permute-done((f32[2,768]{1,0:T(2,128)S(1)}, f32[2,768]{1,0:T(2,128)S(1)}, u32[]{:S(2)}, u32[]{:S(2)}) %collective-permute-start.2) | collective-permute-done | bytes 6176 | tf_op jit(solution)/shard_map/ppermute | solution.py:24
  28.8 3.8 %collective-permute-start.3 = (f32[2,1536]{1,0:T(2,128)S(1)}, f32[2,1536]{1,0:T(2,128)S(1)}, u32[]{:S(2)}, u32[]{:S(2)}) collective-permute-start(f32[2,1536]{1,0:T(2,128)S(1)} %maximum_select_fusion.4), channel_id=1, source_target_pairs={{0,8},{1,9},{2,10},{3,11},{4,12},{5,13},{6,14},{7,15},{8,0},{9,1},... | collective-permute-start | bytes 36872 | tf_op jit(solution)/shard_map/ppermute | solution.py:24
  32.7 4.4 %collective-permute-done.3 = f32[2,1536]{1,0:T(2,128)S(1)} collective-permute-done((f32[2,1536]{1,0:T(2,128)S(1)}, f32[2,1536]{1,0:T(2,128)S(1)}, u32[]{:S(2)}, u32[]{:S(2)}) %collective-permute-start.3) | collective-permute-done | bytes 12320 | tf_op jit(solution)/shard_map/ppermute | solution.py:24
  37.1 4.5 %collective-permute-start.4 = (f32[2,3072]{1,0:T(2,128)S(1)}, f32[2,3072]{1,0:T(2,128)S(1)}, u32[]{:S(2)}, u32[]{:S(2)}) collective-permute-start(f32[2,3072]{1,0:T(2,128)S(1)} %maximum_select_fusion.2), channel_id=1, source_target_pairs={{0,16},{1,17},{2,18},{3,19},{4,20},{5,21},{6,22},{7,23},{8,24},{9,... | collective-permute-start | bytes 73736 | tf_op jit(solution)/shard_map/ppermute | solution.py:24
  41.7 3.9 %collective-permute-done.4 = f32[2,3072]{1,0:T(2,128)S(1)} collective-permute-done((f32[2,3072]{1,0:T(2,128)S(1)}, f32[2,3072]{1,0:T(2,128)S(1)}, u32[]{:S(2)}, u32[]{:S(2)}) %collective-permute-start.4) | collective-permute-done | bytes 24608 | tf_op jit(solution)/shard_map/ppermute | solution.py:24
  49.6 1.9 %collective-permute-start.5 = (f32[2,2048]{1,0:T(2,128)S(1)}, f32[2,2048]{1,0:T(2,128)S(1)}, u32[]{:S(2)}, u32[]{:S(2)}) collective-permute-start(f32[2,2048]{1,0:T(2,128)S(1)} %pad_maximum_fusion.2), channel_id=1, source_target_pairs={{0,32},{32,0},{64,96},{96,64},{128,160},{160,128},{192,224},{224,1... | collective-permute-start | bytes 49160 | tf_op jit(solution)/shard_map/ppermute | solution.py:79
  51.5 2.6 %collective-permute-done.5 = f32[2,2048]{1,0:T(2,128)S(1)} collective-permute-done((f32[2,2048]{1,0:T(2,128)S(1)}, f32[2,2048]{1,0:T(2,128)S(1)}, u32[]{:S(2)}, u32[]{:S(2)}) %collective-permute-start.5) | collective-permute-done | bytes 16416 | tf_op jit(solution)/shard_map/ppermute | solution.py:79
  56.0 3.5 %collective-permute-done.6 = f32[2,2048]{1,0:T(2,128)S(1)} collective-permute-done((f32[2,2048]{1,0:T(2,128)S(1)}, f32[2,2048]{1,0:T(2,128)S(1)}, u32[]{:S(2)}, u32[]{:S(2)}) %collective-permute-start.6) | collective-permute-done | bytes 16416 | tf_op jit(solution)/shard_map/ppermute | solution.py:79
  59.5 1.9 %collective-permute-start.7 = (f32[2,2048]{1,0:T(2,128)S(1)}, f32[2,2048]{1,0:T(2,128)S(1)}, u32[]{:S(2)}, u32[]{:S(2)}) collective-permute-start(f32[2,2048]{1,0:T(2,128)S(1)} %add.224), channel_id=1, source_target_pairs={{0,128},{32,160},{64,192},{96,224},{128,0},{160,32},{192,64},{224,... | collective-permute-start | bytes 49160 | tf_op jit(solution)/shard_map/ppermute | solution.py:79
  61.5 2.5 %collective-permute-done.7 = f32[2,2048]{1,0:T(2,128)S(1)} collective-permute-done((f32[2,2048]{1,0:T(2,128)S(1)}, f32[2,2048]{1,0:T(2,128)S(1)}, u32[]{:S(2)}, u32[]{:S(2)}) %collective-permute-start.7) | collective-permute-done | bytes 16416 | tf_op jit(solution)/shard_map/ppermute | solution.py:79
  66.0 3.3 %collective-permute-done.8 = f32[2,2048]{1,0:T(2,128)S(1)} collective-permute-done((f32[2,2048]{1,0:T(2,128)S(1)}, f32[2,2048]{1,0:T(2,128)S(1)}, u32[]{:S(2)}, u32[]{:S(2)}) %collective-permute-start.8) | collective-permute-done | bytes 16416 | tf_op jit(solution)/shard_map/ppermute | solution.py:79
  69.4 4.6 %collective-permute-start.9 = (f32[2,2048]{1,0:T(2,128)S(1)}, f32[2,2048]{1,0:T(2,128)S(1)}, u32[]{:S(2)}, u32[]{:S(2)}) collective-permute-start(f32[2,2048]{1,0:T(2,128)S(1)} %add.226), channel_id=1, source_target_pairs={{0,512},{32,544},{64,576},{96,608},{128,640},{160,672},{192,704},{... | collective-permute-start | bytes 49160 | tf_op jit(solution)/shard_map/ppermute | solution.py:79
  74.1 3.7 %collective-permute-done.9 = f32[2,2048]{1,0:T(2,128)S(1)} collective-permute-done((f32[2,2048]{1,0:T(2,128)S(1)}, f32[2,2048]{1,0:T(2,128)S(1)}, u32[]{:S(2)}, u32[]{:S(2)}) %collective-permute-start.9) | collective-permute-done | bytes 16416 | tf_op jit(solution)/shard_map/ppermute | solution.py:79
  77.8 3.2 %fusion.8 = (bf16[512,1024]{1,0:T(8,128)(2,1)S(1)}, bf16[512,1024]{1,0:T(8,128)(2,1)S(1)}, bf16[512,1024]{1,0:T(8,128)(2,1)S(1)}, bf16[512,1024]{1,0:T(8,128)(2,...) fusion(f32[512]{0:T(512)S(1)} %bitcast.123, ...), kind=kLoop, calls=%fused_computation.28 | loop fusion | flops 16777216 | bytes 8429568 | tf_op jit(solution)/shard_map/convert_element_type | solution.py:8
  88.9 4.5 %collective-permute-start.10 = (f32[16,2048]{1,0:T(8,128)S(1)}, f32[16,2048]{1,0:T(8,128)S(1)}, u32[]{:S(2)}, u32[]{:S(2)}) collective-permute-start(f32[16,2048]{1,0:T(8,128)S(1)} %pad_maximum_fusion), channel_id=1, source_target_pairs={{0,16},{1,17},{2,18},{3,19},{4,20},{5,21},{6,22},{7,23},{8,24},{9,... | collective-permute-start | bytes 393224 | tf_op jit(solution)/shard_map/ppermute | solution.py:38
  94.1 5.8 %collective-permute-done.10 = f32[16,2048]{1,0:T(8,128)S(1)} collective-permute-done((f32[16,2048]{1,0:T(8,128)S(1)}, f32[16,2048]{1,0:T(8,128)S(1)}, u32[]{:S(2)}, u32[]{:S(2)}) %collective-permute-start.10) | collective-permute-done | bytes 131104 | tf_op jit(solution)/shard_map/ppermute | solution.py:38
  100.0 3.4 %collective-permute-start.11 = (f32[16,1024]{1,0:T(8,128)S(1)}, f32[16,1024]{1,0:T(8,128)S(1)}, u32[]{:S(2)}, u32[]{:S(2)}) collective-permute-start(f32[16,1024]{1,0:T(8,128)S(1)} %constant_dynamic-slice_fusion.4), channel_id=1, source_target_pairs={{0,8},{1,9},{2,10},{3,11},{4,12},{5,13},{6,14},{7,15},{8,0},{9,1},... | collective-permute-start | bytes 196616 | tf_op jit(solution)/shard_map/ppermute | solution.py:46
  103.4 5.8 %collective-permute-done.11 = f32[16,1024]{1,0:T(8,128)S(1)} collective-permute-done((f32[16,1024]{1,0:T(8,128)S(1)}, f32[16,1024]{1,0:T(8,128)S(1)}, u32[]{:S(2)}, u32[]{:S(2)}) %collective-permute-start.11) | collective-permute-done | bytes 65568 | tf_op jit(solution)/shard_map/ppermute | solution.py:46
  109.2 1.9 %collective-permute-start.12 = (f32[16,512]{1,0:T(8,128)S(1)}, f32[16,512]{1,0:T(8,128)S(1)}, u32[]{:S(2)}, u32[]{:S(2)}) collective-permute-start(f32[16,512]{1,0:T(8,128)S(1)} %constant_dynamic-slice_fusion.3), channel_id=1, source_target_pairs={{0,4},{1,5},{2,6},{3,7},{4,0},{5,1},{6,2},{7,3},{8,12},{9,13},{10,... | collective-permute-start | bytes 98312 | tf_op jit(solution)/shard_map/ppermute | solution.py:46
  111.2 3.6 %collective-permute-done.12 = f32[16,512]{1,0:T(8,128)S(1)} collective-permute-done((f32[16,512]{1,0:T(8,128)S(1)}, f32[16,512]{1,0:T(8,128)S(1)}, u32[]{:S(2)}, u32[]{:S(2)}) %collective-permute-start.12) | collective-permute-done | bytes 32800 | tf_op jit(solution)/shard_map/ppermute | solution.py:46
  116.8 2.5 %collective-permute-done.13 = f32[16,256]{1,0:T(8,128)S(1)} collective-permute-done((f32[16,256]{1,0:T(8,128)S(1)}, f32[16,256]{1,0:T(8,128)S(1)}, u32[]{:S(2)}, u32[]{:S(2)}) %collective-permute-start.13) | collective-permute-done | bytes 16416 | tf_op jit(solution)/shard_map/ppermute | solution.py:46
  119.3 17.0 %collective-permute-start.14 = (f32[16,128]{1,0:T(8,128)S(1)}, f32[16,128]{1,0:T(8,128)S(1)}, u32[]{:S(2)}, u32[]{:S(2)}) collective-permute-start(f32[16,128]{1,0:T(8,128)S(1)} %constant_dynamic-slice_fusion.1), channel_id=1, source_target_pairs={{0,1},{1,0},{2,3},{3,2},{4,5},{5,4},{6,7},{7,6},{8,9},{9,8},{10,11... | collective-permute-start | bytes 24584 | tf_op jit(solution)/shard_map/ppermute | solution.py:46
  (74 shorter events, 27.3 us)
Async XLA Ops:
  0.0 81.0 %copy-start = (bf16[16,1024]{1,0:T(8,128)(2,1)S(1)}, bf16[16,1024]{1,0:T(8,128)(2,1)}, u32[]{:S(2)}) copy-start(bf16[16,1024]{1,0:T(8,128)(2,1)} %param.7) | copy-start | bytes 98308
  1.4 16.9 %collective-permute-start = (f32[2,192]{1,0:T(2,128)S(1)}, f32[2,192]{1,0:T(2,128)S(1)}, u32[]{:S(2)}, u32[]{:S(2)}) collective-permute-start(f32[2,192]{1,0:T(2,128)S(1)} %maximum_maximum_fusion), channel_id=1, source_target_pairs={{0,1},{1,0},{2,3},{3,2},{4,5},{5,4},{6,7},{7,6},{8,9},{9,8},{10,11... | collective-permute-start | bytes 4616 | tf_op jit(solution)/shard_map/ppermute | solution.py:24
  19.1 4.3 %collective-permute-start.1 = (f32[2,384]{1,0:T(2,128)S(1)}, f32[2,384]{1,0:T(2,128)S(1)}, u32[]{:S(2)}, u32[]{:S(2)}) collective-permute-start(f32[2,384]{1,0:T(2,128)S(1)} %maximum_select_fusion.7), channel_id=1, source_target_pairs={{0,2},{1,3},{2,0},{3,1},{4,6},{5,7},{6,4},{7,5},{8,10},{9,11},{10,... | collective-permute-start | bytes 9224 | tf_op jit(solution)/shard_map/ppermute | solution.py:24
  23.5 5.3 %collective-permute-start.2 = (f32[2,768]{1,0:T(2,128)S(1)}, f32[2,768]{1,0:T(2,128)S(1)}, u32[]{:S(2)}, u32[]{:S(2)}) collective-permute-start(f32[2,768]{1,0:T(2,128)S(1)} %maximum_select_fusion.6), channel_id=1, source_target_pairs={{0,4},{1,5},{2,6},{3,7},{4,0},{5,1},{6,2},{7,3},{8,12},{9,13},{10,... | collective-permute-start | bytes 18440 | tf_op jit(solution)/shard_map/ppermute | solution.py:24
  28.8 8.3 %collective-permute-start.3 = (f32[2,1536]{1,0:T(2,128)S(1)}, f32[2,1536]{1,0:T(2,128)S(1)}, u32[]{:S(2)}, u32[]{:S(2)}) collective-permute-start(f32[2,1536]{1,0:T(2,128)S(1)} %maximum_select_fusion.4), channel_id=1, source_target_pairs={{0,8},{1,9},{2,10},{3,11},{4,12},{5,13},{6,14},{7,15},{8,0},{9,1},... | collective-permute-start | bytes 36872 | tf_op jit(solution)/shard_map/ppermute | solution.py:24
  37.1 8.5 %collective-permute-start.4 = (f32[2,3072]{1,0:T(2,128)S(1)}, f32[2,3072]{1,0:T(2,128)S(1)}, u32[]{:S(2)}, u32[]{:S(2)}) collective-permute-start(f32[2,3072]{1,0:T(2,128)S(1)} %maximum_select_fusion.2), channel_id=1, source_target_pairs={{0,16},{1,17},{2,18},{3,19},{4,20},{5,21},{6,22},{7,23},{8,24},{9,... | collective-permute-start | bytes 73736 | tf_op jit(solution)/shard_map/ppermute | solution.py:24
  49.6 4.5 %collective-permute-start.5 = (f32[2,2048]{1,0:T(2,128)S(1)}, f32[2,2048]{1,0:T(2,128)S(1)}, u32[]{:S(2)}, u32[]{:S(2)}) collective-permute-start(f32[2,2048]{1,0:T(2,128)S(1)} %pad_maximum_fusion.2), channel_id=1, source_target_pairs={{0,32},{32,0},{64,96},{96,64},{128,160},{160,128},{192,224},{224,1... | collective-permute-start | bytes 49160 | tf_op jit(solution)/shard_map/ppermute | solution.py:79
  54.1 5.4 %collective-permute-start.6 = (f32[2,2048]{1,0:T(2,128)S(1)}, f32[2,2048]{1,0:T(2,128)S(1)}, u32[]{:S(2)}, u32[]{:S(2)}) collective-permute-start(f32[2,2048]{1,0:T(2,128)S(1)} %fusion.59), channel_id=1, source_target_pairs={{0,64},{32,96},{64,0},{96,32},{128,192},{160,224},{192,128},{224,1... | collective-permute-start | bytes 49160 | tf_op jit(solution)/shard_map/ppermute | solution.py:79
  59.5 4.5 %collective-permute-start.7 = (f32[2,2048]{1,0:T(2,128)S(1)}, f32[2,2048]{1,0:T(2,128)S(1)}, u32[]{:S(2)}, u32[]{:S(2)}) collective-permute-start(f32[2,2048]{1,0:T(2,128)S(1)} %add.224), channel_id=1, source_target_pairs={{0,128},{32,160},{64,192},{96,224},{128,0},{160,32},{192,64},{224,... | collective-permute-start | bytes 49160 | tf_op jit(solution)/shard_map/ppermute | solution.py:79
  64.0 5.4 %collective-permute-start.8 = (f32[2,2048]{1,0:T(2,128)S(1)}, f32[2,2048]{1,0:T(2,128)S(1)}, u32[]{:S(2)}, u32[]{:S(2)}) collective-permute-start(f32[2,2048]{1,0:T(2,128)S(1)} %add.225), channel_id=1, source_target_pairs={{0,256},{32,288},{64,320},{96,352},{128,384},{160,416},{192,448},{... | collective-permute-start | bytes 49160 | tf_op jit(solution)/shard_map/ppermute | solution.py:79
  69.4 8.4 %collective-permute-start.9 = (f32[2,2048]{1,0:T(2,128)S(1)}, f32[2,2048]{1,0:T(2,128)S(1)}, u32[]{:S(2)}, u32[]{:S(2)}) collective-permute-start(f32[2,2048]{1,0:T(2,128)S(1)} %add.226), channel_id=1, source_target_pairs={{0,512},{32,544},{64,576},{96,608},{128,640},{160,672},{192,704},{... | collective-permute-start | bytes 49160 | tf_op jit(solution)/shard_map/ppermute | solution.py:79
  88.9 11.0 %collective-permute-start.10 = (f32[16,2048]{1,0:T(8,128)S(1)}, f32[16,2048]{1,0:T(8,128)S(1)}, u32[]{:S(2)}, u32[]{:S(2)}) collective-permute-start(f32[16,2048]{1,0:T(8,128)S(1)} %pad_maximum_fusion), channel_id=1, source_target_pairs={{0,16},{1,17},{2,18},{3,19},{4,20},{5,21},{6,22},{7,23},{8,24},{9,... | collective-permute-start | bytes 393224 | tf_op jit(solution)/shard_map/ppermute | solution.py:38
  100.0 9.2 %collective-permute-start.11 = (f32[16,1024]{1,0:T(8,128)S(1)}, f32[16,1024]{1,0:T(8,128)S(1)}, u32[]{:S(2)}, u32[]{:S(2)}) collective-permute-start(f32[16,1024]{1,0:T(8,128)S(1)} %constant_dynamic-slice_fusion.4), channel_id=1, source_target_pairs={{0,8},{1,9},{2,10},{3,11},{4,12},{5,13},{6,14},{7,15},{8,0},{9,1},... | collective-permute-start | bytes 196616 | tf_op jit(solution)/shard_map/ppermute | solution.py:46
  109.2 5.6 %collective-permute-start.12 = (f32[16,512]{1,0:T(8,128)S(1)}, f32[16,512]{1,0:T(8,128)S(1)}, u32[]{:S(2)}, u32[]{:S(2)}) collective-permute-start(f32[16,512]{1,0:T(8,128)S(1)} %constant_dynamic-slice_fusion.3), channel_id=1, source_target_pairs={{0,4},{1,5},{2,6},{3,7},{4,0},{5,1},{6,2},{7,3},{8,12},{9,13},{10,... | collective-permute-start | bytes 98312 | tf_op jit(solution)/shard_map/ppermute | solution.py:46
  114.8 4.5 %collective-permute-start.13 = (f32[16,256]{1,0:T(8,128)S(1)}, f32[16,256]{1,0:T(8,128)S(1)}, u32[]{:S(2)}, u32[]{:S(2)}) collective-permute-start(f32[16,256]{1,0:T(8,128)S(1)} %constant_dynamic-slice_fusion.2), channel_id=1, source_target_pairs={{0,2},{1,3},{2,0},{3,1},{4,6},{5,7},{6,4},{7,5},{8,10},{9,11},{10,... | collective-permute-start | bytes 49160 | tf_op jit(solution)/shard_map/ppermute | solution.py:46
  119.3 17.9 %collective-permute-start.14 = (f32[16,128]{1,0:T(8,128)S(1)}, f32[16,128]{1,0:T(8,128)S(1)}, u32[]{:S(2)}, u32[]{:S(2)}) collective-permute-start(f32[16,128]{1,0:T(8,128)S(1)} %constant_dynamic-slice_fusion.1), channel_id=1, source_target_pairs={{0,1},{1,0},{2,3},{3,2},{4,5},{5,4},{6,7},{7,6},{8,9},{9,8},{10,11... | collective-permute-start | bytes 24584 | tf_op jit(solution)/shard_map/ppermute | solution.py:46

commit v8 on v7

--- a/solution.py
+++ b/solution.py
@@ -28,24 +28,30 @@
     return held
 
 
-def reduce_by_halves(compute_range, total, axis):
+def reduce_by_halves(compute_range, total, axis, inputs):
     size = lax.axis_size(axis)
     index = lax.axis_index(axis)
-    step = size // 2
+    step = 1
     width = total // 2
-    bit = (index // step) % 2
-    sent = compute_range((1 - bit) * width, width)
+    bit = index % 2
+    sent = compute_range(inputs, (1 - bit) * width, width)
+    sent, inputs = lax.optimization_barrier((sent, inputs))
     got = lax.ppermute(sent, axis, perm=[(i, i ^ step) for i in range(size)])
-    held = compute_range(bit * width, width) + got
-    step //= 2
-    while step >= 1:
+    held = compute_range(inputs, bit * width, width) + got
+    step *= 2
+    while step < size:
         width //= 2
         bit = (index // step) % 2
         sent = lax.dynamic_slice_in_dim(held, (1 - bit) * width, width, -1)
         kept = lax.dynamic_slice_in_dim(held, bit * width, width, -1)
         held = kept + lax.ppermute(sent, axis, perm=[(i, i ^ step) for i in range(size)])
-        step //= 2
+        step *= 2
     return held
+
+
+def bit_reversed(count):
+    width = count.bit_length() - 1
+    return [int(format(i, "0%db" % width)[::-1], 2) for i in range(count)]
 
 
 def per_device(basis, position, poles, weights, kept, eigenvalues, scales):
@@ -86,7 +92,11 @@
     chunk = 512
     contract = (((1,), (1,)), ((), ()))
 
-    def compute_range(offset, width):
+    blocks = value_data.reshape(2, col_total, -1)
+    value_data = jnp.concatenate([blocks[:, b] for b in bit_reversed(col_total)], 1)
+
+    def compute_range(inputs, offset, width):
+        pole_at, live_at, value_data = inputs
         parts = []
         for start in range(0, width, chunk):
             values = lax.dynamic_slice_in_dim(value_data, offset + start, chunk, 1)
@@ -96,7 +106,7 @@
             parts.append(first_term + second_term)
         return jnp.concatenate(parts, 1)
 
-    summed = reduce_by_halves(compute_range, value_data.shape[1], "col")
+    summed = reduce_by_halves(compute_range, value_data.shape[1], "col", (pole_at, live_at, value_data))
     return summed.astype(jnp.bfloat16)
 
 

time: 138 us -> 134 us (0.971); the launches traced: 138 us -> 132 us
  starting transfers between devices: 69.3 us -> 66 us
  waiting for transfers between devices: 47.8 us -> 44.6 us
    ppermute x4, starting transfers between devices: 24.3 us -> 12.6 us  [reduce_by_halves(): lax.ppermute(sent, axis, perm=[(i, i ^ step) for i in range(size)])]
    ppermute x1, starting transfers between devices: 4.51 us -> 13 us  [reduce_by_halves(): got = lax.ppermute(sent, axis, perm=[(i, i ^ step) for i in range(size)])]
    ppermute x1, waiting for transfers between devices: 5.82 us -> 0.01 us  [reduce_by_halves(): got = lax.ppermute(sent, axis, perm=[(i, i ^ step) for i in range(size)])]
    ppermute x4, waiting for transfers between devices: 12.7 us -> 15.5 us  [reduce_by_halves(): lax.ppermute(sent, axis, perm=[(i, i ^ step) for i in range(size)])]
    convert_element_type x1 -> x2, other arithmetic: 3.2 us -> 3.12 us  [split_parts(): upper = cauchy.astype(jnp.bfloat16)]
  transfers between devices with their start and end apart: 15 -> 15, of which waited for: 14 -> 13; matrix products, arithmetic and copies ran while one was open for 1% -> 6% of each run, Pallas kernels for 0% -> 0%
where the time goes in v8:
time: 134 us; the launch traced here: 132 us
  starting transfers between devices  66 us (49%)
  waiting for transfers between devices  44.6 us (33%)
  matrix products  12.5 us (9%)
  other arithmetic  6.94 us (5%)
    ppermute x5, starting transfers between devices, gather_by_pairs(): other = lax.ppermute(held, axis, perm=[(i, i ^ step) for i in range(size)])  28.2 us
    ppermute x4, waiting for transfers between devices, reduce_by_halves(): lax.ppermute(sent, axis, perm=[(i, i ^ step) for i in range(size)])  15.5 us
    ppermute x5, waiting for transfers between devices, per_device(): lax.ppermute(looked, 'row', perm=[(i, i ^ step) for i in range(row_total)])  15.3 us
    ppermute x5, waiting for transfers between devices, gather_by_pairs(): other = lax.ppermute(held, axis, perm=[(i, i ^ step) for i in range(size)])  13.7 us
    ppermute x1, starting transfers between devices, reduce_by_halves(): got = lax.ppermute(sent, axis, perm=[(i, i ^ step) for i in range(size)])  13 us
    ppermute x4, starting transfers between devices, reduce_by_halves(): lax.ppermute(sent, axis, perm=[(i, i ^ step) for i in range(size)])  12.6 us
    ppermute x5, starting transfers between devices, per_device(): lax.ppermute(looked, 'row', perm=[(i, i ^ step) for i in range(row_total)])  12.3 us
    dot_general x8, matrix products, compute_range(): lax.dot_general(basis, lower, contract, preferred_element_type=jnp.float32)  5.81 us
  transfers between devices with their start and end apart: 15, of which 13 were waited for; matrix products, arithmetic and copies ran while one was open for 6% of the time, Pallas kernels for 0%

profile of v8, /device:TPU:1, one launch (start us, length us, event | category | flops | bytes accessed | tf_op | source)
XLA Modules:
  0.0 132.0 jit_solution(15621370407018010072)
XLA Ops:
  1.4 16.1 %collective-permute-start = (f32[2,192]{1,0:T(2,128)S(1)}, f32[2,192]{1,0:T(2,128)S(1)}, u32[]{:S(2)}, u32[]{:S(2)}) collective-permute-start(f32[2,192]{1,0:T(2,128)S(1)} %maximum_maximum_fusion), channel_id=1, source_target_pairs={{0,1},{1,0},{2,3},{3,2},{4,5},{5,4},{6,7},{7,6},{8,9},{9,8},{10,11... | collective-permute-start | bytes 4616 | tf_op jit(solution)/shard_map/ppermute | solution.py:24
  19.2 1.9 %collective-permute-start.1 = (f32[2,384]{1,0:T(2,128)S(1)}, f32[2,384]{1,0:T(2,128)S(1)}, u32[]{:S(2)}, u32[]{:S(2)}) collective-permute-start(f32[2,384]{1,0:T(2,128)S(1)} %maximum_select_fusion.7), channel_id=1, source_target_pairs={{0,2},{1,3},{2,0},{3,1},{4,6},{5,7},{6,4},{7,5},{8,10},{9,11},{10,... | collective-permute-start | bytes 9224 | tf_op jit(solution)/shard_map/ppermute | solution.py:24
  21.3 2.2 %collective-permute-done.1 = f32[2,384]{1,0:T(2,128)S(1)} collective-permute-done((f32[2,384]{1,0:T(2,128)S(1)}, f32[2,384]{1,0:T(2,128)S(1)}, u32[]{:S(2)}, u32[]{:S(2)}) %collective-permute-start.1) | collective-permute-done | bytes 3104 | tf_op jit(solution)/shard_map/ppermute | solution.py:24
  25.6 3.2 %collective-permute-done.2 = f32[2,768]{1,0:T(2,128)S(1)} collective-permute-done((f32[2,768]{1,0:T(2,128)S(1)}, f32[2,768]{1,0:T(2,128)S(1)}, u32[]{:S(2)}, u32[]{:S(2)}) %collective-permute-start.2) | collective-permute-done | bytes 6176 | tf_op jit(solution)/shard_map/ppermute | solution.py:24
  28.8 3.8 %collective-permute-start.3 = (f32[2,1536]{1,0:T(2,128)S(1)}, f32[2,1536]{1,0:T(2,128)S(1)}, u32[]{:S(2)}, u32[]{:S(2)}) collective-permute-start(f32[2,1536]{1,0:T(2,128)S(1)} %maximum_select_fusion.4), channel_id=1, source_target_pairs={{0,8},{1,9},{2,10},{3,11},{4,12},{5,13},{6,14},{7,15},{8,0},{9,1},... | collective-permute-start | bytes 36872 | tf_op jit(solution)/shard_map/ppermute | solution.py:24
  32.8 4.4 %collective-permute-done.3 = f32[2,1536]{1,0:T(2,128)S(1)} collective-permute-done((f32[2,1536]{1,0:T(2,128)S(1)}, f32[2,1536]{1,0:T(2,128)S(1)}, u32[]{:S(2)}, u32[]{:S(2)}) %collective-permute-start.3) | collective-permute-done | bytes 12320 | tf_op jit(solution)/shard_map/ppermute | solution.py:24
  37.2 4.5 %collective-permute-start.4 = (f32[2,3072]{1,0:T(2,128)S(1)}, f32[2,3072]{1,0:T(2,128)S(1)}, u32[]{:S(2)}, u32[]{:S(2)}) collective-permute-start(f32[2,3072]{1,0:T(2,128)S(1)} %maximum_select_fusion.2), channel_id=1, source_target_pairs={{0,16},{1,17},{2,18},{3,19},{4,20},{5,21},{6,22},{7,23},{8,24},{9,... | collective-permute-start | bytes 73736 | tf_op jit(solution)/shard_map/ppermute | solution.py:24
  41.7 3.9 %collective-permute-done.4 = f32[2,3072]{1,0:T(2,128)S(1)} collective-permute-done((f32[2,3072]{1,0:T(2,128)S(1)}, f32[2,3072]{1,0:T(2,128)S(1)}, u32[]{:S(2)}, u32[]{:S(2)}) %collective-permute-start.4) | collective-permute-done | bytes 24608 | tf_op jit(solution)/shard_map/ppermute | solution.py:24
  49.9 1.9 %collective-permute-start.5 = (f32[2,2048]{1,0:T(2,128)S(1)}, f32[2,2048]{1,0:T(2,128)S(1)}, u32[]{:S(2)}, u32[]{:S(2)}) collective-permute-start(f32[2,2048]{1,0:T(2,128)S(1)} %pad_maximum_fusion.2), channel_id=1, source_target_pairs={{0,32},{32,0},{64,96},{96,64},{128,160},{160,128},{192,224},{224,1... | collective-permute-start | bytes 49160 | tf_op jit(solution)/shard_map/ppermute | solution.py:85
  52.1 2.2 %collective-permute-done.5 = f32[2,2048]{1,0:T(2,128)S(1)} collective-permute-done((f32[2,2048]{1,0:T(2,128)S(1)}, f32[2,2048]{1,0:T(2,128)S(1)}, u32[]{:S(2)}, u32[]{:S(2)}) %collective-permute-start.5) | collective-permute-done | bytes 16416 | tf_op jit(solution)/shard_map/ppermute | solution.py:85
  56.3 3.4 %collective-permute-done.6 = f32[2,2048]{1,0:T(2,128)S(1)} collective-permute-done((f32[2,2048]{1,0:T(2,128)S(1)}, f32[2,2048]{1,0:T(2,128)S(1)}, u32[]{:S(2)}, u32[]{:S(2)}) %collective-permute-start.6) | collective-permute-done | bytes 16416 | tf_op jit(solution)/shard_map/ppermute | solution.py:85
  61.7 2.5 %collective-permute-done.7 = f32[2,2048]{1,0:T(2,128)S(1)} collective-permute-done((f32[2,2048]{1,0:T(2,128)S(1)}, f32[2,2048]{1,0:T(2,128)S(1)}, u32[]{:S(2)}, u32[]{:S(2)}) %collective-permute-start.7) | collective-permute-done | bytes 16416 | tf_op jit(solution)/shard_map/ppermute | solution.py:85
  66.2 3.4 %collective-permute-done.8 = f32[2,2048]{1,0:T(2,128)S(1)} collective-permute-done((f32[2,2048]{1,0:T(2,128)S(1)}, f32[2,2048]{1,0:T(2,128)S(1)}, u32[]{:S(2)}, u32[]{:S(2)}) %collective-permute-start.8) | collective-permute-done | bytes 16416 | tf_op jit(solution)/shard_map/ppermute | solution.py:85
  69.6 4.6 %collective-permute-start.9 = (f32[2,2048]{1,0:T(2,128)S(1)}, f32[2,2048]{1,0:T(2,128)S(1)}, u32[]{:S(2)}, u32[]{:S(2)}) collective-permute-start(f32[2,2048]{1,0:T(2,128)S(1)} %add.226), channel_id=1, source_target_pairs={{0,512},{32,544},{64,576},{96,608},{128,640},{160,672},{192,704},{... | collective-permute-start | bytes 49160 | tf_op jit(solution)/shard_map/ppermute | solution.py:85
  74.3 3.7 %collective-permute-done.9 = f32[2,2048]{1,0:T(2,128)S(1)} collective-permute-done((f32[2,2048]{1,0:T(2,128)S(1)}, f32[2,2048]{1,0:T(2,128)S(1)}, u32[]{:S(2)}, u32[]{:S(2)}) %collective-permute-start.9) | collective-permute-done | bytes 16416 | tf_op jit(solution)/shard_map/ppermute | solution.py:85
  84.1 13.0 %collective-permute-start.10 = (f32[16,2048]{1,0:T(8,128)S(1)}, f32[16,2048]{1,0:T(8,128)S(1)}, u32[]{:S(2)}, u32[]{:S(2)}) collective-permute-start(f32[16,2048]{1,0:T(8,128)S(1)} %pad_maximum_fusion), channel_id=1, source_target_pairs={{0,1},{1,0},{2,3},{3,2},{4,5},{5,4},{6,7},{7,6},{8,9},{9,8},{10,11... | collective-permute-start | bytes 393224 | tf_op jit(solution)/shard_map/ppermute | solution.py:39
  103.2 1.9 %collective-permute-start.11 = (f32[16,1024]{1,0:T(8,128)S(1)}, f32[16,1024]{1,0:T(8,128)S(1)}, u32[]{:S(2)}, u32[]{:S(2)}) collective-permute-start(f32[16,1024]{1,0:T(8,128)S(1)} %constant_dynamic-slice_fusion.4), channel_id=1, source_target_pairs={{0,2},{1,3},{2,0},{3,1},{4,6},{5,7},{6,4},{7,5},{8,10},{9,11},{10,... | collective-permute-start | bytes 196616 | tf_op jit(solution)/shard_map/ppermute | solution.py:47
  105.2 3.7 %collective-permute-done.11 = f32[16,1024]{1,0:T(8,128)S(1)} collective-permute-done((f32[16,1024]{1,0:T(8,128)S(1)}, f32[16,1024]{1,0:T(8,128)S(1)}, u32[]{:S(2)}, u32[]{:S(2)}) %collective-permute-start.11) | collective-permute-done | bytes 65568 | tf_op jit(solution)/shard_map/ppermute | solution.py:47
  108.9 1.9 %collective-permute-start.12 = (f32[16,512]{1,0:T(8,128)S(1)}, f32[16,512]{1,0:T(8,128)S(1)}, u32[]{:S(2)}, u32[]{:S(2)}) collective-permute-start(f32[16,512]{1,0:T(8,128)S(1)} %constant_dynamic-slice_fusion.3), channel_id=1, source_target_pairs={{0,4},{1,5},{2,6},{3,7},{4,0},{5,1},{6,2},{7,3},{8,12},{9,13},{10,... | collective-permute-start | bytes 98312 | tf_op jit(solution)/shard_map/ppermute | solution.py:47
  110.8 3.9 %collective-permute-done.12 = f32[16,512]{1,0:T(8,128)S(1)} collective-permute-done((f32[16,512]{1,0:T(8,128)S(1)}, f32[16,512]{1,0:T(8,128)S(1)}, u32[]{:S(2)}, u32[]{:S(2)}) %collective-permute-start.12) | collective-permute-done | bytes 32800 | tf_op jit(solution)/shard_map/ppermute | solution.py:47
  114.7 4.2 %collective-permute-start.13 = (f32[16,256]{1,0:T(8,128)S(1)}, f32[16,256]{1,0:T(8,128)S(1)}, u32[]{:S(2)}, u32[]{:S(2)}) collective-permute-start(f32[16,256]{1,0:T(8,128)S(1)} %constant_dynamic-slice_fusion.2), channel_id=1, source_target_pairs={{0,8},{1,9},{2,10},{3,11},{4,12},{5,13},{6,14},{7,15},{8,0},{9,1},... | collective-permute-start | bytes 49160 | tf_op jit(solution)/shard_map/ppermute | solution.py:47
  118.9 4.2 %collective-permute-done.13 = f32[16,256]{1,0:T(8,128)S(1)} collective-permute-done((f32[16,256]{1,0:T(8,128)S(1)}, f32[16,256]{1,0:T(8,128)S(1)}, u32[]{:S(2)}, u32[]{:S(2)}) %collective-permute-start.13) | collective-permute-done | bytes 16416 | tf_op jit(solution)/shard_map/ppermute | solution.py:47
  123.1 4.6 %collective-permute-start.14 = (f32[16,128]{1,0:T(8,128)S(1)}, f32[16,128]{1,0:T(8,128)S(1)}, u32[]{:S(2)}, u32[]{:S(2)}) collective-permute-start(f32[16,128]{1,0:T(8,128)S(1)} %constant_dynamic-slice_fusion.1), channel_id=1, source_target_pairs={{0,16},{1,17},{2,18},{3,19},{4,20},{5,21},{6,22},{7,23},{8,24},{9,... | collective-permute-start | bytes 24584 | tf_op jit(solution)/shard_map/ppermute | solution.py:47
  127.7 3.7 %collective-permute-done.14 = f32[16,128]{1,0:T(8,128)S(1)} collective-permute-done((f32[16,128]{1,0:T(8,128)S(1)}, f32[16,128]{1,0:T(8,128)S(1)}, u32[]{:S(2)}, u32[]{:S(2)}) %collective-permute-start.14) | collective-permute-done | bytes 8224 | tf_op jit(solution)/shard_map/ppermute | solution.py:47
  (108 shorter events, 28.4 us)
Async XLA Ops:
  0.0 79.6 %copy-start = (bf16[16,1024]{1,0:T(8,128)(2,1)S(1)}, bf16[16,1024]{1,0:T(8,128)(2,1)}, u32[]{:S(2)}) copy-start(bf16[16,1024]{1,0:T(8,128)(2,1)} %param.7) | copy-start | bytes 98308
  1.4 16.9 %collective-permute-start = (f32[2,192]{1,0:T(2,128)S(1)}, f32[2,192]{1,0:T(2,128)S(1)}, u32[]{:S(2)}, u32[]{:S(2)}) collective-permute-start(f32[2,192]{1,0:T(2,128)S(1)} %maximum_maximum_fusion), channel_id=1, source_target_pairs={{0,1},{1,0},{2,3},{3,2},{4,5},{5,4},{6,7},{7,6},{8,9},{9,8},{10,11... | collective-permute-start | bytes 4616 | tf_op jit(solution)/shard_map/ppermute | solution.py:24
  19.2 4.3 %collective-permute-start.1 = (f32[2,384]{1,0:T(2,128)S(1)}, f32[2,384]{1,0:T(2,128)S(1)}, u32[]{:S(2)}, u32[]{:S(2)}) collective-permute-start(f32[2,384]{1,0:T(2,128)S(1)} %maximum_select_fusion.7), channel_id=1, source_target_pairs={{0,2},{1,3},{2,0},{3,1},{4,6},{5,7},{6,4},{7,5},{8,10},{9,11},{10,... | collective-permute-start | bytes 9224 | tf_op jit(solution)/shard_map/ppermute | solution.py:24
  23.5 5.3 %collective-permute-start.2 = (f32[2,768]{1,0:T(2,128)S(1)}, f32[2,768]{1,0:T(2,128)S(1)}, u32[]{:S(2)}, u32[]{:S(2)}) collective-permute-start(f32[2,768]{1,0:T(2,128)S(1)} %maximum_select_fusion.6), channel_id=1, source_target_pairs={{0,4},{1,5},{2,6},{3,7},{4,0},{5,1},{6,2},{7,3},{8,12},{9,13},{10,... | collective-permute-start | bytes 18440 | tf_op jit(solution)/shard_map/ppermute | solution.py:24
  28.8 8.3 %collective-permute-start.3 = (f32[2,1536]{1,0:T(2,128)S(1)}, f32[2,1536]{1,0:T(2,128)S(1)}, u32[]{:S(2)}, u32[]{:S(2)}) collective-permute-start(f32[2,1536]{1,0:T(2,128)S(1)} %maximum_select_fusion.4), channel_id=1, source_target_pairs={{0,8},{1,9},{2,10},{3,11},{4,12},{5,13},{6,14},{7,15},{8,0},{9,1},... | collective-permute-start | bytes 36872 | tf_op jit(solution)/shard_map/ppermute | solution.py:24
  37.2 8.5 %collective-permute-start.4 = (f32[2,3072]{1,0:T(2,128)S(1)}, f32[2,3072]{1,0:T(2,128)S(1)}, u32[]{:S(2)}, u32[]{:S(2)}) collective-permute-start(f32[2,3072]{1,0:T(2,128)S(1)} %maximum_select_fusion.2), channel_id=1, source_target_pairs={{0,16},{1,17},{2,18},{3,19},{4,20},{5,21},{6,22},{7,23},{8,24},{9,... | collective-permute-start | bytes 73736 | tf_op jit(solution)/shard_map/ppermute | solution.py:24
  49.9 4.5 %collective-permute-start.5 = (f32[2,2048]{1,0:T(2,128)S(1)}, f32[2,2048]{1,0:T(2,128)S(1)}, u32[]{:S(2)}, u32[]{:S(2)}) collective-permute-start(f32[2,2048]{1,0:T(2,128)S(1)} %pad_maximum_fusion.2), channel_id=1, source_target_pairs={{0,32},{32,0},{64,96},{96,64},{128,160},{160,128},{192,224},{224,1... | collective-permute-start | bytes 49160 | tf_op jit(solution)/shard_map/ppermute | solution.py:85
  54.4 5.4 %collective-permute-start.6 = (f32[2,2048]{1,0:T(2,128)S(1)}, f32[2,2048]{1,0:T(2,128)S(1)}, u32[]{:S(2)}, u32[]{:S(2)}) collective-permute-start(f32[2,2048]{1,0:T(2,128)S(1)} %fusion.61), channel_id=1, source_target_pairs={{0,64},{32,96},{64,0},{96,32},{128,192},{160,224},{192,128},{224,1... | collective-permute-start | bytes 49160 | tf_op jit(solution)/shard_map/ppermute | solution.py:85
  59.7 4.5 %collective-permute-start.7 = (f32[2,2048]{1,0:T(2,128)S(1)}, f32[2,2048]{1,0:T(2,128)S(1)}, u32[]{:S(2)}, u32[]{:S(2)}) collective-permute-start(f32[2,2048]{1,0:T(2,128)S(1)} %add.224), channel_id=1, source_target_pairs={{0,128},{32,160},{64,192},{96,224},{128,0},{160,32},{192,64},{224,... | collective-permute-start | bytes 49160 | tf_op jit(solution)/shard_map/ppermute | solution.py:85
  64.2 5.4 %collective-permute-start.8 = (f32[2,2048]{1,0:T(2,128)S(1)}, f32[2,2048]{1,0:T(2,128)S(1)}, u32[]{:S(2)}, u32[]{:S(2)}) collective-permute-start(f32[2,2048]{1,0:T(2,128)S(1)} %add.225), channel_id=1, source_target_pairs={{0,256},{32,288},{64,320},{96,352},{128,384},{160,416},{192,448},{... | collective-permute-start | bytes 49160 | tf_op jit(solution)/shard_map/ppermute | solution.py:85
  69.6 8.4 %collective-permute-start.9 = (f32[2,2048]{1,0:T(2,128)S(1)}, f32[2,2048]{1,0:T(2,128)S(1)}, u32[]{:S(2)}, u32[]{:S(2)}) collective-permute-start(f32[2,2048]{1,0:T(2,128)S(1)} %add.226), channel_id=1, source_target_pairs={{0,512},{32,544},{64,576},{96,608},{128,640},{160,672},{192,704},{... | collective-permute-start | bytes 49160 | tf_op jit(solution)/shard_map/ppermute | solution.py:85
  84.1 19.1 %collective-permute-start.10 = (f32[16,2048]{1,0:T(8,128)S(1)}, f32[16,2048]{1,0:T(8,128)S(1)}, u32[]{:S(2)}, u32[]{:S(2)}) collective-permute-start(f32[16,2048]{1,0:T(8,128)S(1)} %pad_maximum_fusion), channel_id=1, source_target_pairs={{0,1},{1,0},{2,3},{3,2},{4,5},{5,4},{6,7},{7,6},{8,9},{9,8},{10,11... | collective-permute-start | bytes 393224 | tf_op jit(solution)/shard_map/ppermute | solution.py:39
  103.2 5.6 %collective-permute-start.11 = (f32[16,1024]{1,0:T(8,128)S(1)}, f32[16,1024]{1,0:T(8,128)S(1)}, u32[]{:S(2)}, u32[]{:S(2)}) collective-permute-start(f32[16,1024]{1,0:T(8,128)S(1)} %constant_dynamic-slice_fusion.4), channel_id=1, source_target_pairs={{0,2},{1,3},{2,0},{3,1},{4,6},{5,7},{6,4},{7,5},{8,10},{9,11},{10,... | collective-permute-start | bytes 196616 | tf_op jit(solution)/shard_map/ppermute | solution.py:47
  108.9 5.8 %collective-permute-start.12 = (f32[16,512]{1,0:T(8,128)S(1)}, f32[16,512]{1,0:T(8,128)S(1)}, u32[]{:S(2)}, u32[]{:S(2)}) collective-permute-start(f32[16,512]{1,0:T(8,128)S(1)} %constant_dynamic-slice_fusion.3), channel_id=1, source_target_pairs={{0,4},{1,5},{2,6},{3,7},{4,0},{5,1},{6,2},{7,3},{8,12},{9,13},{10,... | collective-permute-start | bytes 98312 | tf_op jit(solution)/shard_map/ppermute | solution.py:47
  114.7 8.4 %collective-permute-start.13 = (f32[16,256]{1,0:T(8,128)S(1)}, f32[16,256]{1,0:T(8,128)S(1)}, u32[]{:S(2)}, u32[]{:S(2)}) collective-permute-start(f32[16,256]{1,0:T(8,128)S(1)} %constant_dynamic-slice_fusion.2), channel_id=1, source_target_pairs={{0,8},{1,9},{2,10},{3,11},{4,12},{5,13},{6,14},{7,15},{8,0},{9,1},... | collective-permute-start | bytes 49160 | tf_op jit(solution)/shard_map/ppermute | solution.py:47
  123.1 8.3 %collective-permute-start.14 = (f32[16,128]{1,0:T(8,128)S(1)}, f32[16,128]{1,0:T(8,128)S(1)}, u32[]{:S(2)}, u32[]{:S(2)}) collective-permute-start(f32[16,128]{1,0:T(8,128)S(1)} %constant_dynamic-slice_fusion.1), channel_id=1, source_target_pairs={{0,16},{1,17},{2,18},{3,19},{4,20},{5,21},{6,22},{7,23},{8,24},{9,... | collective-permute-start | bytes 24584 | tf_op jit(solution)/shard_map/ppermute | solution.py:47

commit v9 on v8

--- a/solution.py
+++ b/solution.py
@@ -58,27 +58,41 @@
     live_weight = weights * kept.astype(jnp.float32)
     col_total = lax.axis_size("col")
     pole_dev = poles.shape[0]
-    both = jnp.concatenate([jnp.stack([poles, live_weight]), jnp.stack([eigenvalues, scales])], 1)
-    both = gather_by_pairs(both, "col").reshape(2, col_total, -1)
-    pole_part = both[:, :, :pole_dev].reshape(2, -1)
-    value_data = both[:, :, pole_dev:].reshape(2, -1)
-    part_len = pole_part.shape[1]
-    base = lax.axis_index("row") * part_len
-    pieces = []
-    rest = pole_part
-    for _ in range(3):
-        piece = lax.optimization_barrier(rest.astype(jnp.bfloat16))
-        rest = rest - piece.astype(jnp.float32)
-        pieces.append(piece)
-    table = jnp.concatenate(pieces, 0)
-    local = position.reshape(-1) - base
-    looked = []
-    span = 512
-    for start in range(0, local.shape[0], span):
-        hits = local[start:start + span, None] == lax.iota(jnp.int32, part_len)[None, :]
-        found = lax.dot_general(table, hits.astype(jnp.bfloat16), (((1,), (1,)), ((), ())), preferred_element_type=jnp.float32)
-        looked.append((found[0:2] + found[2:4]) + found[4:6])
-    looked = jnp.concatenate(looked, 1)
+    own = jnp.concatenate([jnp.stack([poles, live_weight]), jnp.stack([eigenvalues, scales])], 1)
+    own_len = own.shape[1]
+    col_index = lax.axis_index("col")
+    row_base = lax.axis_index("row") * (col_total * pole_dev)
+    wanted = position.reshape(-1)
+
+    def look_up(block, first_col):
+        count = block.shape[1] // own_len
+        part = block.reshape(2, count, own_len)[:, :, :pole_dev].reshape(2, -1)
+        pieces = []
+        rest = part
+        for _ in range(3):
+            piece = lax.optimization_barrier(rest.astype(jnp.bfloat16))
+            rest = rest - piece.astype(jnp.float32)
+            pieces.append(piece)
+        table = jnp.concatenate(pieces, 0)
+        local = wanted - (row_base + first_col * pole_dev)
+        found_all = []
+        span = 512
+        for begin in range(0, local.shape[0], span):
+            hits = local[begin:begin + span, None] == lax.iota(jnp.int32, part.shape[1])[None, :]
+            found = lax.dot_general(table, hits.astype(jnp.bfloat16), (((1,), (1,)), ((), ())), preferred_element_type=jnp.float32)
+            found_all.append((found[0:2] + found[2:4]) + found[4:6])
+        return jnp.concatenate(found_all, 1)
+
+    looked = look_up(own, col_index)
+    held = own
+    step = 1
+    while step < col_total:
+        other = lax.ppermute(held, "col", perm=[(i, i ^ step) for i in range(col_total)])
+        looked = looked + look_up(other, ((col_index // step) ^ 1) * step)
+        low_half = (col_index // step) % 2 == 0
+        held = jnp.where(low_half, jnp.concatenate([held, other], -1), jnp.concatenate([other, held], -1))
+        step *= 2
+    value_data = held.reshape(2, col_total, own_len)[:, :, pole_dev:].reshape(2, -1)
     row_total = lax.axis_size("row")
     step = 1
     while step < row_total:

time: 134 us -> 133 us (level)
  waiting for transfers between devices: 44.6 us -> 36.8 us
  matrix products: 12.5 us -> 16.6 us
  starting transfers between devices: 66 us -> 68.4 us
    ppermute x5, waiting for transfers between devices: 13.7 us -> 7.37 us  [per_device(): lax.ppermute(held, 'col', perm=[(i, i ^ step) for i in range(col_total)])]
    dot_general x4 -> x24, matrix products: 3.66 us -> 7.72 us  [look_up(): lax.dot_general(table, hits.astype(jnp.bfloat16), (((1,), (1,)), ((), ())...]
    ppermute x5, starting transfers between devices: 12.3 us -> 14.2 us  [per_device(): lax.ppermute(looked, 'row', perm=[(i, i ^ step) for i in range(row_total)])]
    ppermute x5, waiting for transfers between devices: 15.3 us -> 13.5 us  [per_device(): lax.ppermute(looked, 'row', perm=[(i, i ^ step) for i in range(row_total)])]
  transfers between devices with their start and end apart: 15 -> 15, of which waited for: 13 -> 13; matrix products, arithmetic and copies ran while one was open for 6% -> 11% of each run, Pallas kernels for 0% -> 0%
where the time goes in v9:
time: 133 us; the launch traced here: 132 us
  starting transfers between devices  68.4 us (51%)
  waiting for transfers between devices  36.8 us (28%)
  matrix products  16.6 us (12%)
  other arithmetic  7.35 us (6%)
  local copies, waits for them, and re-layouts  1.57 us (1%)
    ppermute x5, starting transfers between devices, per_device(): lax.ppermute(held, 'col', perm=[(i, i ^ step) for i in range(col_total)])  29.5 us
    ppermute x4, waiting for transfers between devices, reduce_by_halves(): lax.ppermute(sent, axis, perm=[(i, i ^ step) for i in range(size)])  15.9 us
    ppermute x5, starting transfers between devices, per_device(): lax.ppermute(looked, 'row', perm=[(i, i ^ step) for i in range(row_total)])  14.2 us
    ppermute x5, waiting for transfers between devices, per_device(): lax.ppermute(looked, 'row', perm=[(i, i ^ step) for i in range(row_total)])  13.5 us
    ppermute x1, starting transfers between devices, reduce_by_halves(): got = lax.ppermute(sent, axis, perm=[(i, i ^ step) for i in range(size)])  12.6 us
    ppermute x4, starting transfers between devices, reduce_by_halves(): lax.ppermute(sent, axis, perm=[(i, i ^ step) for i in range(size)])  12.1 us
    dot_general x24, matrix products, look_up(): lax.dot_general(table, hits.astype(jnp.bfloat16), (((1,), (1,)), ((), ())...  7.72 us
    ppermute x5, waiting for transfers between devices, per_device(): lax.ppermute(held, 'col', perm=[(i, i ^ step) for i in range(col_total)])  7.37 us
  transfers between devices with their start and end apart: 15, of which 13 were waited for; matrix products, arithmetic and copies ran while one was open for 11% of the time, Pallas kernels for 0%

profile of v9, /device:TPU:1, one launch (start us, length us, event | category | flops | bytes accessed | tf_op | source)
XLA Modules:
  0.0 131.7 jit_solution(12326012713944354933)
XLA Ops:
  1.5 16.1 %collective-permute-start = (f32[2,192]{1,0:T(2,128)S(1)}, f32[2,192]{1,0:T(2,128)S(1)}, u32[]{:S(2)}, u32[]{:S(2)}) collective-permute-start(f32[2,192]{1,0:T(2,128)S(1)} %maximum_maximum_fusion), channel_id=1, source_target_pairs={{0,1},{1,0},{2,3},{3,2},{4,5},{5,4},{6,7},{7,6},{8,9},{9,8},{10,11... | collective-permute-start | bytes 4616 | tf_op jit(solution)/shard_map/ppermute | solution.py:90
  28.1 2.1 %collective-permute-done.2 = f32[2,768]{1,0:T(2,128)S(1)} collective-permute-done((f32[2,768]{1,0:T(2,128)S(1)}, f32[2,768]{1,0:T(2,128)S(1)}, u32[]{:S(2)}, u32[]{:S(2)}) %collective-permute-start.2) | collective-permute-done | bytes 6176 | tf_op jit(solution)/shard_map/ppermute | solution.py:90
  30.2 4.4 %collective-permute-start.3 = (f32[2,1536]{1,0:T(2,128)S(1)}, f32[2,1536]{1,0:T(2,128)S(1)}, u32[]{:S(2)}, u32[]{:S(2)}) collective-permute-start(f32[2,1536]{1,0:T(2,128)S(1)} %maximum_select_fusion.4), channel_id=1, source_target_pairs={{0,8},{1,9},{2,10},{3,11},{4,12},{5,13},{6,14},{7,15},{8,0},{9,1},... | collective-permute-start | bytes 36872 | tf_op jit(solution)/shard_map/ppermute | solution.py:90
  35.9 2.6 %collective-permute-done.3 = f32[2,1536]{1,0:T(2,128)S(1)} collective-permute-done((f32[2,1536]{1,0:T(2,128)S(1)}, f32[2,1536]{1,0:T(2,128)S(1)}, u32[]{:S(2)}, u32[]{:S(2)}) %collective-permute-start.3) | collective-permute-done | bytes 12320 | tf_op jit(solution)/shard_map/ppermute | solution.py:90
  38.6 5.3 %collective-permute-start.4 = (f32[2,3072]{1,0:T(2,128)S(1)}, f32[2,3072]{1,0:T(2,128)S(1)}, u32[]{:S(2)}, u32[]{:S(2)}) collective-permute-start(f32[2,3072]{1,0:T(2,128)S(1)} %maximum_select_fusion.2), channel_id=1, source_target_pairs={{0,16},{1,17},{2,18},{3,19},{4,20},{5,21},{6,22},{7,23},{8,24},{9,... | collective-permute-start | bytes 73736 | tf_op jit(solution)/shard_map/ppermute | solution.py:90
  49.9 1.9 %collective-permute-start.5 = (f32[2,2048]{1,0:T(2,128)S(1)}, f32[2,2048]{1,0:T(2,128)S(1)}, u32[]{:S(2)}, u32[]{:S(2)}) collective-permute-start(f32[2,2048]{1,0:T(2,128)S(1)} %fusion.67), channel_id=1, source_target_pairs={{0,32},{32,0},{64,96},{96,64},{128,160},{160,128},{192,224},{224,1... | collective-permute-start | bytes 49160 | tf_op jit(solution)/shard_map/ppermute | solution.py:99
  52.1 2.2 %collective-permute-done.5 = f32[2,2048]{1,0:T(2,128)S(1)} collective-permute-done((f32[2,2048]{1,0:T(2,128)S(1)}, f32[2,2048]{1,0:T(2,128)S(1)}, u32[]{:S(2)}, u32[]{:S(2)}) %collective-permute-start.5) | collective-permute-done | bytes 16416 | tf_op jit(solution)/shard_map/ppermute | solution.py:99
  54.3 1.9 %collective-permute-start.6 = (f32[2,2048]{1,0:T(2,128)S(1)}, f32[2,2048]{1,0:T(2,128)S(1)}, u32[]{:S(2)}, u32[]{:S(2)}) collective-permute-start(f32[2,2048]{1,0:T(2,128)S(1)} %add.426), channel_id=1, source_target_pairs={{0,64},{32,96},{64,0},{96,32},{128,192},{160,224},{192,128},{224,1... | collective-permute-start | bytes 49160 | tf_op jit(solution)/shard_map/ppermute | solution.py:99
  56.3 3.5 %collective-permute-done.6 = f32[2,2048]{1,0:T(2,128)S(1)} collective-permute-done((f32[2,2048]{1,0:T(2,128)S(1)}, f32[2,2048]{1,0:T(2,128)S(1)}, u32[]{:S(2)}, u32[]{:S(2)}) %collective-permute-start.6) | collective-permute-done | bytes 16416 | tf_op jit(solution)/shard_map/ppermute | solution.py:99
  59.8 1.9 %collective-permute-start.7 = (f32[2,2048]{1,0:T(2,128)S(1)}, f32[2,2048]{1,0:T(2,128)S(1)}, u32[]{:S(2)}, u32[]{:S(2)}) collective-permute-start(f32[2,2048]{1,0:T(2,128)S(1)} %add.427), channel_id=1, source_target_pairs={{0,128},{32,160},{64,192},{96,224},{128,0},{160,32},{192,64},{224,... | collective-permute-start | bytes 49160 | tf_op jit(solution)/shard_map/ppermute | solution.py:99
  61.7 2.5 %collective-permute-done.7 = f32[2,2048]{1,0:T(2,128)S(1)} collective-permute-done((f32[2,2048]{1,0:T(2,128)S(1)}, f32[2,2048]{1,0:T(2,128)S(1)}, u32[]{:S(2)}, u32[]{:S(2)}) %collective-permute-start.7) | collective-permute-done | bytes 16416 | tf_op jit(solution)/shard_map/ppermute | solution.py:99
  64.3 2.6 %collective-permute-start.8 = (f32[2,2048]{1,0:T(2,128)S(1)}, f32[2,2048]{1,0:T(2,128)S(1)}, u32[]{:S(2)}, u32[]{:S(2)}) collective-permute-start(f32[2,2048]{1,0:T(2,128)S(1)} %add.428), channel_id=1, source_target_pairs={{0,256},{32,288},{64,320},{96,352},{128,384},{160,416},{192,448},{... | collective-permute-start | bytes 49160 | tf_op jit(solution)/shard_map/ppermute | solution.py:99
  66.9 2.8 %collective-permute-done.8 = f32[2,2048]{1,0:T(2,128)S(1)} collective-permute-done((f32[2,2048]{1,0:T(2,128)S(1)}, f32[2,2048]{1,0:T(2,128)S(1)}, u32[]{:S(2)}, u32[]{:S(2)}) %collective-permute-start.8) | collective-permute-done | bytes 16416 | tf_op jit(solution)/shard_map/ppermute | solution.py:99
  69.7 5.8 %collective-permute-start.9 = (f32[2,2048]{1,0:T(2,128)S(1)}, f32[2,2048]{1,0:T(2,128)S(1)}, u32[]{:S(2)}, u32[]{:S(2)}) collective-permute-start(f32[2,2048]{1,0:T(2,128)S(1)} %add.429), channel_id=1, source_target_pairs={{0,512},{32,544},{64,576},{96,608},{128,640},{160,672},{192,704},{... | collective-permute-start | bytes 49160 | tf_op jit(solution)/shard_map/ppermute | solution.py:99
  75.6 2.4 %collective-permute-done.9 = f32[2,2048]{1,0:T(2,128)S(1)} collective-permute-done((f32[2,2048]{1,0:T(2,128)S(1)}, f32[2,2048]{1,0:T(2,128)S(1)}, u32[]{:S(2)}, u32[]{:S(2)}) %collective-permute-start.9) | collective-permute-done | bytes 16416 | tf_op jit(solution)/shard_map/ppermute | solution.py:99
  84.1 12.6 %collective-permute-start.10 = (f32[16,2048]{1,0:T(8,128)S(1)}, f32[16,2048]{1,0:T(8,128)S(1)}, u32[]{:S(2)}, u32[]{:S(2)}) collective-permute-start(f32[16,2048]{1,0:T(8,128)S(1)} %pad_maximum_fusion), channel_id=1, source_target_pairs={{0,1},{1,0},{2,3},{3,2},{4,5},{5,4},{6,7},{7,6},{8,9},{9,8},{10,11... | collective-permute-start | bytes 393224 | tf_op jit(solution)/shard_map/ppermute | solution.py:39
  102.9 1.9 %collective-permute-start.11 = (f32[16,1024]{1,0:T(8,128)S(1)}, f32[16,1024]{1,0:T(8,128)S(1)}, u32[]{:S(2)}, u32[]{:S(2)}) collective-permute-start(f32[16,1024]{1,0:T(8,128)S(1)} %constant_dynamic-slice_fusion.4), channel_id=1, source_target_pairs={{0,2},{1,3},{2,0},{3,1},{4,6},{5,7},{6,4},{7,5},{8,10},{9,11},{10,... | collective-permute-start | bytes 196616 | tf_op jit(solution)/shard_map/ppermute | solution.py:47
  104.8 3.7 %collective-permute-done.11 = f32[16,1024]{1,0:T(8,128)S(1)} collective-permute-done((f32[16,1024]{1,0:T(8,128)S(1)}, f32[16,1024]{1,0:T(8,128)S(1)}, u32[]{:S(2)}, u32[]{:S(2)}) %collective-permute-start.11) | collective-permute-done | bytes 65568 | tf_op jit(solution)/shard_map/ppermute | solution.py:47
  108.5 1.9 %collective-permute-start.12 = (f32[16,512]{1,0:T(8,128)S(1)}, f32[16,512]{1,0:T(8,128)S(1)}, u32[]{:S(2)}, u32[]{:S(2)}) collective-permute-start(f32[16,512]{1,0:T(8,128)S(1)} %constant_dynamic-slice_fusion.3), channel_id=1, source_target_pairs={{0,4},{1,5},{2,6},{3,7},{4,0},{5,1},{6,2},{7,3},{8,12},{9,13},{10,... | collective-permute-start | bytes 98312 | tf_op jit(solution)/shard_map/ppermute | solution.py:47
  110.5 3.9 %collective-permute-done.12 = f32[16,512]{1,0:T(8,128)S(1)} collective-permute-done((f32[16,512]{1,0:T(8,128)S(1)}, f32[16,512]{1,0:T(8,128)S(1)}, u32[]{:S(2)}, u32[]{:S(2)}) %collective-permute-start.12) | collective-permute-done | bytes 32800 | tf_op jit(solution)/shard_map/ppermute | solution.py:47
  114.4 4.1 %collective-permute-start.13 = (f32[16,256]{1,0:T(8,128)S(1)}, f32[16,256]{1,0:T(8,128)S(1)}, u32[]{:S(2)}, u32[]{:S(2)}) collective-permute-start(f32[16,256]{1,0:T(8,128)S(1)} %constant_dynamic-slice_fusion.2), channel_id=1, source_target_pairs={{0,8},{1,9},{2,10},{3,11},{4,12},{5,13},{6,14},{7,15},{8,0},{9,1},... | collective-permute-start | bytes 49160 | tf_op jit(solution)/shard_map/ppermute | solution.py:47
  118.5 4.2 %collective-permute-done.13 = f32[16,256]{1,0:T(8,128)S(1)} collective-permute-done((f32[16,256]{1,0:T(8,128)S(1)}, f32[16,256]{1,0:T(8,128)S(1)}, u32[]{:S(2)}, u32[]{:S(2)}) %collective-permute-start.13) | collective-permute-done | bytes 16416 | tf_op jit(solution)/shard_map/ppermute | solution.py:47
  122.8 4.1 %collective-permute-start.14 = (f32[16,128]{1,0:T(8,128)S(1)}, f32[16,128]{1,0:T(8,128)S(1)}, u32[]{:S(2)}, u32[]{:S(2)}) collective-permute-start(f32[16,128]{1,0:T(8,128)S(1)} %constant_dynamic-slice_fusion.1), channel_id=1, source_target_pairs={{0,16},{1,17},{2,18},{3,19},{4,20},{5,21},{6,22},{7,23},{8,24},{9,... | collective-permute-start | bytes 24584 | tf_op jit(solution)/shard_map/ppermute | solution.py:47
  126.9 4.1 %collective-permute-done.14 = f32[16,128]{1,0:T(8,128)S(1)} collective-permute-done((f32[16,128]{1,0:T(8,128)S(1)}, f32[16,128]{1,0:T(8,128)S(1)}, u32[]{:S(2)}, u32[]{:S(2)}) %collective-permute-start.14) | collective-permute-done | bytes 8224 | tf_op jit(solution)/shard_map/ppermute | solution.py:47
  (185 shorter events, 31.9 us)
Async XLA Ops:
  0.0 79.7 %copy-start = (bf16[16,1024]{1,0:T(8,128)(2,1)S(1)}, bf16[16,1024]{1,0:T(8,128)(2,1)}, u32[]{:S(2)}) copy-start(bf16[16,1024]{1,0:T(8,128)(2,1)} %param.7) | copy-start | bytes 98308
  0.0 20.5 %copy-start.1 = (f32[128]{0:T(128)S(1)}, f32[128]{0:T(128)}, u32[]{:S(2)}) copy-start(f32[128]{0:T(128)} %param.13) | copy-start | bytes 1540
  0.0 20.5 %copy-start.2 = (f32[128]{0:T(128)S(1)}, f32[128]{0:T(128)}, u32[]{:S(2)}) copy-start(f32[128]{0:T(128)} %param.12) | copy-start | bytes 1540
  0.0 20.5 %copy-start.3 = (f32[64]{0:T(128)S(1)}, f32[64]{0:T(128)}, u32[]{:S(2)}) copy-start(f32[64]{0:T(128)} %param.9) | copy-start | bytes 772
  1.5 19.0 %collective-permute-start = (f32[2,192]{1,0:T(2,128)S(1)}, f32[2,192]{1,0:T(2,128)S(1)}, u32[]{:S(2)}, u32[]{:S(2)}) collective-permute-start(f32[2,192]{1,0:T(2,128)S(1)} %maximum_maximum_fusion), channel_id=1, source_target_pairs={{0,1},{1,0},{2,3},{3,2},{4,5},{5,4},{6,7},{7,6},{8,9},{9,8},{10,11... | collective-permute-start | bytes 4616 | tf_op jit(solution)/shard_map/ppermute | solution.py:90
  20.6 4.3 %collective-permute-start.1 = (f32[2,384]{1,0:T(2,128)S(1)}, f32[2,384]{1,0:T(2,128)S(1)}, u32[]{:S(2)}, u32[]{:S(2)}) collective-permute-start(f32[2,384]{1,0:T(2,128)S(1)} %maximum_select_fusion.7), channel_id=1, source_target_pairs={{0,2},{1,3},{2,0},{3,1},{4,6},{5,7},{6,4},{7,5},{8,10},{9,11},{10,... | collective-permute-start | bytes 9224 | tf_op jit(solution)/shard_map/ppermute | solution.py:90
  24.9 5.3 %collective-permute-start.2 = (f32[2,768]{1,0:T(2,128)S(1)}, f32[2,768]{1,0:T(2,128)S(1)}, u32[]{:S(2)}, u32[]{:S(2)}) collective-permute-start(f32[2,768]{1,0:T(2,128)S(1)} %maximum_select_fusion.6), channel_id=1, source_target_pairs={{0,4},{1,5},{2,6},{3,7},{4,0},{5,1},{6,2},{7,3},{8,12},{9,13},{10,... | collective-permute-start | bytes 18440 | tf_op jit(solution)/shard_map/ppermute | solution.py:90
  30.2 8.3 %collective-permute-start.3 = (f32[2,1536]{1,0:T(2,128)S(1)}, f32[2,1536]{1,0:T(2,128)S(1)}, u32[]{:S(2)}, u32[]{:S(2)}) collective-permute-start(f32[2,1536]{1,0:T(2,128)S(1)} %maximum_select_fusion.4), channel_id=1, source_target_pairs={{0,8},{1,9},{2,10},{3,11},{4,12},{5,13},{6,14},{7,15},{8,0},{9,1},... | collective-permute-start | bytes 36872 | tf_op jit(solution)/shard_map/ppermute | solution.py:90
  38.6 8.5 %collective-permute-start.4 = (f32[2,3072]{1,0:T(2,128)S(1)}, f32[2,3072]{1,0:T(2,128)S(1)}, u32[]{:S(2)}, u32[]{:S(2)}) collective-permute-start(f32[2,3072]{1,0:T(2,128)S(1)} %maximum_select_fusion.2), channel_id=1, source_target_pairs={{0,16},{1,17},{2,18},{3,19},{4,20},{5,21},{6,22},{7,23},{8,24},{9,... | collective-permute-start | bytes 73736 | tf_op jit(solution)/shard_map/ppermute | solution.py:90
  49.9 4.5 %collective-permute-start.5 = (f32[2,2048]{1,0:T(2,128)S(1)}, f32[2,2048]{1,0:T(2,128)S(1)}, u32[]{:S(2)}, u32[]{:S(2)}) collective-permute-start(f32[2,2048]{1,0:T(2,128)S(1)} %fusion.67), channel_id=1, source_target_pairs={{0,32},{32,0},{64,96},{96,64},{128,160},{160,128},{192,224},{224,1... | collective-permute-start | bytes 49160 | tf_op jit(solution)/shard_map/ppermute | solution.py:99
  54.3 5.4 %collective-permute-start.6 = (f32[2,2048]{1,0:T(2,128)S(1)}, f32[2,2048]{1,0:T(2,128)S(1)}, u32[]{:S(2)}, u32[]{:S(2)}) collective-permute-start(f32[2,2048]{1,0:T(2,128)S(1)} %add.426), channel_id=1, source_target_pairs={{0,64},{32,96},{64,0},{96,32},{128,192},{160,224},{192,128},{224,1... | collective-permute-start | bytes 49160 | tf_op jit(solution)/shard_map/ppermute | solution.py:99
  59.8 4.5 %collective-permute-start.7 = (f32[2,2048]{1,0:T(2,128)S(1)}, f32[2,2048]{1,0:T(2,128)S(1)}, u32[]{:S(2)}, u32[]{:S(2)}) collective-permute-start(f32[2,2048]{1,0:T(2,128)S(1)} %add.427), channel_id=1, source_target_pairs={{0,128},{32,160},{64,192},{96,224},{128,0},{160,32},{192,64},{224,... | collective-permute-start | bytes 49160 | tf_op jit(solution)/shard_map/ppermute | solution.py:99
  64.3 5.4 %collective-permute-start.8 = (f32[2,2048]{1,0:T(2,128)S(1)}, f32[2,2048]{1,0:T(2,128)S(1)}, u32[]{:S(2)}, u32[]{:S(2)}) collective-permute-start(f32[2,2048]{1,0:T(2,128)S(1)} %add.428), channel_id=1, source_target_pairs={{0,256},{32,288},{64,320},{96,352},{128,384},{160,416},{192,448},{... | collective-permute-start | bytes 49160 | tf_op jit(solution)/shard_map/ppermute | solution.py:99
  69.7 8.4 %collective-permute-start.9 = (f32[2,2048]{1,0:T(2,128)S(1)}, f32[2,2048]{1,0:T(2,128)S(1)}, u32[]{:S(2)}, u32[]{:S(2)}) collective-permute-start(f32[2,2048]{1,0:T(2,128)S(1)} %add.429), channel_id=1, source_target_pairs={{0,512},{32,544},{64,576},{96,608},{128,640},{160,672},{192,704},{... | collective-permute-start | bytes 49160 | tf_op jit(solution)/shard_map/ppermute | solution.py:99
  84.1 18.7 %collective-permute-start.10 = (f32[16,2048]{1,0:T(8,128)S(1)}, f32[16,2048]{1,0:T(8,128)S(1)}, u32[]{:S(2)}, u32[]{:S(2)}) collective-permute-start(f32[16,2048]{1,0:T(8,128)S(1)} %pad_maximum_fusion), channel_id=1, source_target_pairs={{0,1},{1,0},{2,3},{3,2},{4,5},{5,4},{6,7},{7,6},{8,9},{9,8},{10,11... | collective-permute-start | bytes 393224 | tf_op jit(solution)/shard_map/ppermute | solution.py:39
  102.9 5.6 %collective-permute-start.11 = (f32[16,1024]{1,0:T(8,128)S(1)}, f32[16,1024]{1,0:T(8,128)S(1)}, u32[]{:S(2)}, u32[]{:S(2)}) collective-permute-start(f32[16,1024]{1,0:T(8,128)S(1)} %constant_dynamic-slice_fusion.4), channel_id=1, source_target_pairs={{0,2},{1,3},{2,0},{3,1},{4,6},{5,7},{6,4},{7,5},{8,10},{9,11},{10,... | collective-permute-start | bytes 196616 | tf_op jit(solution)/shard_map/ppermute | solution.py:47
  108.5 5.8 %collective-permute-start.12 = (f32[16,512]{1,0:T(8,128)S(1)}, f32[16,512]{1,0:T(8,128)S(1)}, u32[]{:S(2)}, u32[]{:S(2)}) collective-permute-start(f32[16,512]{1,0:T(8,128)S(1)} %constant_dynamic-slice_fusion.3), channel_id=1, source_target_pairs={{0,4},{1,5},{2,6},{3,7},{4,0},{5,1},{6,2},{7,3},{8,12},{9,13},{10,... | collective-permute-start | bytes 98312 | tf_op jit(solution)/shard_map/ppermute | solution.py:47
  114.4 8.4 %collective-permute-start.13 = (f32[16,256]{1,0:T(8,128)S(1)}, f32[16,256]{1,0:T(8,128)S(1)}, u32[]{:S(2)}, u32[]{:S(2)}) collective-permute-start(f32[16,256]{1,0:T(8,128)S(1)} %constant_dynamic-slice_fusion.2), channel_id=1, source_target_pairs={{0,8},{1,9},{2,10},{3,11},{4,12},{5,13},{6,14},{7,15},{8,0},{9,1},... | collective-permute-start | bytes 49160 | tf_op jit(solution)/shard_map/ppermute | solution.py:47
  122.8 8.3 %collective-permute-start.14 = (f32[16,128]{1,0:T(8,128)S(1)}, f32[16,128]{1,0:T(8,128)S(1)}, u32[]{:S(2)}, u32[]{:S(2)}) collective-permute-start(f32[16,128]{1,0:T(8,128)S(1)} %constant_dynamic-slice_fusion.1), channel_id=1, source_target_pairs={{0,16},{1,17},{2,18},{3,19},{4,20},{5,21},{6,22},{7,23},{8,24},{9,... | collective-permute-start | bytes 24584 | tf_op jit(solution)/shard_map/ppermute | solution.py:47

commit v10 on v9

--- a/solution.py
+++ b/solution.py
@@ -28,16 +28,15 @@
     return held
 
 
-def reduce_by_halves(compute_range, total, axis, inputs):
+def reduce_by_halves(compute_range, first_offset, total, axis, inputs, step):
     size = lax.axis_size(axis)
     index = lax.axis_index(axis)
-    step = 1
     width = total // 2
-    bit = index % 2
-    sent = compute_range(inputs, (1 - bit) * width, width)
+    bit = (index // step) % 2
+    sent = compute_range(inputs, first_offset + (1 - bit) * width, width)
     sent, inputs = lax.optimization_barrier((sent, inputs))
     got = lax.ppermute(sent, axis, perm=[(i, i ^ step) for i in range(size)])
-    held = compute_range(inputs, bit * width, width) + got
+    held = compute_range(inputs, first_offset + bit * width, width) + got
     step *= 2
     while step < size:
         width //= 2
@@ -62,7 +61,6 @@
     own_len = own.shape[1]
     col_index = lax.axis_index("col")
     row_base = lax.axis_index("row") * (col_total * pole_dev)
-    wanted = position.reshape(-1)
 
     def look_up(block, first_col):
         count = block.shape[1] // own_len
@@ -83,9 +81,19 @@
             found_all.append((found[0:2] + found[2:4]) + found[4:6])
         return jnp.concatenate(found_all, 1)
 
-    looked = look_up(own, col_index)
-    held = own
-    step = 1
+    pos_len = position.size
+    sent = jnp.concatenate([own.reshape(-1), position.astype(jnp.float32).reshape(-1), basis.astype(jnp.float32).reshape(-1)])
+    got = lax.ppermute(sent, "col", perm=[(i, i ^ 1) for i in range(col_total)])
+    other = got[:own.size].reshape(own.shape)
+    mate_position = got[own.size:own.size + pos_len].reshape(position.shape).astype(jnp.int32)
+    mate_basis = got[own.size + pos_len:].reshape(basis.shape).astype(basis.dtype)
+    low_core = col_index % 2 == 0
+    pair_position = jnp.where(low_core, jnp.concatenate([position, mate_position], 1), jnp.concatenate([mate_position, position], 1))
+    pair_basis = jnp.where(low_core, jnp.concatenate([basis, mate_basis], 1), jnp.concatenate([mate_basis, basis], 1))
+    wanted = pair_position.reshape(-1)
+    looked = look_up(own, col_index) + look_up(other, col_index ^ 1)
+    held = jnp.where(low_core, jnp.concatenate([own, other], -1), jnp.concatenate([other, own], -1))
+    step = 2
     while step < col_total:
         other = lax.ppermute(held, "col", perm=[(i, i ^ step) for i in range(col_total)])
         looked = looked + look_up(other, ((col_index // step) ^ 1) * step)
@@ -99,7 +107,7 @@
         looked = looked + lax.ppermute(looked, "row", perm=[(i, i ^ step) for i in range(row_total)])
         step *= 2
     child_id = lax.axis_index("row") // (row_total // 2)
-    own_cols = position.shape[1]
+    own_cols = pair_position.shape[1]
     own_poles = lax.dynamic_slice_in_dim(looked, child_id * own_cols, own_cols, 1)
     pole_at = own_poles[0]
     live_at = own_poles[1]
@@ -115,12 +123,13 @@
         for start in range(0, width, chunk):
             values = lax.dynamic_slice_in_dim(value_data, offset + start, chunk, 1)
             upper, lower = split_parts(cauchy_tile_t(pole_at, live_at, values[0], values[1]))
-            first_term = lax.dot_general(basis, upper, contract, preferred_element_type=jnp.float32)
-            second_term = lax.dot_general(basis, lower, contract, preferred_element_type=jnp.float32)
+            first_term = lax.dot_general(pair_basis, upper, contract, preferred_element_type=jnp.float32)
+            second_term = lax.dot_general(pair_basis, lower, contract, preferred_element_type=jnp.float32)
             parts.append(first_term + second_term)
         return jnp.concatenate(parts, 1)
 
-    summed = reduce_by_halves(compute_range, value_data.shape[1], "col", (pole_at, live_at, value_data))
+    half_new = value_data.shape[1] // 2
+    summed = reduce_by_halves(compute_range, (col_index % 2) * half_new, half_new, "col", (pole_at, live_at, value_data), 2)
     return summed.astype(jnp.bfloat16)
 
 

time: 133 us -> 135 us (1.015)
  the two profiles are of different devices: /device:TPU:1 before, /device:TPU:8 now
where the time goes in v10:
time: 135 us; the launch traced here: 134 us
  starting transfers between devices  68.4 us (51%)
  waiting for transfers between devices  29.7 us (22%)
  matrix products  23 us (17%)
  other arithmetic  10.2 us (8%)
  local copies, waits for them, and re-layouts  1.86 us (1%)
    ppermute x4, starting transfers between devices, per_device(): lax.ppermute(held, 'col', perm=[(i, i ^ step) for i in range(col_total)])  33.1 us
    ppermute x5, waiting for transfers between devices, per_device(): lax.ppermute(looked, 'row', perm=[(i, i ^ step) for i in range(row_total)])  22.2 us
    ppermute x3, starting transfers between devices, reduce_by_halves(): lax.ppermute(sent, axis, perm=[(i, i ^ step) for i in range(size)])  18.4 us
    dot_general x48, matrix products, look_up(): lax.dot_general(table, hits.astype(jnp.bfloat16), (((1,), (1,)), ((), ())...  15.7 us
    ppermute x5, starting transfers between devices, per_device(): lax.ppermute(looked, 'row', perm=[(i, i ^ step) for i in range(row_total)])  13 us
    ppermute x3, waiting for transfers between devices, reduce_by_halves(): lax.ppermute(sent, axis, perm=[(i, i ^ step) for i in range(size)])  7.27 us
    dot_general x4, matrix products, compute_range(): lax.dot_general(pair_basis, lower, contract, preferred_element_type=jnp.f...  4.76 us
    convert_element_type x2, other arithmetic, split_parts(): upper = cauchy.astype(jnp.bfloat16)  3.31 us
  transfers between devices with their start and end apart: 14, of which 9 were waited for; matrix products, arithmetic and copies ran while one was open for 14% of the time, Pallas kernels for 0%

profile of v10, /device:TPU:8, one launch (start us, length us, event | category | flops | bytes accessed | tf_op | source)
XLA Modules:
  0.0 134.2 jit_solution(12341713740059215545)
XLA Ops:
  3.0 1.9 %collective-permute-start = (f32[18816]{0:T(1024)S(1)}, f32[18816]{0:T(1024)S(1)}, u32[]{:S(2)}, u32[]{:S(2)}) collective-permute-start(f32[18816]{0:T(1024)S(1)} %pad_maximum_fusion), channel_id=1, source_target_pairs={{0,1},{1,0},{2,3},{3,2},{4,5},{5,4},{6,7},{7,6},{8,9},{9,8},{10,11... | collective-permute-start | bytes 225800 | tf_op jit(solution)/shard_map/ppermute | solution.py:86
  7.2 5.2 %collective-permute-start.1 = (f32[2,384]{1,0:T(2,128)S(1)}, f32[2,384]{1,0:T(2,128)S(1)}, u32[]{:S(2)}, u32[]{:S(2)}) collective-permute-start(f32[2,384]{1,0:T(2,128)S(1)} %maximum_select_fusion.8), channel_id=1, source_target_pairs={{0,2},{1,3},{2,0},{3,1},{4,6},{5,7},{6,4},{7,5},{8,10},{9,11},{10,... | collective-permute-start | bytes 9224 | tf_op jit(solution)/shard_map/ppermute | solution.py:98
  18.1 7.9 %collective-permute-start.2 = (f32[2,768]{1,0:T(2,128)S(1)}, f32[2,768]{1,0:T(2,128)S(1)}, u32[]{:S(2)}, u32[]{:S(2)}) collective-permute-start(f32[2,768]{1,0:T(2,128)S(1)} %maximum_select_fusion.7), channel_id=1, source_target_pairs={{0,4},{1,5},{2,6},{3,7},{4,0},{5,1},{6,2},{7,3},{8,12},{9,13},{10,... | collective-permute-start | bytes 18440 | tf_op jit(solution)/shard_map/ppermute | solution.py:98
  28.5 11.9 %collective-permute-start.3 = (f32[2,1536]{1,0:T(2,128)S(1)}, f32[2,1536]{1,0:T(2,128)S(1)}, u32[]{:S(2)}, u32[]{:S(2)}) collective-permute-start(f32[2,1536]{1,0:T(2,128)S(1)} %maximum_select_fusion.5), channel_id=1, source_target_pairs={{0,8},{1,9},{2,10},{3,11},{4,12},{5,13},{6,14},{7,15},{8,0},{9,1},... | collective-permute-start | bytes 36872 | tf_op jit(solution)/shard_map/ppermute | solution.py:98
  42.8 8.2 %collective-permute-start.4 = (f32[2,3072]{1,0:T(2,128)S(1)}, f32[2,3072]{1,0:T(2,128)S(1)}, u32[]{:S(2)}, u32[]{:S(2)}) collective-permute-start(f32[2,3072]{1,0:T(2,128)S(1)} %maximum_select_fusion.3), channel_id=1, source_target_pairs={{0,16},{1,17},{2,18},{3,19},{4,20},{5,21},{6,22},{7,23},{8,24},{9,... | collective-permute-start | bytes 73736 | tf_op jit(solution)/shard_map/ppermute | solution.py:98
  59.3 2.7 %collective-permute-start.5 = (f32[2,4096]{1,0:T(2,128)S(1)}, f32[2,4096]{1,0:T(2,128)S(1)}, u32[]{:S(2)}, u32[]{:S(2)}) collective-permute-start(f32[2,4096]{1,0:T(2,128)S(1)} %add_add_fusion), channel_id=1, source_target_pairs={{0,32},{32,0},{64,96},{96,64},{128,160},{160,128},{192,224},{224,1... | collective-permute-start | bytes 98312 | tf_op jit(solution)/shard_map/ppermute | solution.py:107
  62.3 2.8 %collective-permute-done.5 = f32[2,4096]{1,0:T(2,128)S(1)} collective-permute-done((f32[2,4096]{1,0:T(2,128)S(1)}, f32[2,4096]{1,0:T(2,128)S(1)}, u32[]{:S(2)}, u32[]{:S(2)}) %collective-permute-start.5) | collective-permute-done | bytes 32800 | tf_op jit(solution)/shard_map/ppermute | solution.py:107
  65.1 3.1 %collective-permute-start.6 = (f32[2,4096]{1,0:T(2,128)S(1)}, f32[2,4096]{1,0:T(2,128)S(1)}, u32[]{:S(2)}, u32[]{:S(2)}) collective-permute-start(f32[2,4096]{1,0:T(2,128)S(1)} %add.546), channel_id=1, source_target_pairs={{0,64},{32,96},{64,0},{96,32},{128,192},{160,224},{192,128},{224,1... | collective-permute-start | bytes 98312 | tf_op jit(solution)/shard_map/ppermute | solution.py:107
  68.2 3.9 %collective-permute-done.6 = f32[2,4096]{1,0:T(2,128)S(1)} collective-permute-done((f32[2,4096]{1,0:T(2,128)S(1)}, f32[2,4096]{1,0:T(2,128)S(1)}, u32[]{:S(2)}, u32[]{:S(2)}) %collective-permute-start.6) | collective-permute-done | bytes 32800 | tf_op jit(solution)/shard_map/ppermute | solution.py:107
  72.2 2.5 %collective-permute-start.7 = (f32[2,4096]{1,0:T(2,128)S(1)}, f32[2,4096]{1,0:T(2,128)S(1)}, u32[]{:S(2)}, u32[]{:S(2)}) collective-permute-start(f32[2,4096]{1,0:T(2,128)S(1)} %add.547), channel_id=1, source_target_pairs={{0,128},{32,160},{64,192},{96,224},{128,0},{160,32},{192,64},{224,... | collective-permute-start | bytes 98312 | tf_op jit(solution)/shard_map/ppermute | solution.py:107
  74.7 3.3 %collective-permute-done.7 = f32[2,4096]{1,0:T(2,128)S(1)} collective-permute-done((f32[2,4096]{1,0:T(2,128)S(1)}, f32[2,4096]{1,0:T(2,128)S(1)}, u32[]{:S(2)}, u32[]{:S(2)}) %collective-permute-start.7) | collective-permute-done | bytes 32800 | tf_op jit(solution)/shard_map/ppermute | solution.py:107
  78.0 2.5 %collective-permute-start.8 = (f32[2,4096]{1,0:T(2,128)S(1)}, f32[2,4096]{1,0:T(2,128)S(1)}, u32[]{:S(2)}, u32[]{:S(2)}) collective-permute-start(f32[2,4096]{1,0:T(2,128)S(1)} %add.548), channel_id=1, source_target_pairs={{0,256},{32,288},{64,320},{96,352},{128,384},{160,416},{192,448},{... | collective-permute-start | bytes 98312 | tf_op jit(solution)/shard_map/ppermute | solution.py:107
  80.6 4.5 %collective-permute-done.8 = f32[2,4096]{1,0:T(2,128)S(1)} collective-permute-done((f32[2,4096]{1,0:T(2,128)S(1)}, f32[2,4096]{1,0:T(2,128)S(1)}, u32[]{:S(2)}, u32[]{:S(2)}) %collective-permute-start.8) | collective-permute-done | bytes 32800 | tf_op jit(solution)/shard_map/ppermute | solution.py:107
  85.1 2.2 %collective-permute-start.9 = (f32[2,4096]{1,0:T(2,128)S(1)}, f32[2,4096]{1,0:T(2,128)S(1)}, u32[]{:S(2)}, u32[]{:S(2)}) collective-permute-start(f32[2,4096]{1,0:T(2,128)S(1)} %add.549), channel_id=1, source_target_pairs={{0,512},{32,544},{64,576},{96,608},{128,640},{160,672},{192,704},{... | collective-permute-start | bytes 98312 | tf_op jit(solution)/shard_map/ppermute | solution.py:107
  87.4 7.7 %collective-permute-done.9 = f32[2,4096]{1,0:T(2,128)S(1)} collective-permute-done((f32[2,4096]{1,0:T(2,128)S(1)}, f32[2,4096]{1,0:T(2,128)S(1)}, u32[]{:S(2)}, u32[]{:S(2)}) %collective-permute-start.9) | collective-permute-done | bytes 32800 | tf_op jit(solution)/shard_map/ppermute | solution.py:107
  95.1 1.7 %fusion = (bf16[512,2048]{1,0:T(8,128)(2,1)S(1)}, bf16[512,2048]{1,0:T(8,128)(2,1)S(1)}) fusion(f32[512]{0:T(512)S(1)} %bitcast.183, f32[512]{0:T(512)S(1)} %bitcast.181, f32[2048]{0:T(1024)S(1)} %bitcast.168, f32[2048]{0:T(1024)S(1)} %bitcast.162, f32[512]{0:T(512)S(1)} %bitcast.187, f32[512]{0:T(512)S(1)} %bitcast.185), kind=kLoop, calls=%fused_computation.8 | loop fusion | flops 8388608 | bytes 4218880 | tf_op jit(solution)/shard_map/convert_element_type | solution.py:8
  100.5 1.9 %collective-permute-start.10 = (f32[16,1024]{1,0:T(8,128)S(1)}, f32[16,1024]{1,0:T(8,128)S(1)}, u32[]{:S(2)}, u32[]{:S(2)}) collective-permute-start(f32[16,1024]{1,0:T(8,128)S(1)} %pad_maximum_fusion.1), channel_id=1, source_target_pairs={{0,2},{1,3},{2,0},{3,1},{4,6},{5,7},{6,4},{7,5},{8,10},{9,11},{10,... | collective-permute-start | bytes 196616 | tf_op jit(solution)/shard_map/ppermute | solution.py:38
  102.5 1.6 %fusion.2 = (bf16[512,2048]{1,0:T(8,128)(2,1)S(1)}, bf16[512,2048]{1,0:T(8,128)(2,1)S(1)}) fusion(f32[512]{0:T(512)S(1)} %bitcast.191, f32[512]{0:T(512)S(1)} %bitcast.189, f32[2048]{0:T(1024)S(1)} %bitcast.171, f32[2048]{0:T(1024)S(1)} %bitcast.165, f32[512]{0:T(512)S(1)} %bitcast.195, f32[512]{0:T(512)S(1)} %bitcast.193), kind=kLoop, calls=%fused_computation.10 | loop fusion | flops 8388608 | bytes 4218880 | tf_op jit(solution)/shard_map/convert_element_type | solution.py:8
  107.9 4.3 %collective-permute-start.11 = (f32[16,512]{1,0:T(8,128)S(1)}, f32[16,512]{1,0:T(8,128)S(1)}, u32[]{:S(2)}, u32[]{:S(2)}) collective-permute-start(f32[16,512]{1,0:T(8,128)S(1)} %constant_dynamic-slice_fusion.3), channel_id=1, source_target_pairs={{0,4},{1,5},{2,6},{3,7},{4,0},{5,1},{6,2},{7,3},{8,12},{9,13},{10,... | collective-permute-start | bytes 98312 | tf_op jit(solution)/shard_map/ppermute | solution.py:46
  112.3 2.3 %collective-permute-done.11 = f32[16,512]{1,0:T(8,128)S(1)} collective-permute-done((f32[16,512]{1,0:T(8,128)S(1)}, f32[16,512]{1,0:T(8,128)S(1)}, u32[]{:S(2)}, u32[]{:S(2)}) %collective-permute-start.11) | collective-permute-done | bytes 32800 | tf_op jit(solution)/shard_map/ppermute | solution.py:46
  114.6 7.4 %collective-permute-start.12 = (f32[16,256]{1,0:T(8,128)S(1)}, f32[16,256]{1,0:T(8,128)S(1)}, u32[]{:S(2)}, u32[]{:S(2)}) collective-permute-start(f32[16,256]{1,0:T(8,128)S(1)} %constant_dynamic-slice_fusion.2), channel_id=1, source_target_pairs={{0,8},{1,9},{2,10},{3,11},{4,12},{5,13},{6,14},{7,15},{8,0},{9,1},... | collective-permute-start | bytes 49160 | tf_op jit(solution)/shard_map/ppermute | solution.py:46
  122.0 2.1 %collective-permute-done.12 = f32[16,256]{1,0:T(8,128)S(1)} collective-permute-done((f32[16,256]{1,0:T(8,128)S(1)}, f32[16,256]{1,0:T(8,128)S(1)}, u32[]{:S(2)}, u32[]{:S(2)}) %collective-permute-start.12) | collective-permute-done | bytes 16416 | tf_op jit(solution)/shard_map/ppermute | solution.py:46
  124.2 6.6 %collective-permute-start.13 = (f32[16,128]{1,0:T(8,128)S(1)}, f32[16,128]{1,0:T(8,128)S(1)}, u32[]{:S(2)}, u32[]{:S(2)}) collective-permute-start(f32[16,128]{1,0:T(8,128)S(1)} %constant_dynamic-slice_fusion.1), channel_id=1, source_target_pairs={{0,16},{1,17},{2,18},{3,19},{4,20},{5,21},{6,22},{7,23},{8,24},{9,... | collective-permute-start | bytes 24584 | tf_op jit(solution)/shard_map/ppermute | solution.py:46
  130.8 2.8 %collective-permute-done.13 = f32[16,128]{1,0:T(8,128)S(1)} collective-permute-done((f32[16,128]{1,0:T(8,128)S(1)}, f32[16,128]{1,0:T(8,128)S(1)}, u32[]{:S(2)}, u32[]{:S(2)}) %collective-permute-start.13) | collective-permute-done | bytes 8224 | tf_op jit(solution)/shard_map/ppermute | solution.py:46
  (229 shorter events, 32.1 us)
Async XLA Ops:
  3.0 3.2 %collective-permute-start = (f32[18816]{0:T(1024)S(1)}, f32[18816]{0:T(1024)S(1)}, u32[]{:S(2)}, u32[]{:S(2)}) collective-permute-start(f32[18816]{0:T(1024)S(1)} %pad_maximum_fusion), channel_id=1, source_target_pairs={{0,1},{1,0},{2,3},{3,2},{4,5},{5,4},{6,7},{7,6},{8,9},{9,8},{10,11... | collective-permute-start | bytes 225800 | tf_op jit(solution)/shard_map/ppermute | solution.py:86
  7.2 10.7 %collective-permute-start.1 = (f32[2,384]{1,0:T(2,128)S(1)}, f32[2,384]{1,0:T(2,128)S(1)}, u32[]{:S(2)}, u32[]{:S(2)}) collective-permute-start(f32[2,384]{1,0:T(2,128)S(1)} %maximum_select_fusion.8), channel_id=1, source_target_pairs={{0,2},{1,3},{2,0},{3,1},{4,6},{5,7},{6,4},{7,5},{8,10},{9,11},{10,... | collective-permute-start | bytes 9224 | tf_op jit(solution)/shard_map/ppermute | solution.py:98
  18.1 10.1 %collective-permute-start.2 = (f32[2,768]{1,0:T(2,128)S(1)}, f32[2,768]{1,0:T(2,128)S(1)}, u32[]{:S(2)}, u32[]{:S(2)}) collective-permute-start(f32[2,768]{1,0:T(2,128)S(1)} %maximum_select_fusion.7), channel_id=1, source_target_pairs={{0,4},{1,5},{2,6},{3,7},{4,0},{5,1},{6,2},{7,3},{8,12},{9,13},{10,... | collective-permute-start | bytes 18440 | tf_op jit(solution)/shard_map/ppermute | solution.py:98
  28.5 14.2 %collective-permute-start.3 = (f32[2,1536]{1,0:T(2,128)S(1)}, f32[2,1536]{1,0:T(2,128)S(1)}, u32[]{:S(2)}, u32[]{:S(2)}) collective-permute-start(f32[2,1536]{1,0:T(2,128)S(1)} %maximum_select_fusion.5), channel_id=1, source_target_pairs={{0,8},{1,9},{2,10},{3,11},{4,12},{5,13},{6,14},{7,15},{8,0},{9,1},... | collective-permute-start | bytes 36872 | tf_op jit(solution)/shard_map/ppermute | solution.py:98
  42.8 11.4 %collective-permute-start.4 = (f32[2,3072]{1,0:T(2,128)S(1)}, f32[2,3072]{1,0:T(2,128)S(1)}, u32[]{:S(2)}, u32[]{:S(2)}) collective-permute-start(f32[2,3072]{1,0:T(2,128)S(1)} %maximum_select_fusion.3), channel_id=1, source_target_pairs={{0,16},{1,17},{2,18},{3,19},{4,20},{5,21},{6,22},{7,23},{8,24},{9,... | collective-permute-start | bytes 73736 | tf_op jit(solution)/shard_map/ppermute | solution.py:98
  59.3 5.8 %collective-permute-start.5 = (f32[2,4096]{1,0:T(2,128)S(1)}, f32[2,4096]{1,0:T(2,128)S(1)}, u32[]{:S(2)}, u32[]{:S(2)}) collective-permute-start(f32[2,4096]{1,0:T(2,128)S(1)} %add_add_fusion), channel_id=1, source_target_pairs={{0,32},{32,0},{64,96},{96,64},{128,160},{160,128},{192,224},{224,1... | collective-permute-start | bytes 98312 | tf_op jit(solution)/shard_map/ppermute | solution.py:107
  65.1 7.1 %collective-permute-start.6 = (f32[2,4096]{1,0:T(2,128)S(1)}, f32[2,4096]{1,0:T(2,128)S(1)}, u32[]{:S(2)}, u32[]{:S(2)}) collective-permute-start(f32[2,4096]{1,0:T(2,128)S(1)} %add.546), channel_id=1, source_target_pairs={{0,64},{32,96},{64,0},{96,32},{128,192},{160,224},{192,128},{224,1... | collective-permute-start | bytes 98312 | tf_op jit(solution)/shard_map/ppermute | solution.py:107
  72.2 5.8 %collective-permute-start.7 = (f32[2,4096]{1,0:T(2,128)S(1)}, f32[2,4096]{1,0:T(2,128)S(1)}, u32[]{:S(2)}, u32[]{:S(2)}) collective-permute-start(f32[2,4096]{1,0:T(2,128)S(1)} %add.547), channel_id=1, source_target_pairs={{0,128},{32,160},{64,192},{96,224},{128,0},{160,32},{192,64},{224,... | collective-permute-start | bytes 98312 | tf_op jit(solution)/shard_map/ppermute | solution.py:107
  78.0 7.1 %collective-permute-start.8 = (f32[2,4096]{1,0:T(2,128)S(1)}, f32[2,4096]{1,0:T(2,128)S(1)}, u32[]{:S(2)}, u32[]{:S(2)}) collective-permute-start(f32[2,4096]{1,0:T(2,128)S(1)} %add.548), channel_id=1, source_target_pairs={{0,256},{32,288},{64,320},{96,352},{128,384},{160,416},{192,448},{... | collective-permute-start | bytes 98312 | tf_op jit(solution)/shard_map/ppermute | solution.py:107
  85.1 10.0 %collective-permute-start.9 = (f32[2,4096]{1,0:T(2,128)S(1)}, f32[2,4096]{1,0:T(2,128)S(1)}, u32[]{:S(2)}, u32[]{:S(2)}) collective-permute-start(f32[2,4096]{1,0:T(2,128)S(1)} %add.549), channel_id=1, source_target_pairs={{0,512},{32,544},{64,576},{96,608},{128,640},{160,672},{192,704},{... | collective-permute-start | bytes 98312 | tf_op jit(solution)/shard_map/ppermute | solution.py:107
  95.1 1.7 %copy-start = (bf16[16,1024]{1,0:T(8,128)(2,1)S(1)}, bf16[16,1024]{1,0:T(8,128)(2,1)}, u32[]{:S(2)}) copy-start(bf16[16,1024]{1,0:T(8,128)(2,1)} %param.7) | copy-start | bytes 98308
  100.5 7.3 %collective-permute-start.10 = (f32[16,1024]{1,0:T(8,128)S(1)}, f32[16,1024]{1,0:T(8,128)S(1)}, u32[]{:S(2)}, u32[]{:S(2)}) collective-permute-start(f32[16,1024]{1,0:T(8,128)S(1)} %pad_maximum_fusion.1), channel_id=1, source_target_pairs={{0,2},{1,3},{2,0},{3,1},{4,6},{5,7},{6,4},{7,5},{8,10},{9,11},{10,... | collective-permute-start | bytes 196616 | tf_op jit(solution)/shard_map/ppermute | solution.py:38
  107.9 6.7 %collective-permute-start.11 = (f32[16,512]{1,0:T(8,128)S(1)}, f32[16,512]{1,0:T(8,128)S(1)}, u32[]{:S(2)}, u32[]{:S(2)}) collective-permute-start(f32[16,512]{1,0:T(8,128)S(1)} %constant_dynamic-slice_fusion.3), channel_id=1, source_target_pairs={{0,4},{1,5},{2,6},{3,7},{4,0},{5,1},{6,2},{7,3},{8,12},{9,13},{10,... | collective-permute-start | bytes 98312 | tf_op jit(solution)/shard_map/ppermute | solution.py:46
  114.6 9.5 %collective-permute-start.12 = (f32[16,256]{1,0:T(8,128)S(1)}, f32[16,256]{1,0:T(8,128)S(1)}, u32[]{:S(2)}, u32[]{:S(2)}) collective-permute-start(f32[16,256]{1,0:T(8,128)S(1)} %constant_dynamic-slice_fusion.2), channel_id=1, source_target_pairs={{0,8},{1,9},{2,10},{3,11},{4,12},{5,13},{6,14},{7,15},{8,0},{9,1},... | collective-permute-start | bytes 49160 | tf_op jit(solution)/shard_map/ppermute | solution.py:46
  124.2 9.4 %collective-permute-start.13 = (f32[16,128]{1,0:T(8,128)S(1)}, f32[16,128]{1,0:T(8,128)S(1)}, u32[]{:S(2)}, u32[]{:S(2)}) collective-permute-start(f32[16,128]{1,0:T(8,128)S(1)} %constant_dynamic-slice_fusion.1), channel_id=1, source_target_pairs={{0,16},{1,17},{2,18},{3,19},{4,20},{5,21},{6,22},{7,23},{8,24},{9,... | collective-permute-start | bytes 24584 | tf_op jit(solution)/shard_map/ppermute | solution.py:46

commit v11 on v9

--- a/solution.py
+++ b/solution.py
@@ -2,13 +2,6 @@
 import jax.numpy as jnp
 from jax import lax
 from jax.sharding import PartitionSpec as P
-
-
-def split_parts(cauchy):
-    upper = cauchy.astype(jnp.bfloat16)
-    upper = lax.optimization_barrier(upper)
-    lower = (cauchy - upper.astype(jnp.float32)).astype(jnp.bfloat16)
-    return (upper, lower)
 
 
 def cauchy_tile_t(pole_row, live_row, value_at, scale_at):
@@ -109,15 +102,15 @@
     blocks = value_data.reshape(2, col_total, -1)
     value_data = jnp.concatenate([blocks[:, b] for b in bit_reversed(col_total)], 1)
 
+    basis_wide = basis.astype(jnp.float32)
+
     def compute_range(inputs, offset, width):
         pole_at, live_at, value_data = inputs
         parts = []
         for start in range(0, width, chunk):
             values = lax.dynamic_slice_in_dim(value_data, offset + start, chunk, 1)
-            upper, lower = split_parts(cauchy_tile_t(pole_at, live_at, values[0], values[1]))
-            first_term = lax.dot_general(basis, upper, contract, preferred_element_type=jnp.float32)
-            second_term = lax.dot_general(basis, lower, contract, preferred_element_type=jnp.float32)
-            parts.append(first_term + second_term)
+            cauchy = cauchy_tile_t(pole_at, live_at, values[0], values[1])
+            parts.append(lax.dot_general(basis_wide, cauchy, contract, precision=lax.Precision.HIGH, preferred_element_type=jnp.float32))
         return jnp.concatenate(parts, 1)
 
     summed = reduce_by_halves(compute_range, value_data.shape[1], "col", (pole_at, live_at, value_data))

time: 133 us -> 128 us (0.962)
  other arithmetic: 7.35 us -> 2.85 us
    convert_element_type x2 -> x0, other arithmetic: 3.12 us -> none  [split_parts(): upper = cauchy.astype(jnp.bfloat16)]
    dot_general x16 -> x8, matrix products: 8.84 us -> 7.71 us  [compute_range(): lax.dot_general(basis_wide, cauchy, contract, precision=lax.Precision.HIG...]
  transfers between devices with their start and end apart: 15 -> 15, of which waited for: 13 -> 13; matrix products, arithmetic and copies ran while one was open for 11% -> 9% of each run, Pallas kernels for 0% -> 0%
where the time goes in v11:
time: 128 us; the launch traced here: 127 us
  starting transfers between devices  68.4 us (53%)
  waiting for transfers between devices  36.8 us (29%)
  matrix products  15.4 us (12%)
  other arithmetic  2.85 us (2%)
  local copies, waits for them, and re-layouts  2.06 us (2%)
    ppermute x5, starting transfers between devices, per_device(): lax.ppermute(held, 'col', perm=[(i, i ^ step) for i in range(col_total)])  29.5 us
    ppermute x4, waiting for transfers between devices, reduce_by_halves(): lax.ppermute(sent, axis, perm=[(i, i ^ step) for i in range(size)])  15.9 us
    ppermute x5, starting transfers between devices, per_device(): lax.ppermute(looked, 'row', perm=[(i, i ^ step) for i in range(row_total)])  14.2 us
    ppermute x5, waiting for transfers between devices, per_device(): lax.ppermute(looked, 'row', perm=[(i, i ^ step) for i in range(row_total)])  13.5 us
    ppermute x1, starting transfers between devices, reduce_by_halves(): got = lax.ppermute(sent, axis, perm=[(i, i ^ step) for i in range(size)])  12.6 us
    ppermute x4, starting transfers between devices, reduce_by_halves(): lax.ppermute(sent, axis, perm=[(i, i ^ step) for i in range(size)])  12.1 us
    dot_general x24, matrix products, look_up(): lax.dot_general(table, hits.astype(jnp.bfloat16), (((1,), (1,)), ((), ())...  7.72 us
    dot_general x8, matrix products, compute_range(): lax.dot_general(basis_wide, cauchy, contract, precision=lax.Precision.HIG...  7.71 us
  transfers between devices with their start and end apart: 15, of which 13 were waited for; matrix products, arithmetic and copies ran while one was open for 9% of the time, Pallas kernels for 0%

profile of v11, /device:TPU:1, one launch (start us, length us, event | category | flops | bytes accessed | tf_op | source)
XLA Modules:
  0.0 126.5 jit_solution(15792508526064064092)
XLA Ops:
  1.5 16.1 %collective-permute-start = (f32[2,192]{1,0:T(2,128)S(1)}, f32[2,192]{1,0:T(2,128)S(1)}, u32[]{:S(2)}, u32[]{:S(2)}) collective-permute-start(f32[2,192]{1,0:T(2,128)S(1)} %maximum_maximum_fusion), channel_id=1, source_target_pairs={{0,1},{1,0},{2,3},{3,2},{4,5},{5,4},{6,7},{7,6},{8,9},{9,8},{10,11... | collective-permute-start | bytes 4616 | tf_op jit(solution)/shard_map/ppermute | solution.py:83
  27.2 2.1 %collective-permute-done.2 = f32[2,768]{1,0:T(2,128)S(1)} collective-permute-done((f32[2,768]{1,0:T(2,128)S(1)}, f32[2,768]{1,0:T(2,128)S(1)}, u32[]{:S(2)}, u32[]{:S(2)}) %collective-permute-start.2) | collective-permute-done | bytes 6176 | tf_op jit(solution)/shard_map/ppermute | solution.py:83
  29.3 4.4 %collective-permute-start.3 = (f32[2,1536]{1,0:T(2,128)S(1)}, f32[2,1536]{1,0:T(2,128)S(1)}, u32[]{:S(2)}, u32[]{:S(2)}) collective-permute-start(f32[2,1536]{1,0:T(2,128)S(1)} %maximum_select_fusion.4), channel_id=1, source_target_pairs={{0,8},{1,9},{2,10},{3,11},{4,12},{5,13},{6,14},{7,15},{8,0},{9,1},... | collective-permute-start | bytes 36872 | tf_op jit(solution)/shard_map/ppermute | solution.py:83
  35.0 2.6 %collective-permute-done.3 = f32[2,1536]{1,0:T(2,128)S(1)} collective-permute-done((f32[2,1536]{1,0:T(2,128)S(1)}, f32[2,1536]{1,0:T(2,128)S(1)}, u32[]{:S(2)}, u32[]{:S(2)}) %collective-permute-start.3) | collective-permute-done | bytes 12320 | tf_op jit(solution)/shard_map/ppermute | solution.py:83
  37.7 5.3 %collective-permute-start.4 = (f32[2,3072]{1,0:T(2,128)S(1)}, f32[2,3072]{1,0:T(2,128)S(1)}, u32[]{:S(2)}, u32[]{:S(2)}) collective-permute-start(f32[2,3072]{1,0:T(2,128)S(1)} %maximum_select_fusion.2), channel_id=1, source_target_pairs={{0,16},{1,17},{2,18},{3,19},{4,20},{5,21},{6,22},{7,23},{8,24},{9,... | collective-permute-start | bytes 73736 | tf_op jit(solution)/shard_map/ppermute | solution.py:83
  49.0 1.9 %collective-permute-start.5 = (f32[2,2048]{1,0:T(2,128)S(1)}, f32[2,2048]{1,0:T(2,128)S(1)}, u32[]{:S(2)}, u32[]{:S(2)}) collective-permute-start(f32[2,2048]{1,0:T(2,128)S(1)} %fusion.139), channel_id=1, source_target_pairs={{0,32},{32,0},{64,96},{96,64},{128,160},{160,128},{192,224},{224,1... | collective-permute-start | bytes 49160 | tf_op jit(solution)/shard_map/ppermute | solution.py:92
  51.2 2.2 %collective-permute-done.5 = f32[2,2048]{1,0:T(2,128)S(1)} collective-permute-done((f32[2,2048]{1,0:T(2,128)S(1)}, f32[2,2048]{1,0:T(2,128)S(1)}, u32[]{:S(2)}, u32[]{:S(2)}) %collective-permute-start.5) | collective-permute-done | bytes 16416 | tf_op jit(solution)/shard_map/ppermute | solution.py:92
  53.5 1.9 %collective-permute-start.6 = (f32[2,2048]{1,0:T(2,128)S(1)}, f32[2,2048]{1,0:T(2,128)S(1)}, u32[]{:S(2)}, u32[]{:S(2)}) collective-permute-start(f32[2,2048]{1,0:T(2,128)S(1)} %add.378), channel_id=1, source_target_pairs={{0,64},{32,96},{64,0},{96,32},{128,192},{160,224},{192,128},{224,1... | collective-permute-start | bytes 49160 | tf_op jit(solution)/shard_map/ppermute | solution.py:92
  55.4 3.5 %collective-permute-done.6 = f32[2,2048]{1,0:T(2,128)S(1)} collective-permute-done((f32[2,2048]{1,0:T(2,128)S(1)}, f32[2,2048]{1,0:T(2,128)S(1)}, u32[]{:S(2)}, u32[]{:S(2)}) %collective-permute-start.6) | collective-permute-done | bytes 16416 | tf_op jit(solution)/shard_map/ppermute | solution.py:92
  58.9 1.9 %collective-permute-start.7 = (f32[2,2048]{1,0:T(2,128)S(1)}, f32[2,2048]{1,0:T(2,128)S(1)}, u32[]{:S(2)}, u32[]{:S(2)}) collective-permute-start(f32[2,2048]{1,0:T(2,128)S(1)} %add.379), channel_id=1, source_target_pairs={{0,128},{32,160},{64,192},{96,224},{128,0},{160,32},{192,64},{224,... | collective-permute-start | bytes 49160 | tf_op jit(solution)/shard_map/ppermute | solution.py:92
  60.9 2.5 %collective-permute-done.7 = f32[2,2048]{1,0:T(2,128)S(1)} collective-permute-done((f32[2,2048]{1,0:T(2,128)S(1)}, f32[2,2048]{1,0:T(2,128)S(1)}, u32[]{:S(2)}, u32[]{:S(2)}) %collective-permute-start.7) | collective-permute-done | bytes 16416 | tf_op jit(solution)/shard_map/ppermute | solution.py:92
  63.4 2.6 %collective-permute-start.8 = (f32[2,2048]{1,0:T(2,128)S(1)}, f32[2,2048]{1,0:T(2,128)S(1)}, u32[]{:S(2)}, u32[]{:S(2)}) collective-permute-start(f32[2,2048]{1,0:T(2,128)S(1)} %add.380), channel_id=1, source_target_pairs={{0,256},{32,288},{64,320},{96,352},{128,384},{160,416},{192,448},{... | collective-permute-start | bytes 49160 | tf_op jit(solution)/shard_map/ppermute | solution.py:92
  66.0 2.8 %collective-permute-done.8 = f32[2,2048]{1,0:T(2,128)S(1)} collective-permute-done((f32[2,2048]{1,0:T(2,128)S(1)}, f32[2,2048]{1,0:T(2,128)S(1)}, u32[]{:S(2)}, u32[]{:S(2)}) %collective-permute-start.8) | collective-permute-done | bytes 16416 | tf_op jit(solution)/shard_map/ppermute | solution.py:92
  68.8 5.8 %collective-permute-start.9 = (f32[2,2048]{1,0:T(2,128)S(1)}, f32[2,2048]{1,0:T(2,128)S(1)}, u32[]{:S(2)}, u32[]{:S(2)}) collective-permute-start(f32[2,2048]{1,0:T(2,128)S(1)} %add.381), channel_id=1, source_target_pairs={{0,512},{32,544},{64,576},{96,608},{128,640},{160,672},{192,704},{... | collective-permute-start | bytes 49160 | tf_op jit(solution)/shard_map/ppermute | solution.py:92
  74.8 2.4 %collective-permute-done.9 = f32[2,2048]{1,0:T(2,128)S(1)} collective-permute-done((f32[2,2048]{1,0:T(2,128)S(1)}, f32[2,2048]{1,0:T(2,128)S(1)}, u32[]{:S(2)}, u32[]{:S(2)}) %collective-permute-start.9) | collective-permute-done | bytes 16416 | tf_op jit(solution)/shard_map/ppermute | solution.py:92
  81.1 12.6 %collective-permute-start.10 = (f32[16,2048]{1,0:T(8,128)S(1)}, f32[16,2048]{1,0:T(8,128)S(1)}, u32[]{:S(2)}, u32[]{:S(2)}) collective-permute-start(f32[16,2048]{1,0:T(8,128)S(1)} %pad_maximum_fusion), channel_id=1, source_target_pairs={{0,1},{1,0},{2,3},{3,2},{4,5},{5,4},{6,7},{7,6},{8,9},{9,8},{10,11... | collective-permute-start | bytes 393224 | tf_op jit(solution)/shard_map/ppermute | solution.py:32
  97.7 1.9 %collective-permute-start.11 = (f32[16,1024]{1,0:T(8,128)S(1)}, f32[16,1024]{1,0:T(8,128)S(1)}, u32[]{:S(2)}, u32[]{:S(2)}) collective-permute-start(f32[16,1024]{1,0:T(8,128)S(1)} %constant_dynamic-slice_fusion.4), channel_id=1, source_target_pairs={{0,2},{1,3},{2,0},{3,1},{4,6},{5,7},{6,4},{7,5},{8,10},{9,11},{10,... | collective-permute-start | bytes 196616 | tf_op jit(solution)/shard_map/ppermute | solution.py:40
  99.7 3.7 %collective-permute-done.11 = f32[16,1024]{1,0:T(8,128)S(1)} collective-permute-done((f32[16,1024]{1,0:T(8,128)S(1)}, f32[16,1024]{1,0:T(8,128)S(1)}, u32[]{:S(2)}, u32[]{:S(2)}) %collective-permute-start.11) | collective-permute-done | bytes 65568 | tf_op jit(solution)/shard_map/ppermute | solution.py:40
  103.4 1.9 %collective-permute-start.12 = (f32[16,512]{1,0:T(8,128)S(1)}, f32[16,512]{1,0:T(8,128)S(1)}, u32[]{:S(2)}, u32[]{:S(2)}) collective-permute-start(f32[16,512]{1,0:T(8,128)S(1)} %constant_dynamic-slice_fusion.3), channel_id=1, source_target_pairs={{0,4},{1,5},{2,6},{3,7},{4,0},{5,1},{6,2},{7,3},{8,12},{9,13},{10,... | collective-permute-start | bytes 98312 | tf_op jit(solution)/shard_map/ppermute | solution.py:40
  105.3 3.9 %collective-permute-done.12 = f32[16,512]{1,0:T(8,128)S(1)} collective-permute-done((f32[16,512]{1,0:T(8,128)S(1)}, f32[16,512]{1,0:T(8,128)S(1)}, u32[]{:S(2)}, u32[]{:S(2)}) %collective-permute-start.12) | collective-permute-done | bytes 32800 | tf_op jit(solution)/shard_map/ppermute | solution.py:40
  109.2 4.1 %collective-permute-start.13 = (f32[16,256]{1,0:T(8,128)S(1)}, f32[16,256]{1,0:T(8,128)S(1)}, u32[]{:S(2)}, u32[]{:S(2)}) collective-permute-start(f32[16,256]{1,0:T(8,128)S(1)} %constant_dynamic-slice_fusion.2), channel_id=1, source_target_pairs={{0,8},{1,9},{2,10},{3,11},{4,12},{5,13},{6,14},{7,15},{8,0},{9,1},... | collective-permute-start | bytes 49160 | tf_op jit(solution)/shard_map/ppermute | solution.py:40
  113.4 4.2 %collective-permute-done.13 = f32[16,256]{1,0:T(8,128)S(1)} collective-permute-done((f32[16,256]{1,0:T(8,128)S(1)}, f32[16,256]{1,0:T(8,128)S(1)}, u32[]{:S(2)}, u32[]{:S(2)}) %collective-permute-start.13) | collective-permute-done | bytes 16416 | tf_op jit(solution)/shard_map/ppermute | solution.py:40
  117.6 4.1 %collective-permute-start.14 = (f32[16,128]{1,0:T(8,128)S(1)}, f32[16,128]{1,0:T(8,128)S(1)}, u32[]{:S(2)}, u32[]{:S(2)}) collective-permute-start(f32[16,128]{1,0:T(8,128)S(1)} %constant_dynamic-slice_fusion.1), channel_id=1, source_target_pairs={{0,16},{1,17},{2,18},{3,19},{4,20},{5,21},{6,22},{7,23},{8,24},{9,... | collective-permute-start | bytes 24584 | tf_op jit(solution)/shard_map/ppermute | solution.py:40
  121.8 4.1 %collective-permute-done.14 = f32[16,128]{1,0:T(8,128)S(1)} collective-permute-done((f32[16,128]{1,0:T(8,128)S(1)}, f32[16,128]{1,0:T(8,128)S(1)}, u32[]{:S(2)}, u32[]{:S(2)}) %collective-permute-start.14) | collective-permute-done | bytes 8224 | tf_op jit(solution)/shard_map/ppermute | solution.py:40
  (177 shorter events, 26.8 us)
Async XLA Ops:
  0.0 77.2 %copy-start = (bf16[16,1024]{1,0:T(8,128)(2,1)S(1)}, bf16[16,1024]{1,0:T(8,128)(2,1)}, u32[]{:S(2)}) copy-start(bf16[16,1024]{1,0:T(8,128)(2,1)} %param.7) | copy-start | bytes 98308
  0.0 17.7 %copy-start.2 = (f32[128]{0:T(128)S(1)}, f32[128]{0:T(128)}, u32[]{:S(2)}) copy-start(f32[128]{0:T(128)} %param.13) | copy-start | bytes 1540
  0.0 17.7 %copy-start.3 = (f32[128]{0:T(128)S(1)}, f32[128]{0:T(128)}, u32[]{:S(2)}) copy-start(f32[128]{0:T(128)} %param.12) | copy-start | bytes 1540
  0.0 17.7 %copy-start.4 = (f32[64]{0:T(128)S(1)}, f32[64]{0:T(128)}, u32[]{:S(2)}) copy-start(f32[64]{0:T(128)} %param.9) | copy-start | bytes 772
  1.5 18.1 %collective-permute-start = (f32[2,192]{1,0:T(2,128)S(1)}, f32[2,192]{1,0:T(2,128)S(1)}, u32[]{:S(2)}, u32[]{:S(2)}) collective-permute-start(f32[2,192]{1,0:T(2,128)S(1)} %maximum_maximum_fusion), channel_id=1, source_target_pairs={{0,1},{1,0},{2,3},{3,2},{4,5},{5,4},{6,7},{7,6},{8,9},{9,8},{10,11... | collective-permute-start | bytes 4616 | tf_op jit(solution)/shard_map/ppermute | solution.py:83
  17.6 0.7 copy-start.1
  19.7 4.3 %collective-permute-start.1 = (f32[2,384]{1,0:T(2,128)S(1)}, f32[2,384]{1,0:T(2,128)S(1)}, u32[]{:S(2)}, u32[]{:S(2)}) collective-permute-start(f32[2,384]{1,0:T(2,128)S(1)} %maximum_select_fusion.7), channel_id=1, source_target_pairs={{0,2},{1,3},{2,0},{3,1},{4,6},{5,7},{6,4},{7,5},{8,10},{9,11},{10,... | collective-permute-start | bytes 9224 | tf_op jit(solution)/shard_map/ppermute | solution.py:83
  24.0 5.3 %collective-permute-start.2 = (f32[2,768]{1,0:T(2,128)S(1)}, f32[2,768]{1,0:T(2,128)S(1)}, u32[]{:S(2)}, u32[]{:S(2)}) collective-permute-start(f32[2,768]{1,0:T(2,128)S(1)} %maximum_select_fusion.6), channel_id=1, source_target_pairs={{0,4},{1,5},{2,6},{3,7},{4,0},{5,1},{6,2},{7,3},{8,12},{9,13},{10,... | collective-permute-start | bytes 18440 | tf_op jit(solution)/shard_map/ppermute | solution.py:83
  29.3 8.3 %collective-permute-start.3 = (f32[2,1536]{1,0:T(2,128)S(1)}, f32[2,1536]{1,0:T(2,128)S(1)}, u32[]{:S(2)}, u32[]{:S(2)}) collective-permute-start(f32[2,1536]{1,0:T(2,128)S(1)} %maximum_select_fusion.4), channel_id=1, source_target_pairs={{0,8},{1,9},{2,10},{3,11},{4,12},{5,13},{6,14},{7,15},{8,0},{9,1},... | collective-permute-start | bytes 36872 | tf_op jit(solution)/shard_map/ppermute | solution.py:83
  37.7 8.5 %collective-permute-start.4 = (f32[2,3072]{1,0:T(2,128)S(1)}, f32[2,3072]{1,0:T(2,128)S(1)}, u32[]{:S(2)}, u32[]{:S(2)}) collective-permute-start(f32[2,3072]{1,0:T(2,128)S(1)} %maximum_select_fusion.2), channel_id=1, source_target_pairs={{0,16},{1,17},{2,18},{3,19},{4,20},{5,21},{6,22},{7,23},{8,24},{9,... | collective-permute-start | bytes 73736 | tf_op jit(solution)/shard_map/ppermute | solution.py:83
  49.0 4.5 %collective-permute-start.5 = (f32[2,2048]{1,0:T(2,128)S(1)}, f32[2,2048]{1,0:T(2,128)S(1)}, u32[]{:S(2)}, u32[]{:S(2)}) collective-permute-start(f32[2,2048]{1,0:T(2,128)S(1)} %fusion.139), channel_id=1, source_target_pairs={{0,32},{32,0},{64,96},{96,64},{128,160},{160,128},{192,224},{224,1... | collective-permute-start | bytes 49160 | tf_op jit(solution)/shard_map/ppermute | solution.py:92
  53.5 5.4 %collective-permute-start.6 = (f32[2,2048]{1,0:T(2,128)S(1)}, f32[2,2048]{1,0:T(2,128)S(1)}, u32[]{:S(2)}, u32[]{:S(2)}) collective-permute-start(f32[2,2048]{1,0:T(2,128)S(1)} %add.378), channel_id=1, source_target_pairs={{0,64},{32,96},{64,0},{96,32},{128,192},{160,224},{192,128},{224,1... | collective-permute-start | bytes 49160 | tf_op jit(solution)/shard_map/ppermute | solution.py:92
  58.9 4.5 %collective-permute-start.7 = (f32[2,2048]{1,0:T(2,128)S(1)}, f32[2,2048]{1,0:T(2,128)S(1)}, u32[]{:S(2)}, u32[]{:S(2)}) collective-permute-start(f32[2,2048]{1,0:T(2,128)S(1)} %add.379), channel_id=1, source_target_pairs={{0,128},{32,160},{64,192},{96,224},{128,0},{160,32},{192,64},{224,... | collective-permute-start | bytes 49160 | tf_op jit(solution)/shard_map/ppermute | solution.py:92
  63.4 5.4 %collective-permute-start.8 = (f32[2,2048]{1,0:T(2,128)S(1)}, f32[2,2048]{1,0:T(2,128)S(1)}, u32[]{:S(2)}, u32[]{:S(2)}) collective-permute-start(f32[2,2048]{1,0:T(2,128)S(1)} %add.380), channel_id=1, source_target_pairs={{0,256},{32,288},{64,320},{96,352},{128,384},{160,416},{192,448},{... | collective-permute-start | bytes 49160 | tf_op jit(solution)/shard_map/ppermute | solution.py:92
  68.8 8.4 %collective-permute-start.9 = (f32[2,2048]{1,0:T(2,128)S(1)}, f32[2,2048]{1,0:T(2,128)S(1)}, u32[]{:S(2)}, u32[]{:S(2)}) collective-permute-start(f32[2,2048]{1,0:T(2,128)S(1)} %add.381), channel_id=1, source_target_pairs={{0,512},{32,544},{64,576},{96,608},{128,640},{160,672},{192,704},{... | collective-permute-start | bytes 49160 | tf_op jit(solution)/shard_map/ppermute | solution.py:92
  81.1 16.6 %collective-permute-start.10 = (f32[16,2048]{1,0:T(8,128)S(1)}, f32[16,2048]{1,0:T(8,128)S(1)}, u32[]{:S(2)}, u32[]{:S(2)}) collective-permute-start(f32[16,2048]{1,0:T(8,128)S(1)} %pad_maximum_fusion), channel_id=1, source_target_pairs={{0,1},{1,0},{2,3},{3,2},{4,5},{5,4},{6,7},{7,6},{8,9},{9,8},{10,11... | collective-permute-start | bytes 393224 | tf_op jit(solution)/shard_map/ppermute | solution.py:32
  97.7 5.6 %collective-permute-start.11 = (f32[16,1024]{1,0:T(8,128)S(1)}, f32[16,1024]{1,0:T(8,128)S(1)}, u32[]{:S(2)}, u32[]{:S(2)}) collective-permute-start(f32[16,1024]{1,0:T(8,128)S(1)} %constant_dynamic-slice_fusion.4), channel_id=1, source_target_pairs={{0,2},{1,3},{2,0},{3,1},{4,6},{5,7},{6,4},{7,5},{8,10},{9,11},{10,... | collective-permute-start | bytes 196616 | tf_op jit(solution)/shard_map/ppermute | solution.py:40
  103.4 5.8 %collective-permute-start.12 = (f32[16,512]{1,0:T(8,128)S(1)}, f32[16,512]{1,0:T(8,128)S(1)}, u32[]{:S(2)}, u32[]{:S(2)}) collective-permute-start(f32[16,512]{1,0:T(8,128)S(1)} %constant_dynamic-slice_fusion.3), channel_id=1, source_target_pairs={{0,4},{1,5},{2,6},{3,7},{4,0},{5,1},{6,2},{7,3},{8,12},{9,13},{10,... | collective-permute-start | bytes 98312 | tf_op jit(solution)/shard_map/ppermute | solution.py:40
  109.2 8.4 %collective-permute-start.13 = (f32[16,256]{1,0:T(8,128)S(1)}, f32[16,256]{1,0:T(8,128)S(1)}, u32[]{:S(2)}, u32[]{:S(2)}) collective-permute-start(f32[16,256]{1,0:T(8,128)S(1)} %constant_dynamic-slice_fusion.2), channel_id=1, source_target_pairs={{0,8},{1,9},{2,10},{3,11},{4,12},{5,13},{6,14},{7,15},{8,0},{9,1},... | collective-permute-start | bytes 49160 | tf_op jit(solution)/shard_map/ppermute | solution.py:40
  117.6 8.3 %collective-permute-start.14 = (f32[16,128]{1,0:T(8,128)S(1)}, f32[16,128]{1,0:T(8,128)S(1)}, u32[]{:S(2)}, u32[]{:S(2)}) collective-permute-start(f32[16,128]{1,0:T(8,128)S(1)} %constant_dynamic-slice_fusion.1), channel_id=1, source_target_pairs={{0,16},{1,17},{2,18},{3,19},{4,20},{5,21},{6,22},{7,23},{8,24},{9,... | collective-permute-start | bytes 24584 | tf_op jit(solution)/shard_map/ppermute | solution.py:40

commit v12 on v11

--- a/solution.py
+++ b/solution.py
@@ -87,16 +87,19 @@
         step *= 2
     value_data = held.reshape(2, col_total, own_len)[:, :, pole_dev:].reshape(2, -1)
     row_total = lax.axis_size("row")
+    half_rows = row_total // 2
+    child_id = lax.axis_index("row") // half_rows
+    own_cols = position.shape[1]
+    mine = lax.dynamic_slice_in_dim(looked, child_id * own_cols, own_cols, 1)
+    theirs = lax.dynamic_slice_in_dim(looked, (1 - child_id) * own_cols, own_cols, 1)
+    looked = mine + lax.ppermute(theirs, "row", perm=[(i, i ^ half_rows) for i in range(row_total)])
     step = 1
-    while step < row_total:
+    while step < half_rows:
         looked = looked + lax.ppermute(looked, "row", perm=[(i, i ^ step) for i in range(row_total)])
         step *= 2
-    child_id = lax.axis_index("row") // (row_total // 2)
-    own_cols = position.shape[1]
-    own_poles = lax.dynamic_slice_in_dim(looked, child_id * own_cols, own_cols, 1)
-    pole_at = own_poles[0]
-    live_at = own_poles[1]
-    chunk = 512
+    pole_at = looked[0]
+    live_at = looked[1]
+    chunk = 1024
     contract = (((1,), (1,)), ((), ()))
 
     blocks = value_data.reshape(2, col_total, -1)

time: 128 us -> 127 us (level)
    ppermute x5 -> x4, starting transfers between devices: 14.2 us -> 8.36 us  [per_device(): lax.ppermute(looked, 'row', perm=[(i, i ^ step) for i in range(row_total)])]
    ppermute x0 -> x1, starting transfers between devices: none -> 5.71 us  [per_device(): lax.ppermute(theirs, 'row', perm=[(i, i ^ half_rows) for i in range(row_t...]
    ppermute x5 -> x4, waiting for transfers between devices: 13.5 us -> 11.2 us  [per_device(): lax.ppermute(looked, 'row', perm=[(i, i ^ step) for i in range(row_total)])]
    ppermute x0 -> x1, waiting for transfers between devices: none -> 2.24 us  [per_device(): lax.ppermute(theirs, 'row', perm=[(i, i ^ half_rows) for i in range(row_t...]
    dot_general x8 -> x4, matrix products: 7.71 us -> 7.07 us  [compute_range(): lax.dot_general(basis_wide, cauchy, contract, precision=lax.Precision.HIG...]
  transfers between devices with their start and end apart: 15 -> 15, of which waited for: 13 -> 13; matrix products, arithmetic and copies ran while one was open for 9% -> 8% of each run, Pallas kernels for 0% -> 0%
where the time goes in v12:
time: 127 us; the launch traced here: 125 us
  starting transfers between devices  68 us (54%)
  waiting for transfers between devices  36.7 us (29%)
  matrix products  14.8 us (12%)
  other arithmetic  2.83 us (2%)
  local copies, waits for them, and re-layouts  2.05 us (2%)
    ppermute x5, starting transfers between devices, per_device(): lax.ppermute(held, 'col', perm=[(i, i ^ step) for i in range(col_total)])  29.5 us
    ppermute x4, waiting for transfers between devices, reduce_by_halves(): lax.ppermute(sent, axis, perm=[(i, i ^ step) for i in range(size)])  15.9 us
    ppermute x1, starting transfers between devices, reduce_by_halves(): got = lax.ppermute(sent, axis, perm=[(i, i ^ step) for i in range(size)])  12.3 us
    ppermute x4, starting transfers between devices, reduce_by_halves(): lax.ppermute(sent, axis, perm=[(i, i ^ step) for i in range(size)])  12.1 us
    ppermute x4, waiting for transfers between devices, per_device(): lax.ppermute(looked, 'row', perm=[(i, i ^ step) for i in range(row_total)])  11.2 us
    ppermute x4, starting transfers between devices, per_device(): lax.ppermute(looked, 'row', perm=[(i, i ^ step) for i in range(row_total)])  8.36 us
    dot_general x24, matrix products, look_up(): lax.dot_general(table, hits.astype(jnp.bfloat16), (((1,), (1,)), ((), ())...  7.72 us
    ppermute x5, waiting for transfers between devices, per_device(): lax.ppermute(held, 'col', perm=[(i, i ^ step) for i in range(col_total)])  7.37 us
  transfers between devices with their start and end apart: 15, of which 13 were waited for; matrix products, arithmetic and copies ran while one was open for 8% of the time, Pallas kernels for 0%

profile of v12, /device:TPU:1, one launch (start us, length us, event | category | flops | bytes accessed | tf_op | source)
XLA Modules:
  0.0 125.4 jit_solution(16263417882070658787)
XLA Ops:
  1.5 16.1 %collective-permute-start = (f32[2,192]{1,0:T(2,128)S(1)}, f32[2,192]{1,0:T(2,128)S(1)}, u32[]{:S(2)}, u32[]{:S(2)}) collective-permute-start(f32[2,192]{1,0:T(2,128)S(1)} %maximum_maximum_fusion), channel_id=1, source_target_pairs={{0,1},{1,0},{2,3},{3,2},{4,5},{5,4},{6,7},{7,6},{8,9},{9,8},{10,11... | collective-permute-start | bytes 4616 | tf_op jit(solution)/shard_map/ppermute | solution.py:83
  19.7 1.9 %collective-permute-start.1 = (f32[2,384]{1,0:T(2,128)S(1)}, f32[2,384]{1,0:T(2,128)S(1)}, u32[]{:S(2)}, u32[]{:S(2)}) collective-permute-start(f32[2,384]{1,0:T(2,128)S(1)} %maximum_select_fusion.7), channel_id=1, source_target_pairs={{0,2},{1,3},{2,0},{3,1},{4,6},{5,7},{6,4},{7,5},{8,10},{9,11},{10,... | collective-permute-start | bytes 9224 | tf_op jit(solution)/shard_map/ppermute | solution.py:83
  24.0 1.9 %collective-permute-start.2 = (f32[2,768]{1,0:T(2,128)S(1)}, f32[2,768]{1,0:T(2,128)S(1)}, u32[]{:S(2)}, u32[]{:S(2)}) collective-permute-start(f32[2,768]{1,0:T(2,128)S(1)} %maximum_select_fusion.6), channel_id=1, source_target_pairs={{0,4},{1,5},{2,6},{3,7},{4,0},{5,1},{6,2},{7,3},{8,12},{9,13},{10,... | collective-permute-start | bytes 18440 | tf_op jit(solution)/shard_map/ppermute | solution.py:83
  27.2 2.1 %collective-permute-done.2 = f32[2,768]{1,0:T(2,128)S(1)} collective-permute-done((f32[2,768]{1,0:T(2,128)S(1)}, f32[2,768]{1,0:T(2,128)S(1)}, u32[]{:S(2)}, u32[]{:S(2)}) %collective-permute-start.2) | collective-permute-done | bytes 6176 | tf_op jit(solution)/shard_map/ppermute | solution.py:83
  29.3 4.4 %collective-permute-start.3 = (f32[2,1536]{1,0:T(2,128)S(1)}, f32[2,1536]{1,0:T(2,128)S(1)}, u32[]{:S(2)}, u32[]{:S(2)}) collective-permute-start(f32[2,1536]{1,0:T(2,128)S(1)} %maximum_select_fusion.4), channel_id=1, source_target_pairs={{0,8},{1,9},{2,10},{3,11},{4,12},{5,13},{6,14},{7,15},{8,0},{9,1},... | collective-permute-start | bytes 36872 | tf_op jit(solution)/shard_map/ppermute | solution.py:83
  35.0 2.6 %collective-permute-done.3 = f32[2,1536]{1,0:T(2,128)S(1)} collective-permute-done((f32[2,1536]{1,0:T(2,128)S(1)}, f32[2,1536]{1,0:T(2,128)S(1)}, u32[]{:S(2)}, u32[]{:S(2)}) %collective-permute-start.3) | collective-permute-done | bytes 12320 | tf_op jit(solution)/shard_map/ppermute | solution.py:83
  37.7 5.3 %collective-permute-start.4 = (f32[2,3072]{1,0:T(2,128)S(1)}, f32[2,3072]{1,0:T(2,128)S(1)}, u32[]{:S(2)}, u32[]{:S(2)}) collective-permute-start(f32[2,3072]{1,0:T(2,128)S(1)} %maximum_select_fusion.2), channel_id=1, source_target_pairs={{0,16},{1,17},{2,18},{3,19},{4,20},{5,21},{6,22},{7,23},{8,24},{9,... | collective-permute-start | bytes 73736 | tf_op jit(solution)/shard_map/ppermute | solution.py:83
  49.0 5.7 %collective-permute-start.5 = (f32[2,1024]{1,0:T(2,128)S(1)}, f32[2,1024]{1,0:T(2,128)S(1)}, u32[]{:S(2)}, u32[]{:S(2)}) collective-permute-start(f32[2,1024]{1,0:T(2,128)S(1)} %constant_dynamic-slice_fusion.8), channel_id=1, source_target_pairs={{0,512},{32,544},{64,576},{96,608},{128,640},{160,672},{192,704},{... | collective-permute-start | bytes 24584 | tf_op jit(solution)/shard_map/ppermute | solution.py:95
  55.0 2.2 %collective-permute-done.5 = f32[2,1024]{1,0:T(2,128)S(1)} collective-permute-done((f32[2,1024]{1,0:T(2,128)S(1)}, f32[2,1024]{1,0:T(2,128)S(1)}, u32[]{:S(2)}, u32[]{:S(2)}) %collective-permute-start.5) | collective-permute-done | bytes 8224 | tf_op jit(solution)/shard_map/ppermute | solution.py:95
  57.3 1.9 %collective-permute-start.6 = (f32[2,1024]{1,0:T(2,128)S(1)}, f32[2,1024]{1,0:T(2,128)S(1)}, u32[]{:S(2)}, u32[]{:S(2)}) collective-permute-start(f32[2,1024]{1,0:T(2,128)S(1)} %dynamic-slice_add_fusion.3), channel_id=1, source_target_pairs={{0,32},{32,0},{64,96},{96,64},{128,160},{160,128},{192,224},{224,1... | collective-permute-start | bytes 24584 | tf_op jit(solution)/shard_map/ppermute | solution.py:98
  59.2 2.7 %collective-permute-done.6 = f32[2,1024]{1,0:T(2,128)S(1)} collective-permute-done((f32[2,1024]{1,0:T(2,128)S(1)}, f32[2,1024]{1,0:T(2,128)S(1)}, u32[]{:S(2)}, u32[]{:S(2)}) %collective-permute-start.6) | collective-permute-done | bytes 8224 | tf_op jit(solution)/shard_map/ppermute | solution.py:98
  63.9 3.4 %collective-permute-done.7 = f32[2,1024]{1,0:T(2,128)S(1)} collective-permute-done((f32[2,1024]{1,0:T(2,128)S(1)}, f32[2,1024]{1,0:T(2,128)S(1)}, u32[]{:S(2)}, u32[]{:S(2)}) %collective-permute-start.7) | collective-permute-done | bytes 8224 | tf_op jit(solution)/shard_map/ppermute | solution.py:98
  69.2 2.5 %collective-permute-done.8 = f32[2,1024]{1,0:T(2,128)S(1)} collective-permute-done((f32[2,1024]{1,0:T(2,128)S(1)}, f32[2,1024]{1,0:T(2,128)S(1)}, u32[]{:S(2)}, u32[]{:S(2)}) %collective-permute-start.8) | collective-permute-done | bytes 8224 | tf_op jit(solution)/shard_map/ppermute | solution.py:98
  71.6 2.6 %collective-permute-start.9 = (f32[2,1024]{1,0:T(2,128)S(1)}, f32[2,1024]{1,0:T(2,128)S(1)}, u32[]{:S(2)}, u32[]{:S(2)}) collective-permute-start(f32[2,1024]{1,0:T(2,128)S(1)} %add.354), channel_id=1, source_target_pairs={{0,256},{32,288},{64,320},{96,352},{128,384},{160,416},{192,448},{... | collective-permute-start | bytes 24584 | tf_op jit(solution)/shard_map/ppermute | solution.py:98
  74.4 2.6 %collective-permute-done.9 = f32[2,1024]{1,0:T(2,128)S(1)} collective-permute-done((f32[2,1024]{1,0:T(2,128)S(1)}, f32[2,1024]{1,0:T(2,128)S(1)}, u32[]{:S(2)}, u32[]{:S(2)}) %collective-permute-start.9) | collective-permute-done | bytes 8224 | tf_op jit(solution)/shard_map/ppermute | solution.py:98
  80.6 12.3 %collective-permute-start.10 = (f32[16,2048]{1,0:T(8,128)S(1)}, f32[16,2048]{1,0:T(8,128)S(1)}, u32[]{:S(2)}, u32[]{:S(2)}) collective-permute-start(f32[16,2048]{1,0:T(8,128)S(1)} %pad_maximum_fusion), channel_id=1, source_target_pairs={{0,1},{1,0},{2,3},{3,2},{4,5},{5,4},{6,7},{7,6},{8,9},{9,8},{10,11... | collective-permute-start | bytes 393224 | tf_op jit(solution)/shard_map/ppermute | solution.py:32
  96.6 1.9 %collective-permute-start.11 = (f32[16,1024]{1,0:T(8,128)S(1)}, f32[16,1024]{1,0:T(8,128)S(1)}, u32[]{:S(2)}, u32[]{:S(2)}) collective-permute-start(f32[16,1024]{1,0:T(8,128)S(1)} %constant_dynamic-slice_fusion.4), channel_id=1, source_target_pairs={{0,2},{1,3},{2,0},{3,1},{4,6},{5,7},{6,4},{7,5},{8,10},{9,11},{10,... | collective-permute-start | bytes 196616 | tf_op jit(solution)/shard_map/ppermute | solution.py:40
  98.5 3.7 %collective-permute-done.11 = f32[16,1024]{1,0:T(8,128)S(1)} collective-permute-done((f32[16,1024]{1,0:T(8,128)S(1)}, f32[16,1024]{1,0:T(8,128)S(1)}, u32[]{:S(2)}, u32[]{:S(2)}) %collective-permute-start.11) | collective-permute-done | bytes 65568 | tf_op jit(solution)/shard_map/ppermute | solution.py:40
  102.2 1.9 %collective-permute-start.12 = (f32[16,512]{1,0:T(8,128)S(1)}, f32[16,512]{1,0:T(8,128)S(1)}, u32[]{:S(2)}, u32[]{:S(2)}) collective-permute-start(f32[16,512]{1,0:T(8,128)S(1)} %constant_dynamic-slice_fusion.3), channel_id=1, source_target_pairs={{0,4},{1,5},{2,6},{3,7},{4,0},{5,1},{6,2},{7,3},{8,12},{9,13},{10,... | collective-permute-start | bytes 98312 | tf_op jit(solution)/shard_map/ppermute | solution.py:40
  104.2 3.9 %collective-permute-done.12 = f32[16,512]{1,0:T(8,128)S(1)} collective-permute-done((f32[16,512]{1,0:T(8,128)S(1)}, f32[16,512]{1,0:T(8,128)S(1)}, u32[]{:S(2)}, u32[]{:S(2)}) %collective-permute-start.12) | collective-permute-done | bytes 32800 | tf_op jit(solution)/shard_map/ppermute | solution.py:40
  108.1 4.1 %collective-permute-start.13 = (f32[16,256]{1,0:T(8,128)S(1)}, f32[16,256]{1,0:T(8,128)S(1)}, u32[]{:S(2)}, u32[]{:S(2)}) collective-permute-start(f32[16,256]{1,0:T(8,128)S(1)} %constant_dynamic-slice_fusion.2), channel_id=1, source_target_pairs={{0,8},{1,9},{2,10},{3,11},{4,12},{5,13},{6,14},{7,15},{8,0},{9,1},... | collective-permute-start | bytes 49160 | tf_op jit(solution)/shard_map/ppermute | solution.py:40
  112.2 4.2 %collective-permute-done.13 = f32[16,256]{1,0:T(8,128)S(1)} collective-permute-done((f32[16,256]{1,0:T(8,128)S(1)}, f32[16,256]{1,0:T(8,128)S(1)}, u32[]{:S(2)}, u32[]{:S(2)}) %collective-permute-start.13) | collective-permute-done | bytes 16416 | tf_op jit(solution)/shard_map/ppermute | solution.py:40
  116.5 4.1 %collective-permute-start.14 = (f32[16,128]{1,0:T(8,128)S(1)}, f32[16,128]{1,0:T(8,128)S(1)}, u32[]{:S(2)}, u32[]{:S(2)}) collective-permute-start(f32[16,128]{1,0:T(8,128)S(1)} %constant_dynamic-slice_fusion.1), channel_id=1, source_target_pairs={{0,16},{1,17},{2,18},{3,19},{4,20},{5,21},{6,22},{7,23},{8,24},{9,... | collective-permute-start | bytes 24584 | tf_op jit(solution)/shard_map/ppermute | solution.py:40
  120.6 4.1 %collective-permute-done.14 = f32[16,128]{1,0:T(8,128)S(1)} collective-permute-done((f32[16,128]{1,0:T(8,128)S(1)}, f32[16,128]{1,0:T(8,128)S(1)}, u32[]{:S(2)}, u32[]{:S(2)}) %collective-permute-start.14) | collective-permute-done | bytes 8224 | tf_op jit(solution)/shard_map/ppermute | solution.py:40
  (174 shorter events, 26.1 us)
Async XLA Ops:
  0.0 77.0 %copy-start = (bf16[16,1024]{1,0:T(8,128)(2,1)S(1)}, bf16[16,1024]{1,0:T(8,128)(2,1)}, u32[]{:S(2)}) copy-start(bf16[16,1024]{1,0:T(8,128)(2,1)} %param.7) | copy-start | bytes 98308
  0.0 17.7 %copy-start.2 = (f32[128]{0:T(128)S(1)}, f32[128]{0:T(128)}, u32[]{:S(2)}) copy-start(f32[128]{0:T(128)} %param.13) | copy-start | bytes 1540
  0.0 17.7 %copy-start.3 = (f32[128]{0:T(128)S(1)}, f32[128]{0:T(128)}, u32[]{:S(2)}) copy-start(f32[128]{0:T(128)} %param.12) | copy-start | bytes 1540
  0.0 17.7 %copy-start.4 = (f32[64]{0:T(128)S(1)}, f32[64]{0:T(128)}, u32[]{:S(2)}) copy-start(f32[64]{0:T(128)} %param.9) | copy-start | bytes 772
  1.5 18.1 %collective-permute-start = (f32[2,192]{1,0:T(2,128)S(1)}, f32[2,192]{1,0:T(2,128)S(1)}, u32[]{:S(2)}, u32[]{:S(2)}) collective-permute-start(f32[2,192]{1,0:T(2,128)S(1)} %maximum_maximum_fusion), channel_id=1, source_target_pairs={{0,1},{1,0},{2,3},{3,2},{4,5},{5,4},{6,7},{7,6},{8,9},{9,8},{10,11... | collective-permute-start | bytes 4616 | tf_op jit(solution)/shard_map/ppermute | solution.py:83
  17.6 0.7 copy-start.1
  19.7 4.3 %collective-permute-start.1 = (f32[2,384]{1,0:T(2,128)S(1)}, f32[2,384]{1,0:T(2,128)S(1)}, u32[]{:S(2)}, u32[]{:S(2)}) collective-permute-start(f32[2,384]{1,0:T(2,128)S(1)} %maximum_select_fusion.7), channel_id=1, source_target_pairs={{0,2},{1,3},{2,0},{3,1},{4,6},{5,7},{6,4},{7,5},{8,10},{9,11},{10,... | collective-permute-start | bytes 9224 | tf_op jit(solution)/shard_map/ppermute | solution.py:83
  24.0 5.3 %collective-permute-start.2 = (f32[2,768]{1,0:T(2,128)S(1)}, f32[2,768]{1,0:T(2,128)S(1)}, u32[]{:S(2)}, u32[]{:S(2)}) collective-permute-start(f32[2,768]{1,0:T(2,128)S(1)} %maximum_select_fusion.6), channel_id=1, source_target_pairs={{0,4},{1,5},{2,6},{3,7},{4,0},{5,1},{6,2},{7,3},{8,12},{9,13},{10,... | collective-permute-start | bytes 18440 | tf_op jit(solution)/shard_map/ppermute | solution.py:83
  29.3 8.3 %collective-permute-start.3 = (f32[2,1536]{1,0:T(2,128)S(1)}, f32[2,1536]{1,0:T(2,128)S(1)}, u32[]{:S(2)}, u32[]{:S(2)}) collective-permute-start(f32[2,1536]{1,0:T(2,128)S(1)} %maximum_select_fusion.4), channel_id=1, source_target_pairs={{0,8},{1,9},{2,10},{3,11},{4,12},{5,13},{6,14},{7,15},{8,0},{9,1},... | collective-permute-start | bytes 36872 | tf_op jit(solution)/shard_map/ppermute | solution.py:83
  37.7 8.5 %collective-permute-start.4 = (f32[2,3072]{1,0:T(2,128)S(1)}, f32[2,3072]{1,0:T(2,128)S(1)}, u32[]{:S(2)}, u32[]{:S(2)}) collective-permute-start(f32[2,3072]{1,0:T(2,128)S(1)} %maximum_select_fusion.2), channel_id=1, source_target_pairs={{0,16},{1,17},{2,18},{3,19},{4,20},{5,21},{6,22},{7,23},{8,24},{9,... | collective-permute-start | bytes 73736 | tf_op jit(solution)/shard_map/ppermute | solution.py:83
  49.0 8.3 %collective-permute-start.5 = (f32[2,1024]{1,0:T(2,128)S(1)}, f32[2,1024]{1,0:T(2,128)S(1)}, u32[]{:S(2)}, u32[]{:S(2)}) collective-permute-start(f32[2,1024]{1,0:T(2,128)S(1)} %constant_dynamic-slice_fusion.8), channel_id=1, source_target_pairs={{0,512},{32,544},{64,576},{96,608},{128,640},{160,672},{192,704},{... | collective-permute-start | bytes 24584 | tf_op jit(solution)/shard_map/ppermute | solution.py:95
  57.3 4.7 %collective-permute-start.6 = (f32[2,1024]{1,0:T(2,128)S(1)}, f32[2,1024]{1,0:T(2,128)S(1)}, u32[]{:S(2)}, u32[]{:S(2)}) collective-permute-start(f32[2,1024]{1,0:T(2,128)S(1)} %dynamic-slice_add_fusion.3), channel_id=1, source_target_pairs={{0,32},{32,0},{64,96},{96,64},{128,160},{160,128},{192,224},{224,1... | collective-permute-start | bytes 24584 | tf_op jit(solution)/shard_map/ppermute | solution.py:98
  62.0 5.3 %collective-permute-start.7 = (f32[2,1024]{1,0:T(2,128)S(1)}, f32[2,1024]{1,0:T(2,128)S(1)}, u32[]{:S(2)}, u32[]{:S(2)}) collective-permute-start(f32[2,1024]{1,0:T(2,128)S(1)} %add.352), channel_id=1, source_target_pairs={{0,64},{32,96},{64,0},{96,32},{128,192},{160,224},{192,128},{224,1... | collective-permute-start | bytes 24584 | tf_op jit(solution)/shard_map/ppermute | solution.py:98
  67.2 4.4 %collective-permute-start.8 = (f32[2,1024]{1,0:T(2,128)S(1)}, f32[2,1024]{1,0:T(2,128)S(1)}, u32[]{:S(2)}, u32[]{:S(2)}) collective-permute-start(f32[2,1024]{1,0:T(2,128)S(1)} %add.353), channel_id=1, source_target_pairs={{0,128},{32,160},{64,192},{96,224},{128,0},{160,32},{192,64},{224,... | collective-permute-start | bytes 24584 | tf_op jit(solution)/shard_map/ppermute | solution.py:98
  71.6 5.3 %collective-permute-start.9 = (f32[2,1024]{1,0:T(2,128)S(1)}, f32[2,1024]{1,0:T(2,128)S(1)}, u32[]{:S(2)}, u32[]{:S(2)}) collective-permute-start(f32[2,1024]{1,0:T(2,128)S(1)} %add.354), channel_id=1, source_target_pairs={{0,256},{32,288},{64,320},{96,352},{128,384},{160,416},{192,448},{... | collective-permute-start | bytes 24584 | tf_op jit(solution)/shard_map/ppermute | solution.py:98
  80.6 16.0 %collective-permute-start.10 = (f32[16,2048]{1,0:T(8,128)S(1)}, f32[16,2048]{1,0:T(8,128)S(1)}, u32[]{:S(2)}, u32[]{:S(2)}) collective-permute-start(f32[16,2048]{1,0:T(8,128)S(1)} %pad_maximum_fusion), channel_id=1, source_target_pairs={{0,1},{1,0},{2,3},{3,2},{4,5},{5,4},{6,7},{7,6},{8,9},{9,8},{10,11... | collective-permute-start | bytes 393224 | tf_op jit(solution)/shard_map/ppermute | solution.py:32
  96.6 5.6 %collective-permute-start.11 = (f32[16,1024]{1,0:T(8,128)S(1)}, f32[16,1024]{1,0:T(8,128)S(1)}, u32[]{:S(2)}, u32[]{:S(2)}) collective-permute-start(f32[16,1024]{1,0:T(8,128)S(1)} %constant_dynamic-slice_fusion.4), channel_id=1, source_target_pairs={{0,2},{1,3},{2,0},{3,1},{4,6},{5,7},{6,4},{7,5},{8,10},{9,11},{10,... | collective-permute-start | bytes 196616 | tf_op jit(solution)/shard_map/ppermute | solution.py:40
  102.2 5.8 %collective-permute-start.12 = (f32[16,512]{1,0:T(8,128)S(1)}, f32[16,512]{1,0:T(8,128)S(1)}, u32[]{:S(2)}, u32[]{:S(2)}) collective-permute-start(f32[16,512]{1,0:T(8,128)S(1)} %constant_dynamic-slice_fusion.3), channel_id=1, source_target_pairs={{0,4},{1,5},{2,6},{3,7},{4,0},{5,1},{6,2},{7,3},{8,12},{9,13},{10,... | collective-permute-start | bytes 98312 | tf_op jit(solution)/shard_map/ppermute | solution.py:40
  108.1 8.4 %collective-permute-start.13 = (f32[16,256]{1,0:T(8,128)S(1)}, f32[16,256]{1,0:T(8,128)S(1)}, u32[]{:S(2)}, u32[]{:S(2)}) collective-permute-start(f32[16,256]{1,0:T(8,128)S(1)} %constant_dynamic-slice_fusion.2), channel_id=1, source_target_pairs={{0,8},{1,9},{2,10},{3,11},{4,12},{5,13},{6,14},{7,15},{8,0},{9,1},... | collective-permute-start | bytes 49160 | tf_op jit(solution)/shard_map/ppermute | solution.py:40
  116.5 8.3 %collective-permute-start.14 = (f32[16,128]{1,0:T(8,128)S(1)}, f32[16,128]{1,0:T(8,128)S(1)}, u32[]{:S(2)}, u32[]{:S(2)}) collective-permute-start(f32[16,128]{1,0:T(8,128)S(1)} %constant_dynamic-slice_fusion.1), channel_id=1, source_target_pairs={{0,16},{1,17},{2,18},{3,19},{4,20},{5,21},{6,22},{7,23},{8,24},{9,... | collective-permute-start | bytes 24584 | tf_op jit(solution)/shard_map/ppermute | solution.py:40

commit v13 on v12

--- a/solution.py
+++ b/solution.py
@@ -99,7 +99,7 @@
         step *= 2
     pole_at = looked[0]
     live_at = looked[1]
-    chunk = 1024
+    chunk = 2048
     contract = (((1,), (1,)), ((), ()))
 
     blocks = value_data.reshape(2, col_total, -1)

time: 127 us -> 128 us (level)
  the two profiles are of different devices: /device:TPU:1 before, /device:TPU:2 now
where the time goes in v13:
time: 128 us; the launch traced here: 127 us
  starting transfers between devices  74.9 us (59%)
  waiting for transfers between devices  32.2 us (25%)
  matrix products  14.4 us (11%)
  other arithmetic  2.79 us (2%)
  local copies, waits for them, and re-layouts  2 us (2%)
    ppermute x5, starting transfers between devices, per_device(): lax.ppermute(held, 'col', perm=[(i, i ^ step) for i in range(col_total)])  35 us
    ppermute x4, waiting for transfers between devices, reduce_by_halves(): lax.ppermute(sent, axis, perm=[(i, i ^ step) for i in range(size)])  16.7 us
    ppermute x4, starting transfers between devices, per_device(): lax.ppermute(looked, 'row', perm=[(i, i ^ step) for i in range(row_total)])  16.2 us
    ppermute x4, starting transfers between devices, reduce_by_halves(): lax.ppermute(sent, axis, perm=[(i, i ^ step) for i in range(size)])  15.1 us
    ppermute x4, waiting for transfers between devices, per_device(): lax.ppermute(looked, 'row', perm=[(i, i ^ step) for i in range(row_total)])  10.2 us
    dot_general x24, matrix products, look_up(): lax.dot_general(table, hits.astype(jnp.bfloat16), (((1,), (1,)), ((), ())...  7.73 us
    dot_general x2, matrix products, compute_range(): lax.dot_general(basis_wide, cauchy, contract, precision=lax.Precision.HIG...  6.7 us
    ppermute x1, starting transfers between devices, per_device(): lax.ppermute(theirs, 'row', perm=[(i, i ^ half_rows) for i in range(row_t...  6.49 us
  transfers between devices with their start and end apart: 15, of which 14 were waited for; matrix products, arithmetic and copies ran while one was open for 5% of the time, Pallas kernels for 0%

profile of v13, /device:TPU:2, one launch (start us, length us, event | category | flops | bytes accessed | tf_op | source)
XLA Modules:
  0.0 127.3 jit_solution(2754655552419078738)
XLA Ops:
  1.5 1.9 %collective-permute-start = (f32[2,192]{1,0:T(2,128)S(1)}, f32[2,192]{1,0:T(2,128)S(1)}, u32[]{:S(2)}, u32[]{:S(2)}) collective-permute-start(f32[2,192]{1,0:T(2,128)S(1)} %maximum_maximum_fusion), channel_id=1, source_target_pairs={{0,1},{1,0},{2,3},{3,2},{4,5},{5,4},{6,7},{7,6},{8,9},{9,8},{10,11... | collective-permute-start | bytes 4616 | tf_op jit(solution)/shard_map/ppermute | solution.py:83
  5.5 5.2 %collective-permute-start.1 = (f32[2,384]{1,0:T(2,128)S(1)}, f32[2,384]{1,0:T(2,128)S(1)}, u32[]{:S(2)}, u32[]{:S(2)}) collective-permute-start(f32[2,384]{1,0:T(2,128)S(1)} %maximum_select_fusion.7), channel_id=1, source_target_pairs={{0,2},{1,3},{2,0},{3,1},{4,6},{5,7},{6,4},{7,5},{8,10},{9,11},{10,... | collective-permute-start | bytes 9224 | tf_op jit(solution)/shard_map/ppermute | solution.py:83
  12.5 7.9 %collective-permute-start.2 = (f32[2,768]{1,0:T(2,128)S(1)}, f32[2,768]{1,0:T(2,128)S(1)}, u32[]{:S(2)}, u32[]{:S(2)}) collective-permute-start(f32[2,768]{1,0:T(2,128)S(1)} %maximum_select_fusion.6), channel_id=1, source_target_pairs={{0,4},{1,5},{2,6},{3,7},{4,0},{5,1},{6,2},{7,3},{8,12},{9,13},{10,... | collective-permute-start | bytes 18440 | tf_op jit(solution)/shard_map/ppermute | solution.py:83
  22.2 11.9 %collective-permute-start.3 = (f32[2,1536]{1,0:T(2,128)S(1)}, f32[2,1536]{1,0:T(2,128)S(1)}, u32[]{:S(2)}, u32[]{:S(2)}) collective-permute-start(f32[2,1536]{1,0:T(2,128)S(1)} %maximum_select_fusion.4), channel_id=1, source_target_pairs={{0,8},{1,9},{2,10},{3,11},{4,12},{5,13},{6,14},{7,15},{8,0},{9,1},... | collective-permute-start | bytes 36872 | tf_op jit(solution)/shard_map/ppermute | solution.py:83
  36.0 8.2 %collective-permute-start.4 = (f32[2,3072]{1,0:T(2,128)S(1)}, f32[2,3072]{1,0:T(2,128)S(1)}, u32[]{:S(2)}, u32[]{:S(2)}) collective-permute-start(f32[2,3072]{1,0:T(2,128)S(1)} %maximum_select_fusion.2), channel_id=1, source_target_pairs={{0,16},{1,17},{2,18},{3,19},{4,20},{5,21},{6,22},{7,23},{8,24},{9,... | collective-permute-start | bytes 73736 | tf_op jit(solution)/shard_map/ppermute | solution.py:83
  48.7 6.5 %collective-permute-start.5 = (f32[2,1024]{1,0:T(2,128)S(1)}, f32[2,1024]{1,0:T(2,128)S(1)}, u32[]{:S(2)}, u32[]{:S(2)}) collective-permute-start(f32[2,1024]{1,0:T(2,128)S(1)} %constant_dynamic-slice_fusion.6), channel_id=1, source_target_pairs={{0,512},{32,544},{64,576},{96,608},{128,640},{160,672},{192,704},{... | collective-permute-start | bytes 24584 | tf_op jit(solution)/shard_map/ppermute | solution.py:95
  55.6 2.6 %collective-permute-done.5 = f32[2,1024]{1,0:T(2,128)S(1)} collective-permute-done((f32[2,1024]{1,0:T(2,128)S(1)}, f32[2,1024]{1,0:T(2,128)S(1)}, u32[]{:S(2)}, u32[]{:S(2)}) %collective-permute-start.5) | collective-permute-done | bytes 8224 | tf_op jit(solution)/shard_map/ppermute | solution.py:95
  58.2 3.2 %collective-permute-start.6 = (f32[2,1024]{1,0:T(2,128)S(1)}, f32[2,1024]{1,0:T(2,128)S(1)}, u32[]{:S(2)}, u32[]{:S(2)}) collective-permute-start(f32[2,1024]{1,0:T(2,128)S(1)} %dynamic-slice_add_fusion.3), channel_id=1, source_target_pairs={{0,32},{32,0},{64,96},{96,64},{128,160},{160,128},{192,224},{224,1... | collective-permute-start | bytes 24584 | tf_op jit(solution)/shard_map/ppermute | solution.py:98
  61.4 2.3 %collective-permute-done.6 = f32[2,1024]{1,0:T(2,128)S(1)} collective-permute-done((f32[2,1024]{1,0:T(2,128)S(1)}, f32[2,1024]{1,0:T(2,128)S(1)}, u32[]{:S(2)}, u32[]{:S(2)}) %collective-permute-start.6) | collective-permute-done | bytes 8224 | tf_op jit(solution)/shard_map/ppermute | solution.py:98
  63.7 4.5 %collective-permute-start.7 = (f32[2,1024]{1,0:T(2,128)S(1)}, f32[2,1024]{1,0:T(2,128)S(1)}, u32[]{:S(2)}, u32[]{:S(2)}) collective-permute-start(f32[2,1024]{1,0:T(2,128)S(1)} %add.336), channel_id=1, source_target_pairs={{0,64},{32,96},{64,0},{96,32},{128,192},{160,224},{192,128},{224,1... | collective-permute-start | bytes 24584 | tf_op jit(solution)/shard_map/ppermute | solution.py:98
  70.2 6.6 %collective-permute-start.8 = (f32[2,1024]{1,0:T(2,128)S(1)}, f32[2,1024]{1,0:T(2,128)S(1)}, u32[]{:S(2)}, u32[]{:S(2)}) collective-permute-start(f32[2,1024]{1,0:T(2,128)S(1)} %add.337), channel_id=1, source_target_pairs={{0,128},{32,160},{64,192},{96,224},{128,0},{160,32},{192,64},{224,... | collective-permute-start | bytes 24584 | tf_op jit(solution)/shard_map/ppermute | solution.py:98
  78.4 1.9 %collective-permute-start.9 = (f32[2,1024]{1,0:T(2,128)S(1)}, f32[2,1024]{1,0:T(2,128)S(1)}, u32[]{:S(2)}, u32[]{:S(2)}) collective-permute-start(f32[2,1024]{1,0:T(2,128)S(1)} %add.338), channel_id=1, source_target_pairs={{0,256},{32,288},{64,320},{96,352},{128,384},{160,416},{192,448},{... | collective-permute-start | bytes 24584 | tf_op jit(solution)/shard_map/ppermute | solution.py:98
  80.4 4.4 %collective-permute-done.9 = f32[2,1024]{1,0:T(2,128)S(1)} collective-permute-done((f32[2,1024]{1,0:T(2,128)S(1)}, f32[2,1024]{1,0:T(2,128)S(1)}, u32[]{:S(2)}, u32[]{:S(2)}) %collective-permute-start.9) | collective-permute-done | bytes 8224 | tf_op jit(solution)/shard_map/ppermute | solution.py:98
  84.8 3.3 %fusion.16 = f32[16,2048]{1,0:T(8,128)S(1)} fusion(bf16[16,1024]{1,0:T(8,128)(2,1)S(1)} %copy-done, f32[2048]{0:T(1024)S(1)} %bitcast.164, f32[2048]{0:T(1024)S(1)} %bitcast.163, f32[1024]{0:T(1024)S(1)} %bitcast.197, f32[1024]{0:T(1024)S(1)} %bitcast.195), kind=kOutput, calls=%fused_computation.16 | convolution fusion | flops 207618048 | bytes 188416 | tf_op jit(solution)/shard_map/dot_general | solution.py:116
  88.2 2.1 %collective-permute-start.10 = (f32[16,2048]{1,0:T(8,128)S(1)}, f32[16,2048]{1,0:T(8,128)S(1)}, u32[]{:S(2)}, u32[]{:S(2)}) collective-permute-start(f32[16,2048]{1,0:T(8,128)S(1)} %fusion.16), channel_id=1, source_target_pairs={{0,1},{1,0},{2,3},{3,2},{4,5},{5,4},{6,7},{7,6},{8,9},{9,8},{10,11... | collective-permute-start | bytes 393224 | tf_op jit(solution)/shard_map/ppermute | solution.py:32
  91.4 3.3 %fusion.22 = f32[16,2048]{1,0:T(8,128)S(1)} fusion(f32[16,2048]{1,0:T(8,128)S(1)} %collective-permute-done.10, bf16[16,1024]{1,0:T(8,128)(2,1)S(1)} %copy-done, f32[2048]{0:T(1024)S(1)} %bitcast.166, f32[2048]{0:T(1024)S(1)} %bitcast.165, f32[1024]{0:T(1024)S(1)} %bitcast.198, f32[1024]{0:T(1024)S(1)} %bitcast.196), kind=kOutput, calls=%fused_computation.18 | convolution fusion | flops 207650816 | bytes 319488 | tf_op jit(solution)/shard_map/dot_general | solution.py:116
  94.8 1.9 %collective-permute-start.11 = (f32[16,1024]{1,0:T(8,128)S(1)}, f32[16,1024]{1,0:T(8,128)S(1)}, u32[]{:S(2)}, u32[]{:S(2)}) collective-permute-start(f32[16,1024]{1,0:T(8,128)S(1)} %constant_dynamic-slice_fusion.4), channel_id=1, source_target_pairs={{0,2},{1,3},{2,0},{3,1},{4,6},{5,7},{6,4},{7,5},{8,10},{9,11},{10,... | collective-permute-start | bytes 196616 | tf_op jit(solution)/shard_map/ppermute | solution.py:40
  96.7 4.2 %collective-permute-done.11 = f32[16,1024]{1,0:T(8,128)S(1)} collective-permute-done((f32[16,1024]{1,0:T(8,128)S(1)}, f32[16,1024]{1,0:T(8,128)S(1)}, u32[]{:S(2)}, u32[]{:S(2)}) %collective-permute-start.11) | collective-permute-done | bytes 65568 | tf_op jit(solution)/shard_map/ppermute | solution.py:40
  101.0 2.3 %collective-permute-start.12 = (f32[16,512]{1,0:T(8,128)S(1)}, f32[16,512]{1,0:T(8,128)S(1)}, u32[]{:S(2)}, u32[]{:S(2)}) collective-permute-start(f32[16,512]{1,0:T(8,128)S(1)} %constant_dynamic-slice_fusion.3), channel_id=1, source_target_pairs={{0,4},{1,5},{2,6},{3,7},{4,0},{5,1},{6,2},{7,3},{8,12},{9,13},{10,... | collective-permute-start | bytes 98312 | tf_op jit(solution)/shard_map/ppermute | solution.py:40
  103.3 4.4 %collective-permute-done.12 = f32[16,512]{1,0:T(8,128)S(1)} collective-permute-done((f32[16,512]{1,0:T(8,128)S(1)}, f32[16,512]{1,0:T(8,128)S(1)}, u32[]{:S(2)}, u32[]{:S(2)}) %collective-permute-start.12) | collective-permute-done | bytes 32800 | tf_op jit(solution)/shard_map/ppermute | solution.py:40
  107.7 5.6 %collective-permute-start.13 = (f32[16,256]{1,0:T(8,128)S(1)}, f32[16,256]{1,0:T(8,128)S(1)}, u32[]{:S(2)}, u32[]{:S(2)}) collective-permute-start(f32[16,256]{1,0:T(8,128)S(1)} %constant_dynamic-slice_fusion.2), channel_id=1, source_target_pairs={{0,8},{1,9},{2,10},{3,11},{4,12},{5,13},{6,14},{7,15},{8,0},{9,1},... | collective-permute-start | bytes 49160 | tf_op jit(solution)/shard_map/ppermute | solution.py:40
  113.3 4.0 %collective-permute-done.13 = f32[16,256]{1,0:T(8,128)S(1)} collective-permute-done((f32[16,256]{1,0:T(8,128)S(1)}, f32[16,256]{1,0:T(8,128)S(1)}, u32[]{:S(2)}, u32[]{:S(2)}) %collective-permute-start.13) | collective-permute-done | bytes 16416 | tf_op jit(solution)/shard_map/ppermute | solution.py:40
  117.3 5.3 %collective-permute-start.14 = (f32[16,128]{1,0:T(8,128)S(1)}, f32[16,128]{1,0:T(8,128)S(1)}, u32[]{:S(2)}, u32[]{:S(2)}) collective-permute-start(f32[16,128]{1,0:T(8,128)S(1)} %constant_dynamic-slice_fusion.1), channel_id=1, source_target_pairs={{0,16},{1,17},{2,18},{3,19},{4,20},{5,21},{6,22},{7,23},{8,24},{9,... | collective-permute-start | bytes 24584 | tf_op jit(solution)/shard_map/ppermute | solution.py:40
  122.6 4.1 %collective-permute-done.14 = f32[16,128]{1,0:T(8,128)S(1)} collective-permute-done((f32[16,128]{1,0:T(8,128)S(1)}, f32[16,128]{1,0:T(8,128)S(1)}, u32[]{:S(2)}, u32[]{:S(2)}) %collective-permute-start.14) | collective-permute-done | bytes 8224 | tf_op jit(solution)/shard_map/ppermute | solution.py:40
  (170 shorter events, 18.7 us)
Async XLA Ops:
  0.0 84.8 %copy-start = (bf16[16,1024]{1,0:T(8,128)(2,1)S(1)}, bf16[16,1024]{1,0:T(8,128)(2,1)}, u32[]{:S(2)}) copy-start(bf16[16,1024]{1,0:T(8,128)(2,1)} %param.7) | copy-start | bytes 98308
  0.0 3.6 %copy-start.2 = (f32[128]{0:T(128)S(1)}, f32[128]{0:T(128)}, u32[]{:S(2)}) copy-start(f32[128]{0:T(128)} %param.13) | copy-start | bytes 1540
  0.0 3.6 %copy-start.3 = (f32[128]{0:T(128)S(1)}, f32[128]{0:T(128)}, u32[]{:S(2)}) copy-start(f32[128]{0:T(128)} %param.12) | copy-start | bytes 1540
  0.0 3.6 %copy-start.4 = (f32[64]{0:T(128)S(1)}, f32[64]{0:T(128)}, u32[]{:S(2)}) copy-start(f32[64]{0:T(128)} %param.9) | copy-start | bytes 772
  1.5 3.9 %collective-permute-start = (f32[2,192]{1,0:T(2,128)S(1)}, f32[2,192]{1,0:T(2,128)S(1)}, u32[]{:S(2)}, u32[]{:S(2)}) collective-permute-start(f32[2,192]{1,0:T(2,128)S(1)} %maximum_maximum_fusion), channel_id=1, source_target_pairs={{0,1},{1,0},{2,3},{3,2},{4,5},{5,4},{6,7},{7,6},{8,9},{9,8},{10,11... | collective-permute-start | bytes 4616 | tf_op jit(solution)/shard_map/ppermute | solution.py:83
  3.4 0.7 copy-start.1
  5.5 6.8 %collective-permute-start.1 = (f32[2,384]{1,0:T(2,128)S(1)}, f32[2,384]{1,0:T(2,128)S(1)}, u32[]{:S(2)}, u32[]{:S(2)}) collective-permute-start(f32[2,384]{1,0:T(2,128)S(1)} %maximum_select_fusion.7), channel_id=1, source_target_pairs={{0,2},{1,3},{2,0},{3,1},{4,6},{5,7},{6,4},{7,5},{8,10},{9,11},{10,... | collective-permute-start | bytes 9224 | tf_op jit(solution)/shard_map/ppermute | solution.py:83
  12.5 9.5 %collective-permute-start.2 = (f32[2,768]{1,0:T(2,128)S(1)}, f32[2,768]{1,0:T(2,128)S(1)}, u32[]{:S(2)}, u32[]{:S(2)}) collective-permute-start(f32[2,768]{1,0:T(2,128)S(1)} %maximum_select_fusion.6), channel_id=1, source_target_pairs={{0,4},{1,5},{2,6},{3,7},{4,0},{5,1},{6,2},{7,3},{8,12},{9,13},{10,... | collective-permute-start | bytes 18440 | tf_op jit(solution)/shard_map/ppermute | solution.py:83
  22.2 13.5 %collective-permute-start.3 = (f32[2,1536]{1,0:T(2,128)S(1)}, f32[2,1536]{1,0:T(2,128)S(1)}, u32[]{:S(2)}, u32[]{:S(2)}) collective-permute-start(f32[2,1536]{1,0:T(2,128)S(1)} %maximum_select_fusion.4), channel_id=1, source_target_pairs={{0,8},{1,9},{2,10},{3,11},{4,12},{5,13},{6,14},{7,15},{8,0},{9,1},... | collective-permute-start | bytes 36872 | tf_op jit(solution)/shard_map/ppermute | solution.py:83
  36.0 10.0 %collective-permute-start.4 = (f32[2,3072]{1,0:T(2,128)S(1)}, f32[2,3072]{1,0:T(2,128)S(1)}, u32[]{:S(2)}, u32[]{:S(2)}) collective-permute-start(f32[2,3072]{1,0:T(2,128)S(1)} %maximum_select_fusion.2), channel_id=1, source_target_pairs={{0,16},{1,17},{2,18},{3,19},{4,20},{5,21},{6,22},{7,23},{8,24},{9,... | collective-permute-start | bytes 73736 | tf_op jit(solution)/shard_map/ppermute | solution.py:83
  48.7 9.5 %collective-permute-start.5 = (f32[2,1024]{1,0:T(2,128)S(1)}, f32[2,1024]{1,0:T(2,128)S(1)}, u32[]{:S(2)}, u32[]{:S(2)}) collective-permute-start(f32[2,1024]{1,0:T(2,128)S(1)} %constant_dynamic-slice_fusion.6), channel_id=1, source_target_pairs={{0,512},{32,544},{64,576},{96,608},{128,640},{160,672},{192,704},{... | collective-permute-start | bytes 24584 | tf_op jit(solution)/shard_map/ppermute | solution.py:95
  58.2 5.5 %collective-permute-start.6 = (f32[2,1024]{1,0:T(2,128)S(1)}, f32[2,1024]{1,0:T(2,128)S(1)}, u32[]{:S(2)}, u32[]{:S(2)}) collective-permute-start(f32[2,1024]{1,0:T(2,128)S(1)} %dynamic-slice_add_fusion.3), channel_id=1, source_target_pairs={{0,32},{32,0},{64,96},{96,64},{128,160},{160,128},{192,224},{224,1... | collective-permute-start | bytes 24584 | tf_op jit(solution)/shard_map/ppermute | solution.py:98
  63.7 6.4 %collective-permute-start.7 = (f32[2,1024]{1,0:T(2,128)S(1)}, f32[2,1024]{1,0:T(2,128)S(1)}, u32[]{:S(2)}, u32[]{:S(2)}) collective-permute-start(f32[2,1024]{1,0:T(2,128)S(1)} %add.336), channel_id=1, source_target_pairs={{0,64},{32,96},{64,0},{96,32},{128,192},{160,224},{192,128},{224,1... | collective-permute-start | bytes 24584 | tf_op jit(solution)/shard_map/ppermute | solution.py:98
  70.2 8.2 %collective-permute-start.8 = (f32[2,1024]{1,0:T(2,128)S(1)}, f32[2,1024]{1,0:T(2,128)S(1)}, u32[]{:S(2)}, u32[]{:S(2)}) collective-permute-start(f32[2,1024]{1,0:T(2,128)S(1)} %add.337), channel_id=1, source_target_pairs={{0,128},{32,160},{64,192},{96,224},{128,0},{160,32},{192,64},{224,... | collective-permute-start | bytes 24584 | tf_op jit(solution)/shard_map/ppermute | solution.py:98
  78.4 6.4 %collective-permute-start.9 = (f32[2,1024]{1,0:T(2,128)S(1)}, f32[2,1024]{1,0:T(2,128)S(1)}, u32[]{:S(2)}, u32[]{:S(2)}) collective-permute-start(f32[2,1024]{1,0:T(2,128)S(1)} %add.338), channel_id=1, source_target_pairs={{0,256},{32,288},{64,320},{96,352},{128,384},{160,416},{192,448},{... | collective-permute-start | bytes 24584 | tf_op jit(solution)/shard_map/ppermute | solution.py:98
  88.2 3.2 %collective-permute-start.10 = (f32[16,2048]{1,0:T(8,128)S(1)}, f32[16,2048]{1,0:T(8,128)S(1)}, u32[]{:S(2)}, u32[]{:S(2)}) collective-permute-start(f32[16,2048]{1,0:T(8,128)S(1)} %fusion.16), channel_id=1, source_target_pairs={{0,1},{1,0},{2,3},{3,2},{4,5},{5,4},{6,7},{7,6},{8,9},{9,8},{10,11... | collective-permute-start | bytes 393224 | tf_op jit(solution)/shard_map/ppermute | solution.py:32
  94.8 6.2 %collective-permute-start.11 = (f32[16,1024]{1,0:T(8,128)S(1)}, f32[16,1024]{1,0:T(8,128)S(1)}, u32[]{:S(2)}, u32[]{:S(2)}) collective-permute-start(f32[16,1024]{1,0:T(8,128)S(1)} %constant_dynamic-slice_fusion.4), channel_id=1, source_target_pairs={{0,2},{1,3},{2,0},{3,1},{4,6},{5,7},{6,4},{7,5},{8,10},{9,11},{10,... | collective-permute-start | bytes 196616 | tf_op jit(solution)/shard_map/ppermute | solution.py:40
  101.0 6.7 %collective-permute-start.12 = (f32[16,512]{1,0:T(8,128)S(1)}, f32[16,512]{1,0:T(8,128)S(1)}, u32[]{:S(2)}, u32[]{:S(2)}) collective-permute-start(f32[16,512]{1,0:T(8,128)S(1)} %constant_dynamic-slice_fusion.3), channel_id=1, source_target_pairs={{0,4},{1,5},{2,6},{3,7},{4,0},{5,1},{6,2},{7,3},{8,12},{9,13},{10,... | collective-permute-start | bytes 98312 | tf_op jit(solution)/shard_map/ppermute | solution.py:40
  107.7 9.5 %collective-permute-start.13 = (f32[16,256]{1,0:T(8,128)S(1)}, f32[16,256]{1,0:T(8,128)S(1)}, u32[]{:S(2)}, u32[]{:S(2)}) collective-permute-start(f32[16,256]{1,0:T(8,128)S(1)} %constant_dynamic-slice_fusion.2), channel_id=1, source_target_pairs={{0,8},{1,9},{2,10},{3,11},{4,12},{5,13},{6,14},{7,15},{8,0},{9,1},... | collective-permute-start | bytes 49160 | tf_op jit(solution)/shard_map/ppermute | solution.py:40
  117.3 9.4 %collective-permute-start.14 = (f32[16,128]{1,0:T(8,128)S(1)}, f32[16,128]{1,0:T(8,128)S(1)}, u32[]{:S(2)}, u32[]{:S(2)}) collective-permute-start(f32[16,128]{1,0:T(8,128)S(1)} %constant_dynamic-slice_fusion.1), channel_id=1, source_target_pairs={{0,16},{1,17},{2,18},{3,19},{4,20},{5,21},{6,22},{7,23},{8,24},{9,... | collective-permute-start | bytes 24584 | tf_op jit(solution)/shard_map/ppermute | solution.py:40

commit v14 on v12

--- a/solution.py
+++ b/solution.py
@@ -29,17 +29,20 @@
     bit = index % 2
     sent = compute_range(inputs, (1 - bit) * width, width)
     sent, inputs = lax.optimization_barrier((sent, inputs))
-    got = lax.ppermute(sent, axis, perm=[(i, i ^ step) for i in range(size)])
-    held = compute_range(inputs, bit * width, width) + got
+    pending = lax.ppermute(sent, axis, perm=[(i, i ^ step) for i in range(size)])
+    low = bit * width
     step *= 2
     while step < size:
         width //= 2
         bit = (index // step) % 2
-        sent = lax.dynamic_slice_in_dim(held, (1 - bit) * width, width, -1)
-        kept = lax.dynamic_slice_in_dim(held, bit * width, width, -1)
-        held = kept + lax.ppermute(sent, axis, perm=[(i, i ^ step) for i in range(size)])
+        sent = compute_range(inputs, low + (1 - bit) * width, width)
+        sent = sent + lax.dynamic_slice_in_dim(pending, (1 - bit) * width, width, -1)
+        kept = lax.dynamic_slice_in_dim(pending, bit * width, width, -1)
+        sent, inputs = lax.optimization_barrier((sent, inputs))
+        pending = kept + lax.ppermute(sent, axis, perm=[(i, i ^ step) for i in range(size)])
+        low = low + bit * width
         step *= 2
-    return held
+    return compute_range(inputs, low, width) + pending
 
 
 def bit_reversed(count):
@@ -110,8 +113,9 @@
     def compute_range(inputs, offset, width):
         pole_at, live_at, value_data = inputs
         parts = []
-        for start in range(0, width, chunk):
-            values = lax.dynamic_slice_in_dim(value_data, offset + start, chunk, 1)
+        size = min(chunk, width)
+        for start in range(0, width, size):
+            values = lax.dynamic_slice_in_dim(value_data, offset + start, size, 1)
             cauchy = cauchy_tile_t(pole_at, live_at, values[0], values[1])
             parts.append(lax.dot_general(basis_wide, cauchy, contract, precision=lax.Precision.HIGH, preferred_element_type=jnp.float32))
         return jnp.concatenate(parts, 1)

time: 127 us -> 130 us (1.024)
  local copies, waits for them, and re-layouts: 2.05 us -> 3.75 us
    ppermute x4 -> x5, starting transfers between devices: 12.1 us -> 25.4 us  [reduce_by_halves(): lax.ppermute(sent, axis, perm=[(i, i ^ step) for i in range(size)])]
    ppermute x1 -> x0, starting transfers between devices: 12.3 us -> none  [reduce_by_halves(): got = lax.ppermute(sent, axis, perm=[(i, i ^ step) for i in range(size)])]
    unnamed x41, local copies, waits for them, and re-layouts: 0.77 us -> 2.42 us
    ppermute x4 -> x5, waiting for transfers between devices: 15.9 us -> 14.5 us  [reduce_by_halves(): lax.ppermute(sent, axis, perm=[(i, i ^ step) for i in range(size)])]
    dot_general x4 -> x7, matrix products: 7.07 us -> 8.1 us  [compute_range(): lax.dot_general(basis_wide, cauchy, contract, precision=lax.Precision.HIG...]
  transfers between devices with their start and end apart: 15 -> 15, of which waited for: 13 -> 14; matrix products, arithmetic and copies ran while one was open for 8% -> 6% of each run, Pallas kernels for 0% -> 0%
where the time goes in v14:
time: 130 us; the launch traced here: 127 us
  starting transfers between devices  67.9 us (52%)
  waiting for transfers between devices  36.8 us (28%)
  matrix products  15.8 us (12%)
  local copies, waits for them, and re-layouts  3.75 us (3%)
  other arithmetic  2.25 us (2%)
    ppermute x5, starting transfers between devices, per_device(): lax.ppermute(held, 'col', perm=[(i, i ^ step) for i in range(col_total)])  29.2 us
    ppermute x5, starting transfers between devices, reduce_by_halves(): lax.ppermute(sent, axis, perm=[(i, i ^ step) for i in range(size)])  25.4 us
    ppermute x5, waiting for transfers between devices, reduce_by_halves(): lax.ppermute(sent, axis, perm=[(i, i ^ step) for i in range(size)])  14.5 us
    ppermute x4, waiting for transfers between devices, per_device(): lax.ppermute(looked, 'row', perm=[(i, i ^ step) for i in range(row_total)])  11.5 us
    dot_general x7, matrix products, compute_range(): lax.dot_general(basis_wide, cauchy, contract, precision=lax.Precision.HIG...  8.1 us
    ppermute x5, waiting for transfers between devices, per_device(): lax.ppermute(held, 'col', perm=[(i, i ^ step) for i in range(col_total)])  7.93 us
    ppermute x4, starting transfers between devices, per_device(): lax.ppermute(looked, 'row', perm=[(i, i ^ step) for i in range(row_total)])  7.78 us
    dot_general x24, matrix products, look_up(): lax.dot_general(table, hits.astype(jnp.bfloat16), (((1,), (1,)), ((), ())...  7.72 us
  transfers between devices with their start and end apart: 15, of which 14 were waited for; matrix products, arithmetic and copies ran while one was open for 6% of the time, Pallas kernels for 0%

profile of v14, /device:TPU:1, one launch (start us, length us, event | category | flops | bytes accessed | tf_op | source)
XLA Modules:
  0.0 127.4 jit_solution(2290361497443058011)
XLA Ops:
  1.5 16.1 %collective-permute-start = (f32[2,192]{1,0:T(2,128)S(1)}, f32[2,192]{1,0:T(2,128)S(1)}, u32[]{:S(2)}, u32[]{:S(2)}) collective-permute-start(f32[2,192]{1,0:T(2,128)S(1)} %maximum_maximum_fusion), channel_id=1, source_target_pairs={{0,1},{1,0},{2,3},{3,2},{4,5},{5,4},{6,7},{7,6},{8,9},{9,8},{10,11... | collective-permute-start | bytes 4616 | tf_op jit(solution)/shard_map/ppermute | solution.py:86
  19.2 1.9 %collective-permute-start.1 = (f32[2,384]{1,0:T(2,128)S(1)}, f32[2,384]{1,0:T(2,128)S(1)}, u32[]{:S(2)}, u32[]{:S(2)}) collective-permute-start(f32[2,384]{1,0:T(2,128)S(1)} %maximum_select_fusion.7), channel_id=1, source_target_pairs={{0,2},{1,3},{2,0},{3,1},{4,6},{5,7},{6,4},{7,5},{8,10},{9,11},{10,... | collective-permute-start | bytes 9224 | tf_op jit(solution)/shard_map/ppermute | solution.py:86
  23.6 1.9 %collective-permute-start.2 = (f32[2,768]{1,0:T(2,128)S(1)}, f32[2,768]{1,0:T(2,128)S(1)}, u32[]{:S(2)}, u32[]{:S(2)}) collective-permute-start(f32[2,768]{1,0:T(2,128)S(1)} %maximum_select_fusion.6), channel_id=1, source_target_pairs={{0,4},{1,5},{2,6},{3,7},{4,0},{5,1},{6,2},{7,3},{8,12},{9,13},{10,... | collective-permute-start | bytes 18440 | tf_op jit(solution)/shard_map/ppermute | solution.py:86
  26.8 2.2 %collective-permute-done.2 = f32[2,768]{1,0:T(2,128)S(1)} collective-permute-done((f32[2,768]{1,0:T(2,128)S(1)}, f32[2,768]{1,0:T(2,128)S(1)}, u32[]{:S(2)}, u32[]{:S(2)}) %collective-permute-start.2) | collective-permute-done | bytes 6176 | tf_op jit(solution)/shard_map/ppermute | solution.py:86
  29.1 4.3 %collective-permute-start.3 = (f32[2,1536]{1,0:T(2,128)S(1)}, f32[2,1536]{1,0:T(2,128)S(1)}, u32[]{:S(2)}, u32[]{:S(2)}) collective-permute-start(f32[2,1536]{1,0:T(2,128)S(1)} %maximum_select_fusion.4), channel_id=1, source_target_pairs={{0,8},{1,9},{2,10},{3,11},{4,12},{5,13},{6,14},{7,15},{8,0},{9,1},... | collective-permute-start | bytes 36872 | tf_op jit(solution)/shard_map/ppermute | solution.py:86
  34.6 2.8 %collective-permute-done.3 = f32[2,1536]{1,0:T(2,128)S(1)} collective-permute-done((f32[2,1536]{1,0:T(2,128)S(1)}, f32[2,1536]{1,0:T(2,128)S(1)}, u32[]{:S(2)}, u32[]{:S(2)}) %collective-permute-start.3) | collective-permute-done | bytes 12320 | tf_op jit(solution)/shard_map/ppermute | solution.py:86
  37.5 5.1 %collective-permute-start.4 = (f32[2,3072]{1,0:T(2,128)S(1)}, f32[2,3072]{1,0:T(2,128)S(1)}, u32[]{:S(2)}, u32[]{:S(2)}) collective-permute-start(f32[2,3072]{1,0:T(2,128)S(1)} %maximum_select_fusion.2), channel_id=1, source_target_pairs={{0,16},{1,17},{2,18},{3,19},{4,20},{5,21},{6,22},{7,23},{8,24},{9,... | collective-permute-start | bytes 73736 | tf_op jit(solution)/shard_map/ppermute | solution.py:86
  50.8 5.4 %collective-permute-start.5 = (f32[2,1024]{1,0:T(2,128)S(1)}, f32[2,1024]{1,0:T(2,128)S(1)}, u32[]{:S(2)}, u32[]{:S(2)}) collective-permute-start(f32[2,1024]{1,0:T(2,128)S(1)} %constant_dynamic-slice_fusion.7), channel_id=1, source_target_pairs={{0,512},{32,544},{64,576},{96,608},{128,640},{160,672},{192,704},{... | collective-permute-start | bytes 24584 | tf_op jit(solution)/shard_map/ppermute | solution.py:98
  56.3 2.8 %collective-permute-done.5 = f32[2,1024]{1,0:T(2,128)S(1)} collective-permute-done((f32[2,1024]{1,0:T(2,128)S(1)}, f32[2,1024]{1,0:T(2,128)S(1)}, u32[]{:S(2)}, u32[]{:S(2)}) %collective-permute-start.5) | collective-permute-done | bytes 8224 | tf_op jit(solution)/shard_map/ppermute | solution.py:98
  59.1 1.9 %collective-permute-start.6 = (f32[2,1024]{1,0:T(2,128)S(1)}, f32[2,1024]{1,0:T(2,128)S(1)}, u32[]{:S(2)}, u32[]{:S(2)}) collective-permute-start(f32[2,1024]{1,0:T(2,128)S(1)} %dynamic-slice_add_fusion.7), channel_id=1, source_target_pairs={{0,32},{32,0},{64,96},{96,64},{128,160},{160,128},{192,224},{224,1... | collective-permute-start | bytes 24584 | tf_op jit(solution)/shard_map/ppermute | solution.py:101
  61.1 2.7 %collective-permute-done.6 = f32[2,1024]{1,0:T(2,128)S(1)} collective-permute-done((f32[2,1024]{1,0:T(2,128)S(1)}, f32[2,1024]{1,0:T(2,128)S(1)}, u32[]{:S(2)}, u32[]{:S(2)}) %collective-permute-start.6) | collective-permute-done | bytes 8224 | tf_op jit(solution)/shard_map/ppermute | solution.py:101
  65.8 3.3 %collective-permute-done.7 = f32[2,1024]{1,0:T(2,128)S(1)} collective-permute-done((f32[2,1024]{1,0:T(2,128)S(1)}, f32[2,1024]{1,0:T(2,128)S(1)}, u32[]{:S(2)}, u32[]{:S(2)}) %collective-permute-start.7) | collective-permute-done | bytes 8224 | tf_op jit(solution)/shard_map/ppermute | solution.py:101
  71.1 2.4 %collective-permute-done.8 = f32[2,1024]{1,0:T(2,128)S(1)} collective-permute-done((f32[2,1024]{1,0:T(2,128)S(1)}, f32[2,1024]{1,0:T(2,128)S(1)}, u32[]{:S(2)}, u32[]{:S(2)}) %collective-permute-start.8) | collective-permute-done | bytes 8224 | tf_op jit(solution)/shard_map/ppermute | solution.py:101
  73.5 2.1 %collective-permute-start.9 = (f32[2,1024]{1,0:T(2,128)S(1)}, f32[2,1024]{1,0:T(2,128)S(1)}, u32[]{:S(2)}, u32[]{:S(2)}) collective-permute-start(f32[2,1024]{1,0:T(2,128)S(1)} %add.394), channel_id=1, source_target_pairs={{0,256},{32,288},{64,320},{96,352},{128,384},{160,416},{192,448},{... | collective-permute-start | bytes 24584 | tf_op jit(solution)/shard_map/ppermute | solution.py:101
  75.6 3.2 %collective-permute-done.9 = f32[2,1024]{1,0:T(2,128)S(1)} collective-permute-done((f32[2,1024]{1,0:T(2,128)S(1)}, f32[2,1024]{1,0:T(2,128)S(1)}, u32[]{:S(2)}, u32[]{:S(2)}) %collective-permute-start.9) | collective-permute-done | bytes 8224 | tf_op jit(solution)/shard_map/ppermute | solution.py:101
  82.4 12.1 %collective-permute-start.10 = (f32[16,2048]{1,0:T(8,128)S(1)}, f32[16,2048]{1,0:T(8,128)S(1)}, u32[]{:S(2)}, u32[]{:S(2)}) collective-permute-start(f32[16,2048]{1,0:T(8,128)S(1)} %pad_maximum_fusion), channel_id=1, source_target_pairs={{0,1},{1,0},{2,3},{3,2},{4,5},{5,4},{6,7},{7,6},{8,9},{9,8},{10,11... | collective-permute-start | bytes 393224 | tf_op jit(solution)/shard_map/ppermute | solution.py:32
  97.3 1.9 %collective-permute-start.11 = (f32[16,1024]{1,0:T(8,128)S(1)}, f32[16,1024]{1,0:T(8,128)S(1)}, u32[]{:S(2)}, u32[]{:S(2)}) collective-permute-start(f32[16,1024]{1,0:T(8,128)S(1)} %dynamic-slice_add_fusion.1), channel_id=1, source_target_pairs={{0,2},{1,3},{2,0},{3,1},{4,6},{5,7},{6,4},{7,5},{8,10},{9,11},{10,... | collective-permute-start | bytes 196616 | tf_op jit(solution)/shard_map/ppermute | solution.py:42
  99.3 3.0 %collective-permute-done.11 = f32[16,1024]{1,0:T(8,128)S(1)} collective-permute-done((f32[16,1024]{1,0:T(8,128)S(1)}, f32[16,1024]{1,0:T(8,128)S(1)}, u32[]{:S(2)}, u32[]{:S(2)}) %collective-permute-start.11) | collective-permute-done | bytes 65568 | tf_op jit(solution)/shard_map/ppermute | solution.py:42
  103.3 1.9 %collective-permute-start.12 = (f32[16,512]{1,0:T(8,128)S(1)}, f32[16,512]{1,0:T(8,128)S(1)}, u32[]{:S(2)}, u32[]{:S(2)}) collective-permute-start(f32[16,512]{1,0:T(8,128)S(1)} %dynamic-slice_add_fusion.3), channel_id=1, source_target_pairs={{0,4},{1,5},{2,6},{3,7},{4,0},{5,1},{6,2},{7,3},{8,12},{9,13},{10,... | collective-permute-start | bytes 98312 | tf_op jit(solution)/shard_map/ppermute | solution.py:42
  105.3 3.6 %collective-permute-done.12 = f32[16,512]{1,0:T(8,128)S(1)} collective-permute-done((f32[16,512]{1,0:T(8,128)S(1)}, f32[16,512]{1,0:T(8,128)S(1)}, u32[]{:S(2)}, u32[]{:S(2)}) %collective-permute-start.12) | collective-permute-done | bytes 32800 | tf_op jit(solution)/shard_map/ppermute | solution.py:42
  109.4 4.8 %collective-permute-start.13 = (f32[16,256]{1,0:T(8,128)S(1)}, f32[16,256]{1,0:T(8,128)S(1)}, u32[]{:S(2)}, u32[]{:S(2)}) collective-permute-start(f32[16,256]{1,0:T(8,128)S(1)} %dynamic-slice_add_fusion.5), channel_id=1, source_target_pairs={{0,8},{1,9},{2,10},{3,11},{4,12},{5,13},{6,14},{7,15},{8,0},{9,1},... | collective-permute-start | bytes 49160 | tf_op jit(solution)/shard_map/ppermute | solution.py:42
  114.2 3.6 %collective-permute-done.13 = f32[16,256]{1,0:T(8,128)S(1)} collective-permute-done((f32[16,256]{1,0:T(8,128)S(1)}, f32[16,256]{1,0:T(8,128)S(1)}, u32[]{:S(2)}, u32[]{:S(2)}) %collective-permute-start.13) | collective-permute-done | bytes 16416 | tf_op jit(solution)/shard_map/ppermute | solution.py:42
  118.1 4.7 %collective-permute-start.14 = (f32[16,128]{1,0:T(8,128)S(1)}, f32[16,128]{1,0:T(8,128)S(1)}, u32[]{:S(2)}, u32[]{:S(2)}) collective-permute-start(f32[16,128]{1,0:T(8,128)S(1)} %dynamic-slice_add_fusion.6), channel_id=1, source_target_pairs={{0,16},{1,17},{2,18},{3,19},{4,20},{5,21},{6,22},{7,23},{8,24},{9,... | collective-permute-start | bytes 24584 | tf_op jit(solution)/shard_map/ppermute | solution.py:42
  122.9 3.6 %collective-permute-done.14 = f32[16,128]{1,0:T(8,128)S(1)} collective-permute-done((f32[16,128]{1,0:T(8,128)S(1)}, f32[16,128]{1,0:T(8,128)S(1)}, u32[]{:S(2)}, u32[]{:S(2)}) %collective-permute-start.14) | collective-permute-done | bytes 8224 | tf_op jit(solution)/shard_map/ppermute | solution.py:42
  (180 shorter events, 29.4 us)
Async XLA Ops:
  0.0 78.9 %copy-start = (bf16[16,1024]{1,0:T(8,128)(2,1)S(1)}, bf16[16,1024]{1,0:T(8,128)(2,1)}, u32[]{:S(2)}) copy-start(bf16[16,1024]{1,0:T(8,128)(2,1)} %param.7) | copy-start | bytes 98308
  0.0 17.7 %copy-start.2 = (f32[128]{0:T(128)S(1)}, f32[128]{0:T(128)}, u32[]{:S(2)}) copy-start(f32[128]{0:T(128)} %param.13) | copy-start | bytes 1540
  0.0 17.7 %copy-start.3 = (f32[128]{0:T(128)S(1)}, f32[128]{0:T(128)}, u32[]{:S(2)}) copy-start(f32[128]{0:T(128)} %param.12) | copy-start | bytes 1540
  0.0 17.7 %copy-start.4 = (f32[64]{0:T(128)S(1)}, f32[64]{0:T(128)}, u32[]{:S(2)}) copy-start(f32[64]{0:T(128)} %param.9) | copy-start | bytes 772
  0.0 17.8 %copy-start.1 = (s32[2,1024]{1,0:T(2,128)S(1)}, s32[2,1024]{1,0:T(2,128)}, u32[]{:S(2)}) copy-start(s32[2,1024]{1,0:T(2,128)} %param.8) | copy-start | bytes 24580
  1.5 17.6 %collective-permute-start = (f32[2,192]{1,0:T(2,128)S(1)}, f32[2,192]{1,0:T(2,128)S(1)}, u32[]{:S(2)}, u32[]{:S(2)}) collective-permute-start(f32[2,192]{1,0:T(2,128)S(1)} %maximum_maximum_fusion), channel_id=1, source_target_pairs={{0,1},{1,0},{2,3},{3,2},{4,5},{5,4},{6,7},{7,6},{8,9},{9,8},{10,11... | collective-permute-start | bytes 4616 | tf_op jit(solution)/shard_map/ppermute | solution.py:86
  19.2 4.3 %collective-permute-start.1 = (f32[2,384]{1,0:T(2,128)S(1)}, f32[2,384]{1,0:T(2,128)S(1)}, u32[]{:S(2)}, u32[]{:S(2)}) collective-permute-start(f32[2,384]{1,0:T(2,128)S(1)} %maximum_select_fusion.7), channel_id=1, source_target_pairs={{0,2},{1,3},{2,0},{3,1},{4,6},{5,7},{6,4},{7,5},{8,10},{9,11},{10,... | collective-permute-start | bytes 9224 | tf_op jit(solution)/shard_map/ppermute | solution.py:86
  23.6 5.3 %collective-permute-start.2 = (f32[2,768]{1,0:T(2,128)S(1)}, f32[2,768]{1,0:T(2,128)S(1)}, u32[]{:S(2)}, u32[]{:S(2)}) collective-permute-start(f32[2,768]{1,0:T(2,128)S(1)} %maximum_select_fusion.6), channel_id=1, source_target_pairs={{0,4},{1,5},{2,6},{3,7},{4,0},{5,1},{6,2},{7,3},{8,12},{9,13},{10,... | collective-permute-start | bytes 18440 | tf_op jit(solution)/shard_map/ppermute | solution.py:86
  29.1 8.3 %collective-permute-start.3 = (f32[2,1536]{1,0:T(2,128)S(1)}, f32[2,1536]{1,0:T(2,128)S(1)}, u32[]{:S(2)}, u32[]{:S(2)}) collective-permute-start(f32[2,1536]{1,0:T(2,128)S(1)} %maximum_select_fusion.4), channel_id=1, source_target_pairs={{0,8},{1,9},{2,10},{3,11},{4,12},{5,13},{6,14},{7,15},{8,0},{9,1},... | collective-permute-start | bytes 36872 | tf_op jit(solution)/shard_map/ppermute | solution.py:86
  37.5 8.5 %collective-permute-start.4 = (f32[2,3072]{1,0:T(2,128)S(1)}, f32[2,3072]{1,0:T(2,128)S(1)}, u32[]{:S(2)}, u32[]{:S(2)}) collective-permute-start(f32[2,3072]{1,0:T(2,128)S(1)} %maximum_select_fusion.2), channel_id=1, source_target_pairs={{0,16},{1,17},{2,18},{3,19},{4,20},{5,21},{6,22},{7,23},{8,24},{9,... | collective-permute-start | bytes 73736 | tf_op jit(solution)/shard_map/ppermute | solution.py:86
  50.8 8.3 %collective-permute-start.5 = (f32[2,1024]{1,0:T(2,128)S(1)}, f32[2,1024]{1,0:T(2,128)S(1)}, u32[]{:S(2)}, u32[]{:S(2)}) collective-permute-start(f32[2,1024]{1,0:T(2,128)S(1)} %constant_dynamic-slice_fusion.7), channel_id=1, source_target_pairs={{0,512},{32,544},{64,576},{96,608},{128,640},{160,672},{192,704},{... | collective-permute-start | bytes 24584 | tf_op jit(solution)/shard_map/ppermute | solution.py:98
  59.1 4.7 %collective-permute-start.6 = (f32[2,1024]{1,0:T(2,128)S(1)}, f32[2,1024]{1,0:T(2,128)S(1)}, u32[]{:S(2)}, u32[]{:S(2)}) collective-permute-start(f32[2,1024]{1,0:T(2,128)S(1)} %dynamic-slice_add_fusion.7), channel_id=1, source_target_pairs={{0,32},{32,0},{64,96},{96,64},{128,160},{160,128},{192,224},{224,1... | collective-permute-start | bytes 24584 | tf_op jit(solution)/shard_map/ppermute | solution.py:101
  63.8 5.3 %collective-permute-start.7 = (f32[2,1024]{1,0:T(2,128)S(1)}, f32[2,1024]{1,0:T(2,128)S(1)}, u32[]{:S(2)}, u32[]{:S(2)}) collective-permute-start(f32[2,1024]{1,0:T(2,128)S(1)} %add.392), channel_id=1, source_target_pairs={{0,64},{32,96},{64,0},{96,32},{128,192},{160,224},{192,128},{224,1... | collective-permute-start | bytes 24584 | tf_op jit(solution)/shard_map/ppermute | solution.py:101
  69.1 4.4 %collective-permute-start.8 = (f32[2,1024]{1,0:T(2,128)S(1)}, f32[2,1024]{1,0:T(2,128)S(1)}, u32[]{:S(2)}, u32[]{:S(2)}) collective-permute-start(f32[2,1024]{1,0:T(2,128)S(1)} %add.393), channel_id=1, source_target_pairs={{0,128},{32,160},{64,192},{96,224},{128,0},{160,32},{192,64},{224,... | collective-permute-start | bytes 24584 | tf_op jit(solution)/shard_map/ppermute | solution.py:101
  73.5 5.3 %collective-permute-start.9 = (f32[2,1024]{1,0:T(2,128)S(1)}, f32[2,1024]{1,0:T(2,128)S(1)}, u32[]{:S(2)}, u32[]{:S(2)}) collective-permute-start(f32[2,1024]{1,0:T(2,128)S(1)} %add.394), channel_id=1, source_target_pairs={{0,256},{32,288},{64,320},{96,352},{128,384},{160,416},{192,448},{... | collective-permute-start | bytes 24584 | tf_op jit(solution)/shard_map/ppermute | solution.py:101
  82.4 13.1 %collective-permute-start.10 = (f32[16,2048]{1,0:T(8,128)S(1)}, f32[16,2048]{1,0:T(8,128)S(1)}, u32[]{:S(2)}, u32[]{:S(2)}) collective-permute-start(f32[16,2048]{1,0:T(8,128)S(1)} %pad_maximum_fusion), channel_id=1, source_target_pairs={{0,1},{1,0},{2,3},{3,2},{4,5},{5,4},{6,7},{7,6},{8,9},{9,8},{10,11... | collective-permute-start | bytes 393224 | tf_op jit(solution)/shard_map/ppermute | solution.py:32
  97.3 5.0 %collective-permute-start.11 = (f32[16,1024]{1,0:T(8,128)S(1)}, f32[16,1024]{1,0:T(8,128)S(1)}, u32[]{:S(2)}, u32[]{:S(2)}) collective-permute-start(f32[16,1024]{1,0:T(8,128)S(1)} %dynamic-slice_add_fusion.1), channel_id=1, source_target_pairs={{0,2},{1,3},{2,0},{3,1},{4,6},{5,7},{6,4},{7,5},{8,10},{9,11},{10,... | collective-permute-start | bytes 196616 | tf_op jit(solution)/shard_map/ppermute | solution.py:42
  103.3 5.6 %collective-permute-start.12 = (f32[16,512]{1,0:T(8,128)S(1)}, f32[16,512]{1,0:T(8,128)S(1)}, u32[]{:S(2)}, u32[]{:S(2)}) collective-permute-start(f32[16,512]{1,0:T(8,128)S(1)} %dynamic-slice_add_fusion.3), channel_id=1, source_target_pairs={{0,4},{1,5},{2,6},{3,7},{4,0},{5,1},{6,2},{7,3},{8,12},{9,13},{10,... | collective-permute-start | bytes 98312 | tf_op jit(solution)/shard_map/ppermute | solution.py:42
  109.4 8.4 %collective-permute-start.13 = (f32[16,256]{1,0:T(8,128)S(1)}, f32[16,256]{1,0:T(8,128)S(1)}, u32[]{:S(2)}, u32[]{:S(2)}) collective-permute-start(f32[16,256]{1,0:T(8,128)S(1)} %dynamic-slice_add_fusion.5), channel_id=1, source_target_pairs={{0,8},{1,9},{2,10},{3,11},{4,12},{5,13},{6,14},{7,15},{8,0},{9,1},... | collective-permute-start | bytes 49160 | tf_op jit(solution)/shard_map/ppermute | solution.py:42
  118.1 8.3 %collective-permute-start.14 = (f32[16,128]{1,0:T(8,128)S(1)}, f32[16,128]{1,0:T(8,128)S(1)}, u32[]{:S(2)}, u32[]{:S(2)}) collective-permute-start(f32[16,128]{1,0:T(8,128)S(1)} %dynamic-slice_add_fusion.6), channel_id=1, source_target_pairs={{0,16},{1,17},{2,18},{3,19},{4,20},{5,21},{6,22},{7,23},{8,24},{9,... | collective-permute-start | bytes 24584 | tf_op jit(solution)/shard_map/ppermute | solution.py:42

commit v15 on v12

--- a/solution.py
+++ b/solution.py
@@ -92,7 +92,9 @@
     own_cols = position.shape[1]
     mine = lax.dynamic_slice_in_dim(looked, child_id * own_cols, own_cols, 1)
     theirs = lax.dynamic_slice_in_dim(looked, (1 - child_id) * own_cols, own_cols, 1)
-    looked = mine + lax.ppermute(theirs, "row", perm=[(i, i ^ half_rows) for i in range(row_total)])
+    fast = row_total // 8
+    mirror = [(row_total // fast - 1 - i // fast) * fast + i % fast for i in range(row_total)]
+    looked = mine + lax.ppermute(theirs, "row", perm=[(i, mirror[i]) for i in range(row_total)])
     step = 1
     while step < half_rows:
         looked = looked + lax.ppermute(looked, "row", perm=[(i, i ^ step) for i in range(row_total)])

time: 127 us -> 124 us (0.976)
  waiting for transfers between devices: 36.7 us -> 30.4 us
  starting transfers between devices: 68 us -> 71.6 us
    ppermute x4, starting transfers between devices: 8.36 us -> 11.9 us  [per_device(): lax.ppermute(looked, 'row', perm=[(i, i ^ step) for i in range(row_total)])]
    ppermute x4, waiting for transfers between devices: 11.2 us -> 7.75 us  [per_device(): lax.ppermute(looked, 'row', perm=[(i, i ^ step) for i in range(row_total)])]
    ppermute x4, starting transfers between devices: 12.1 us -> 15 us  [reduce_by_halves(): lax.ppermute(sent, axis, perm=[(i, i ^ step) for i in range(size)])]
    ppermute x4, waiting for transfers between devices: 15.9 us -> 13.1 us  [reduce_by_halves(): lax.ppermute(sent, axis, perm=[(i, i ^ step) for i in range(size)])]
    ppermute x1, starting transfers between devices: 5.71 us -> 3.1 us  [per_device(): lax.ppermute(theirs, 'row', perm=[(i, mirror[i]) for i in range(row_total)])]
  transfers between devices with their start and end apart: 15 -> 15, of which waited for: 13 -> 13; matrix products, arithmetic and copies ran while one was open for 8% -> 9% of each run, Pallas kernels for 0% -> 0%
where the time goes in v15:
time: 124 us; the launch traced here: 123 us
  starting transfers between devices  71.6 us (58%)
  waiting for transfers between devices  30.4 us (25%)
  matrix products  14.8 us (12%)
  other arithmetic  2.83 us (2%)
  local copies, waits for them, and re-layouts  2.05 us (2%)
    ppermute x5, starting transfers between devices, per_device(): lax.ppermute(held, 'col', perm=[(i, i ^ step) for i in range(col_total)])  29.5 us
    ppermute x4, starting transfers between devices, reduce_by_halves(): lax.ppermute(sent, axis, perm=[(i, i ^ step) for i in range(size)])  15 us
    ppermute x4, waiting for transfers between devices, reduce_by_halves(): lax.ppermute(sent, axis, perm=[(i, i ^ step) for i in range(size)])  13.1 us
    ppermute x1, starting transfers between devices, reduce_by_halves(): got = lax.ppermute(sent, axis, perm=[(i, i ^ step) for i in range(size)])  12.2 us
    ppermute x4, starting transfers between devices, per_device(): lax.ppermute(looked, 'row', perm=[(i, i ^ step) for i in range(row_total)])  11.9 us
    ppermute x4, waiting for transfers between devices, per_device(): lax.ppermute(looked, 'row', perm=[(i, i ^ step) for i in range(row_total)])  7.75 us
    dot_general x24, matrix products, look_up(): lax.dot_general(table, hits.astype(jnp.bfloat16), (((1,), (1,)), ((), ())...  7.72 us
    ppermute x5, waiting for transfers between devices, per_device(): lax.ppermute(held, 'col', perm=[(i, i ^ step) for i in range(col_total)])  7.37 us
  transfers between devices with their start and end apart: 15, of which 13 were waited for; matrix products, arithmetic and copies ran while one was open for 9% of the time, Pallas kernels for 0%

profile of v15, /device:TPU:1, one launch (start us, length us, event | category | flops | bytes accessed | tf_op | source)
XLA Modules:
  0.0 122.7 jit_solution(6638961192448446595)
XLA Ops:
  1.5 16.1 %collective-permute-start = (f32[2,192]{1,0:T(2,128)S(1)}, f32[2,192]{1,0:T(2,128)S(1)}, u32[]{:S(2)}, u32[]{:S(2)}) collective-permute-start(f32[2,192]{1,0:T(2,128)S(1)} %maximum_maximum_fusion), channel_id=1, source_target_pairs={{0,1},{1,0},{2,3},{3,2},{4,5},{5,4},{6,7},{7,6},{8,9},{9,8},{10,11... | collective-permute-start | bytes 4616 | tf_op jit(solution)/shard_map/ppermute | solution.py:83
  19.7 1.9 %collective-permute-start.1 = (f32[2,384]{1,0:T(2,128)S(1)}, f32[2,384]{1,0:T(2,128)S(1)}, u32[]{:S(2)}, u32[]{:S(2)}) collective-permute-start(f32[2,384]{1,0:T(2,128)S(1)} %maximum_select_fusion.7), channel_id=1, source_target_pairs={{0,2},{1,3},{2,0},{3,1},{4,6},{5,7},{6,4},{7,5},{8,10},{9,11},{10,... | collective-permute-start | bytes 9224 | tf_op jit(solution)/shard_map/ppermute | solution.py:83
  24.0 1.9 %collective-permute-start.2 = (f32[2,768]{1,0:T(2,128)S(1)}, f32[2,768]{1,0:T(2,128)S(1)}, u32[]{:S(2)}, u32[]{:S(2)}) collective-permute-start(f32[2,768]{1,0:T(2,128)S(1)} %maximum_select_fusion.6), channel_id=1, source_target_pairs={{0,4},{1,5},{2,6},{3,7},{4,0},{5,1},{6,2},{7,3},{8,12},{9,13},{10,... | collective-permute-start | bytes 18440 | tf_op jit(solution)/shard_map/ppermute | solution.py:83
  27.2 2.1 %collective-permute-done.2 = f32[2,768]{1,0:T(2,128)S(1)} collective-permute-done((f32[2,768]{1,0:T(2,128)S(1)}, f32[2,768]{1,0:T(2,128)S(1)}, u32[]{:S(2)}, u32[]{:S(2)}) %collective-permute-start.2) | collective-permute-done | bytes 6176 | tf_op jit(solution)/shard_map/ppermute | solution.py:83
  29.3 4.4 %collective-permute-start.3 = (f32[2,1536]{1,0:T(2,128)S(1)}, f32[2,1536]{1,0:T(2,128)S(1)}, u32[]{:S(2)}, u32[]{:S(2)}) collective-permute-start(f32[2,1536]{1,0:T(2,128)S(1)} %maximum_select_fusion.4), channel_id=1, source_target_pairs={{0,8},{1,9},{2,10},{3,11},{4,12},{5,13},{6,14},{7,15},{8,0},{9,1},... | collective-permute-start | bytes 36872 | tf_op jit(solution)/shard_map/ppermute | solution.py:83
  35.0 2.6 %collective-permute-done.3 = f32[2,1536]{1,0:T(2,128)S(1)} collective-permute-done((f32[2,1536]{1,0:T(2,128)S(1)}, f32[2,1536]{1,0:T(2,128)S(1)}, u32[]{:S(2)}, u32[]{:S(2)}) %collective-permute-start.3) | collective-permute-done | bytes 12320 | tf_op jit(solution)/shard_map/ppermute | solution.py:83
  37.7 5.3 %collective-permute-start.4 = (f32[2,3072]{1,0:T(2,128)S(1)}, f32[2,3072]{1,0:T(2,128)S(1)}, u32[]{:S(2)}, u32[]{:S(2)}) collective-permute-start(f32[2,3072]{1,0:T(2,128)S(1)} %maximum_select_fusion.2), channel_id=1, source_target_pairs={{0,16},{1,17},{2,18},{3,19},{4,20},{5,21},{6,22},{7,23},{8,24},{9,... | collective-permute-start | bytes 73736 | tf_op jit(solution)/shard_map/ppermute | solution.py:83
  49.0 3.1 %collective-permute-start.5 = (f32[2,1024]{1,0:T(2,128)S(1)}, f32[2,1024]{1,0:T(2,128)S(1)}, u32[]{:S(2)}, u32[]{:S(2)}) collective-permute-start(f32[2,1024]{1,0:T(2,128)S(1)} %constant_dynamic-slice_fusion.8), channel_id=1, source_target_pairs={{0,896},{32,928},{64,960},{96,992},{128,768},{160,800},{192,832},{... | collective-permute-start | bytes 24584 | tf_op jit(solution)/shard_map/ppermute | solution.py:97
  52.4 2.2 %collective-permute-done.5 = f32[2,1024]{1,0:T(2,128)S(1)} collective-permute-done((f32[2,1024]{1,0:T(2,128)S(1)}, f32[2,1024]{1,0:T(2,128)S(1)}, u32[]{:S(2)}, u32[]{:S(2)}) %collective-permute-start.5) | collective-permute-done | bytes 8224 | tf_op jit(solution)/shard_map/ppermute | solution.py:97
  54.6 1.9 %collective-permute-start.6 = (f32[2,1024]{1,0:T(2,128)S(1)}, f32[2,1024]{1,0:T(2,128)S(1)}, u32[]{:S(2)}, u32[]{:S(2)}) collective-permute-start(f32[2,1024]{1,0:T(2,128)S(1)} %dynamic-slice_add_fusion.3), channel_id=1, source_target_pairs={{0,32},{32,0},{64,96},{96,64},{128,160},{160,128},{192,224},{224,1... | collective-permute-start | bytes 24584 | tf_op jit(solution)/shard_map/ppermute | solution.py:100
  56.5 2.5 %collective-permute-done.6 = f32[2,1024]{1,0:T(2,128)S(1)} collective-permute-done((f32[2,1024]{1,0:T(2,128)S(1)}, f32[2,1024]{1,0:T(2,128)S(1)}, u32[]{:S(2)}, u32[]{:S(2)}) %collective-permute-start.6) | collective-permute-done | bytes 8224 | tf_op jit(solution)/shard_map/ppermute | solution.py:100
  59.0 1.9 %collective-permute-start.7 = (f32[2,1024]{1,0:T(2,128)S(1)}, f32[2,1024]{1,0:T(2,128)S(1)}, u32[]{:S(2)}, u32[]{:S(2)}) collective-permute-start(f32[2,1024]{1,0:T(2,128)S(1)} %add.352), channel_id=1, source_target_pairs={{0,64},{32,96},{64,0},{96,32},{128,192},{160,224},{192,128},{224,1... | collective-permute-start | bytes 24584 | tf_op jit(solution)/shard_map/ppermute | solution.py:100
  60.9 3.4 %collective-permute-done.7 = f32[2,1024]{1,0:T(2,128)S(1)} collective-permute-done((f32[2,1024]{1,0:T(2,128)S(1)}, f32[2,1024]{1,0:T(2,128)S(1)}, u32[]{:S(2)}, u32[]{:S(2)}) %collective-permute-start.7) | collective-permute-done | bytes 8224 | tf_op jit(solution)/shard_map/ppermute | solution.py:100
  64.3 3.5 %collective-permute-start.8 = (f32[2,1024]{1,0:T(2,128)S(1)}, f32[2,1024]{1,0:T(2,128)S(1)}, u32[]{:S(2)}, u32[]{:S(2)}) collective-permute-start(f32[2,1024]{1,0:T(2,128)S(1)} %add.353), channel_id=1, source_target_pairs={{0,128},{32,160},{64,192},{96,224},{128,0},{160,32},{192,64},{224,... | collective-permute-start | bytes 24584 | tf_op jit(solution)/shard_map/ppermute | solution.py:100
  68.8 4.6 %collective-permute-start.9 = (f32[2,1024]{1,0:T(2,128)S(1)}, f32[2,1024]{1,0:T(2,128)S(1)}, u32[]{:S(2)}, u32[]{:S(2)}) collective-permute-start(f32[2,1024]{1,0:T(2,128)S(1)} %add.354), channel_id=1, source_target_pairs={{0,256},{32,288},{64,320},{96,352},{128,384},{160,416},{192,448},{... | collective-permute-start | bytes 24584 | tf_op jit(solution)/shard_map/ppermute | solution.py:100
  78.0 12.2 %collective-permute-start.10 = (f32[16,2048]{1,0:T(8,128)S(1)}, f32[16,2048]{1,0:T(8,128)S(1)}, u32[]{:S(2)}, u32[]{:S(2)}) collective-permute-start(f32[16,2048]{1,0:T(8,128)S(1)} %pad_maximum_fusion), channel_id=1, source_target_pairs={{0,1},{1,0},{2,3},{3,2},{4,5},{5,4},{6,7},{7,6},{8,9},{9,8},{10,11... | collective-permute-start | bytes 393224 | tf_op jit(solution)/shard_map/ppermute | solution.py:32
  93.9 1.9 %collective-permute-start.11 = (f32[16,1024]{1,0:T(8,128)S(1)}, f32[16,1024]{1,0:T(8,128)S(1)}, u32[]{:S(2)}, u32[]{:S(2)}) collective-permute-start(f32[16,1024]{1,0:T(8,128)S(1)} %constant_dynamic-slice_fusion.4), channel_id=1, source_target_pairs={{0,2},{1,3},{2,0},{3,1},{4,6},{5,7},{6,4},{7,5},{8,10},{9,11},{10,... | collective-permute-start | bytes 196616 | tf_op jit(solution)/shard_map/ppermute | solution.py:40
  95.8 3.7 %collective-permute-done.11 = f32[16,1024]{1,0:T(8,128)S(1)} collective-permute-done((f32[16,1024]{1,0:T(8,128)S(1)}, f32[16,1024]{1,0:T(8,128)S(1)}, u32[]{:S(2)}, u32[]{:S(2)}) %collective-permute-start.11) | collective-permute-done | bytes 65568 | tf_op jit(solution)/shard_map/ppermute | solution.py:40
  99.5 2.2 %collective-permute-start.12 = (f32[16,512]{1,0:T(8,128)S(1)}, f32[16,512]{1,0:T(8,128)S(1)}, u32[]{:S(2)}, u32[]{:S(2)}) collective-permute-start(f32[16,512]{1,0:T(8,128)S(1)} %constant_dynamic-slice_fusion.3), channel_id=1, source_target_pairs={{0,4},{1,5},{2,6},{3,7},{4,0},{5,1},{6,2},{7,3},{8,12},{9,13},{10,... | collective-permute-start | bytes 98312 | tf_op jit(solution)/shard_map/ppermute | solution.py:40
  101.7 3.6 %collective-permute-done.12 = f32[16,512]{1,0:T(8,128)S(1)} collective-permute-done((f32[16,512]{1,0:T(8,128)S(1)}, f32[16,512]{1,0:T(8,128)S(1)}, u32[]{:S(2)}, u32[]{:S(2)}) %collective-permute-start.12) | collective-permute-done | bytes 32800 | tf_op jit(solution)/shard_map/ppermute | solution.py:40
  105.4 5.4 %collective-permute-start.13 = (f32[16,256]{1,0:T(8,128)S(1)}, f32[16,256]{1,0:T(8,128)S(1)}, u32[]{:S(2)}, u32[]{:S(2)}) collective-permute-start(f32[16,256]{1,0:T(8,128)S(1)} %constant_dynamic-slice_fusion.2), channel_id=1, source_target_pairs={{0,8},{1,9},{2,10},{3,11},{4,12},{5,13},{6,14},{7,15},{8,0},{9,1},... | collective-permute-start | bytes 49160 | tf_op jit(solution)/shard_map/ppermute | solution.py:40
  110.8 2.9 %collective-permute-done.13 = f32[16,256]{1,0:T(8,128)S(1)} collective-permute-done((f32[16,256]{1,0:T(8,128)S(1)}, f32[16,256]{1,0:T(8,128)S(1)}, u32[]{:S(2)}, u32[]{:S(2)}) %collective-permute-start.13) | collective-permute-done | bytes 16416 | tf_op jit(solution)/shard_map/ppermute | solution.py:40
  113.8 5.4 %collective-permute-start.14 = (f32[16,128]{1,0:T(8,128)S(1)}, f32[16,128]{1,0:T(8,128)S(1)}, u32[]{:S(2)}, u32[]{:S(2)}) collective-permute-start(f32[16,128]{1,0:T(8,128)S(1)} %constant_dynamic-slice_fusion.1), channel_id=1, source_target_pairs={{0,16},{1,17},{2,18},{3,19},{4,20},{5,21},{6,22},{7,23},{8,24},{9,... | collective-permute-start | bytes 24584 | tf_op jit(solution)/shard_map/ppermute | solution.py:40
  119.2 2.8 %collective-permute-done.14 = f32[16,128]{1,0:T(8,128)S(1)} collective-permute-done((f32[16,128]{1,0:T(8,128)S(1)}, f32[16,128]{1,0:T(8,128)S(1)}, u32[]{:S(2)}, u32[]{:S(2)}) %collective-permute-start.14) | collective-permute-done | bytes 8224 | tf_op jit(solution)/shard_map/ppermute | solution.py:40
  (174 shorter events, 24.2 us)
Async XLA Ops:
  0.0 74.4 %copy-start = (bf16[16,1024]{1,0:T(8,128)(2,1)S(1)}, bf16[16,1024]{1,0:T(8,128)(2,1)}, u32[]{:S(2)}) copy-start(bf16[16,1024]{1,0:T(8,128)(2,1)} %param.7) | copy-start | bytes 98308
  0.0 17.7 %copy-start.2 = (f32[128]{0:T(128)S(1)}, f32[128]{0:T(128)}, u32[]{:S(2)}) copy-start(f32[128]{0:T(128)} %param.13) | copy-start | bytes 1540
  0.0 17.7 %copy-start.3 = (f32[128]{0:T(128)S(1)}, f32[128]{0:T(128)}, u32[]{:S(2)}) copy-start(f32[128]{0:T(128)} %param.12) | copy-start | bytes 1540
  0.0 17.7 %copy-start.4 = (f32[64]{0:T(128)S(1)}, f32[64]{0:T(128)}, u32[]{:S(2)}) copy-start(f32[64]{0:T(128)} %param.9) | copy-start | bytes 772
  1.5 18.1 %collective-permute-start = (f32[2,192]{1,0:T(2,128)S(1)}, f32[2,192]{1,0:T(2,128)S(1)}, u32[]{:S(2)}, u32[]{:S(2)}) collective-permute-start(f32[2,192]{1,0:T(2,128)S(1)} %maximum_maximum_fusion), channel_id=1, source_target_pairs={{0,1},{1,0},{2,3},{3,2},{4,5},{5,4},{6,7},{7,6},{8,9},{9,8},{10,11... | collective-permute-start | bytes 4616 | tf_op jit(solution)/shard_map/ppermute | solution.py:83
  17.6 0.7 copy-start.1
  19.7 4.3 %collective-permute-start.1 = (f32[2,384]{1,0:T(2,128)S(1)}, f32[2,384]{1,0:T(2,128)S(1)}, u32[]{:S(2)}, u32[]{:S(2)}) collective-permute-start(f32[2,384]{1,0:T(2,128)S(1)} %maximum_select_fusion.7), channel_id=1, source_target_pairs={{0,2},{1,3},{2,0},{3,1},{4,6},{5,7},{6,4},{7,5},{8,10},{9,11},{10,... | collective-permute-start | bytes 9224 | tf_op jit(solution)/shard_map/ppermute | solution.py:83
  24.0 5.3 %collective-permute-start.2 = (f32[2,768]{1,0:T(2,128)S(1)}, f32[2,768]{1,0:T(2,128)S(1)}, u32[]{:S(2)}, u32[]{:S(2)}) collective-permute-start(f32[2,768]{1,0:T(2,128)S(1)} %maximum_select_fusion.6), channel_id=1, source_target_pairs={{0,4},{1,5},{2,6},{3,7},{4,0},{5,1},{6,2},{7,3},{8,12},{9,13},{10,... | collective-permute-start | bytes 18440 | tf_op jit(solution)/shard_map/ppermute | solution.py:83
  29.3 8.3 %collective-permute-start.3 = (f32[2,1536]{1,0:T(2,128)S(1)}, f32[2,1536]{1,0:T(2,128)S(1)}, u32[]{:S(2)}, u32[]{:S(2)}) collective-permute-start(f32[2,1536]{1,0:T(2,128)S(1)} %maximum_select_fusion.4), channel_id=1, source_target_pairs={{0,8},{1,9},{2,10},{3,11},{4,12},{5,13},{6,14},{7,15},{8,0},{9,1},... | collective-permute-start | bytes 36872 | tf_op jit(solution)/shard_map/ppermute | solution.py:83
  37.7 8.5 %collective-permute-start.4 = (f32[2,3072]{1,0:T(2,128)S(1)}, f32[2,3072]{1,0:T(2,128)S(1)}, u32[]{:S(2)}, u32[]{:S(2)}) collective-permute-start(f32[2,3072]{1,0:T(2,128)S(1)} %maximum_select_fusion.2), channel_id=1, source_target_pairs={{0,16},{1,17},{2,18},{3,19},{4,20},{5,21},{6,22},{7,23},{8,24},{9,... | collective-permute-start | bytes 73736 | tf_op jit(solution)/shard_map/ppermute | solution.py:83
  49.0 5.6 %collective-permute-start.5 = (f32[2,1024]{1,0:T(2,128)S(1)}, f32[2,1024]{1,0:T(2,128)S(1)}, u32[]{:S(2)}, u32[]{:S(2)}) collective-permute-start(f32[2,1024]{1,0:T(2,128)S(1)} %constant_dynamic-slice_fusion.8), channel_id=1, source_target_pairs={{0,896},{32,928},{64,960},{96,992},{128,768},{160,800},{192,832},{... | collective-permute-start | bytes 24584 | tf_op jit(solution)/shard_map/ppermute | solution.py:97
  54.6 4.4 %collective-permute-start.6 = (f32[2,1024]{1,0:T(2,128)S(1)}, f32[2,1024]{1,0:T(2,128)S(1)}, u32[]{:S(2)}, u32[]{:S(2)}) collective-permute-start(f32[2,1024]{1,0:T(2,128)S(1)} %dynamic-slice_add_fusion.3), channel_id=1, source_target_pairs={{0,32},{32,0},{64,96},{96,64},{128,160},{160,128},{192,224},{224,1... | collective-permute-start | bytes 24584 | tf_op jit(solution)/shard_map/ppermute | solution.py:100
  59.0 5.3 %collective-permute-start.7 = (f32[2,1024]{1,0:T(2,128)S(1)}, f32[2,1024]{1,0:T(2,128)S(1)}, u32[]{:S(2)}, u32[]{:S(2)}) collective-permute-start(f32[2,1024]{1,0:T(2,128)S(1)} %add.352), channel_id=1, source_target_pairs={{0,64},{32,96},{64,0},{96,32},{128,192},{160,224},{192,128},{224,1... | collective-permute-start | bytes 24584 | tf_op jit(solution)/shard_map/ppermute | solution.py:100
  64.3 4.5 %collective-permute-start.8 = (f32[2,1024]{1,0:T(2,128)S(1)}, f32[2,1024]{1,0:T(2,128)S(1)}, u32[]{:S(2)}, u32[]{:S(2)}) collective-permute-start(f32[2,1024]{1,0:T(2,128)S(1)} %add.353), channel_id=1, source_target_pairs={{0,128},{32,160},{64,192},{96,224},{128,0},{160,32},{192,64},{224,... | collective-permute-start | bytes 24584 | tf_op jit(solution)/shard_map/ppermute | solution.py:100
  68.8 5.6 %collective-permute-start.9 = (f32[2,1024]{1,0:T(2,128)S(1)}, f32[2,1024]{1,0:T(2,128)S(1)}, u32[]{:S(2)}, u32[]{:S(2)}) collective-permute-start(f32[2,1024]{1,0:T(2,128)S(1)} %add.354), channel_id=1, source_target_pairs={{0,256},{32,288},{64,320},{96,352},{128,384},{160,416},{192,448},{... | collective-permute-start | bytes 24584 | tf_op jit(solution)/shard_map/ppermute | solution.py:100
  78.0 15.8 %collective-permute-start.10 = (f32[16,2048]{1,0:T(8,128)S(1)}, f32[16,2048]{1,0:T(8,128)S(1)}, u32[]{:S(2)}, u32[]{:S(2)}) collective-permute-start(f32[16,2048]{1,0:T(8,128)S(1)} %pad_maximum_fusion), channel_id=1, source_target_pairs={{0,1},{1,0},{2,3},{3,2},{4,5},{5,4},{6,7},{7,6},{8,9},{9,8},{10,11... | collective-permute-start | bytes 393224 | tf_op jit(solution)/shard_map/ppermute | solution.py:32
  93.9 5.6 %collective-permute-start.11 = (f32[16,1024]{1,0:T(8,128)S(1)}, f32[16,1024]{1,0:T(8,128)S(1)}, u32[]{:S(2)}, u32[]{:S(2)}) collective-permute-start(f32[16,1024]{1,0:T(8,128)S(1)} %constant_dynamic-slice_fusion.4), channel_id=1, source_target_pairs={{0,2},{1,3},{2,0},{3,1},{4,6},{5,7},{6,4},{7,5},{8,10},{9,11},{10,... | collective-permute-start | bytes 196616 | tf_op jit(solution)/shard_map/ppermute | solution.py:40
  99.5 5.8 %collective-permute-start.12 = (f32[16,512]{1,0:T(8,128)S(1)}, f32[16,512]{1,0:T(8,128)S(1)}, u32[]{:S(2)}, u32[]{:S(2)}) collective-permute-start(f32[16,512]{1,0:T(8,128)S(1)} %constant_dynamic-slice_fusion.3), channel_id=1, source_target_pairs={{0,4},{1,5},{2,6},{3,7},{4,0},{5,1},{6,2},{7,3},{8,12},{9,13},{10,... | collective-permute-start | bytes 98312 | tf_op jit(solution)/shard_map/ppermute | solution.py:40
  105.4 8.4 %collective-permute-start.13 = (f32[16,256]{1,0:T(8,128)S(1)}, f32[16,256]{1,0:T(8,128)S(1)}, u32[]{:S(2)}, u32[]{:S(2)}) collective-permute-start(f32[16,256]{1,0:T(8,128)S(1)} %constant_dynamic-slice_fusion.2), channel_id=1, source_target_pairs={{0,8},{1,9},{2,10},{3,11},{4,12},{5,13},{6,14},{7,15},{8,0},{9,1},... | collective-permute-start | bytes 49160 | tf_op jit(solution)/shard_map/ppermute | solution.py:40
  113.8 8.3 %collective-permute-start.14 = (f32[16,128]{1,0:T(8,128)S(1)}, f32[16,128]{1,0:T(8,128)S(1)}, u32[]{:S(2)}, u32[]{:S(2)}) collective-permute-start(f32[16,128]{1,0:T(8,128)S(1)} %constant_dynamic-slice_fusion.1), channel_id=1, source_target_pairs={{0,16},{1,17},{2,18},{3,19},{4,20},{5,21},{6,22},{7,23},{8,24},{9,... | collective-permute-start | bytes 24584 | tf_op jit(solution)/shard_map/ppermute | solution.py:40
